TPU v7x, 32 devices: a whole 2x2x4 slice. The times are simulated.
32 devices in a mesh: grp: 2 (over x), tm: 8 (over z, y), row: 2 (over core).
Axes of the slice: x: 2, y: 2, z: 4, core: 2. Of those that a mesh axis runs over, the one named last changes fastest.
Arguments:
- frames: bfloat16 [16, 256, 64, 48], P(('grp', 'tm'), None, 'row'), parts along dimension 0, may hold values from 0 to 31, as said below
- clip_start: int32 [16], P('grp'), parts along dimension 0, may hold values 0 or 1
- semantic: int32 [16, 64, 48], P(('grp', 'tm'), 'row'), parts along dimension 0, may hold values from 0 to 18
- instance: int32 [16, 64, 48], P(('grp', 'tm'), 'row'), parts along dimension 0, may hold values from 0 to 63
- aspp_point: bfloat16 [256, 512], replicated, may hold values from -0.25 to 0.25
- aspp_dilated: bfloat16 [3, 9, 256, 512], replicated, may hold values from -0.09375 to 0.09375
- pool_weight: bfloat16 [256, 512], replicated, may hold values from -0.25 to 0.25
- proj_weight: bfloat16 [256, 1280], replicated, may hold values from -0.15625 to 0.15625
- head_weight: bfloat16 [25, 96, 256], replicated, may hold values from -0.078125 to 0.078125
- out_weight: bfloat16 [4, 32], replicated, may hold values from -1 to 1
Outputs:
- predictions: float32 [16, 4, 64, 48], P(('grp', 'tm'), None, 'row'), parts along dimension 0
- losses: float32 [4], P('grp'), parts along dimension 0
There are 2 independent parts, one for each index of `grp`. A program takes and returns all parts, laid end to end along the dimension named above; an argument that names none is the same for every part. Nothing has to cross between parts.
Inputs may be any that keep to these rules, and one draw needn't show every extreme that they name: `frames`: every entry is zero or positive.
All inputs are finite; a program needn't handle non-finite values.
Results may differ from a plain program's by a relative error of at most 0.0075.
Values may be sent and summed in bfloat16 or wider, within the bound.
No kernel may reach another device: no remote copies, remote signals or barrier semaphores. Data moves between devices by JAX's collectives and lax.ppermute only.
A program may use at most 128 MiB of HBM per device.

v0:
```python
import jax
import jax.numpy as jnp
from jax import lax
from jax.sharding import PartitionSpec as P
from jax.experimental import pallas as pl
from jax.experimental.pallas import tpu as pltpu

THING_FIRST = 11
INSTANCES = 64


DILATIONS = (6, 12, 18)
aspp_reach = 18
center_sigma = 8.0
offset_weight = 0.01


def padded_2(block, sides, width):
    for axis, dim in sides:
        count = lax.axis_size(axis)
        forward = [(i, i + 1) for i in range(count - 1)]
        backward = [(target, source) for source, target in forward]
        low = lax.ppermute(
            lax.slice_in_dim(block, block.shape[dim] - width, None, axis=dim), axis, forward
        )
        high = lax.ppermute(lax.slice_in_dim(block, 0, width, axis=dim), axis, backward)
        block = jnp.concatenate([low, block, high], axis=dim)
    return block


def shifted(value, axis, steps):
    count = lax.axis_size(axis)
    pairs = [(source, (source + steps) % count) for source in range(count)]
    return lax.ppermute(value, axis, pairs)


def all_sum(value, axes):
    for axis in axes:
        count = lax.axis_size(axis)
        if count & (count - 1):
            value = jax.tree.map(lambda v: lax.psum(v, axis), value)
            continue
        step = 1
        while step < count:
            pairs = [(i, i ^ step) for i in range(count)]
            other = lax.ppermute(value, axis, pairs)
            value = jax.tree.map(jnp.add, value, other)
            step *= 2
    return value


def aspp_projected(x, aspp_point, aspp_dilated, proj_weight, pool_term, geometry):
    front, pitch, margin, block, blocks = geometry
    width = aspp_point.shape[0]
    contract = (((1,), (1,)), ((), ()))

    def body(x_ref, point_ref, dilated_ref, proj_ref, pool_ref, out_ref):
        for index in range(blocks):
            base = front + margin * pitch + index * block

            def window(shift):
                return x_ref[pl.ds(base + shift, block), :].astype(jnp.bfloat16)

            sums = [
                lax.dot_general(
                    window(0), point_ref[...], contract, preferred_element_type=jnp.float32
                )
            ]
            for branch, spread in enumerate(DILATIONS):
                total = None
                for vertical in range(3):
                    for lateral in range(3):
                        shift = (vertical - 1) * spread * pitch + (lateral - 1) * spread
                        term = lax.dot_general(
                            window(shift),
                            dilated_ref[branch, 3 * vertical + lateral],
                            contract,
                            preferred_element_type=jnp.float32,
                        )
                        total = term if total is None else total + term
                sums.append(total)
            mixed = None
            for branch, total in enumerate(sums):
                term = lax.dot_general(
                    relu_bf16(total),
                    proj_ref[:, branch * width : (branch + 1) * width],
                    contract,
                    preferred_element_type=jnp.float32,
                )
                mixed = term if mixed is None else mixed + term
            mixed = mixed + pool_ref[...]
            out_ref[pl.ds(index * block, block), :] = relu_bf16(mixed)

    taps = 1 + 9 * len(DILATIONS)
    flops = 2 * blocks * block * x.shape[1] * width * taps + 2 * blocks * block * 4 * width * width
    return pl.pallas_call(
        body,
        out_shape=jax.ShapeDtypeStruct((blocks * block, width), jnp.bfloat16),
        compiler_params=pltpu.CompilerParams(vmem_limit_bytes=56 * 1024 * 1024),
        cost_estimate=pl.CostEstimate(
            flops=flops,
            transcendentals=0,
            bytes_accessed=x.size * 4 + aspp_dilated.size * 2 + blocks * block * width * 2,
        ),
    )(x, aspp_point, aspp_dilated, proj_weight, pool_term)


def relu_bf16(values):
    return jnp.maximum(values, 0.0).astype(jnp.bfloat16)


def emit_heads(head_out, out_weight):
    groups = head_out.reshape(3, -1, head_out.shape[1], head_out.shape[2])
    center_map = jnp.einsum(
        "c,crw->rw", out_weight[0], groups[0], preferred_element_type=jnp.float32
    )
    offset_map = jnp.einsum(
        "oc,crw->orw", out_weight[1:3], groups[1], preferred_element_type=jnp.float32
    )
    depth_map = jnp.einsum(
        "c,crw->rw", out_weight[3], groups[2], preferred_element_type=jnp.float32
    )
    return jnp.concatenate([center_map[None], offset_map, depth_map[None]], 0)


def shards(
    frames,
    clip_start,
    semantic,
    instance,
    aspp_point,
    aspp_dilated,
    pool_weight,
    proj_weight,
    head_weight,
    out_weight,
):
    own_band = frames[0]
    channel_count, band_rows, columns = own_band.shape
    frame_count = clip_start.shape[0]
    height = band_rows * lax.axis_size("row")
    time_index = lax.axis_index("tm")
    row_index = lax.axis_index("row")
    ahead = (time_index + 1) % frame_count
    at_end = lax.dynamic_index_in_dim(clip_start, ahead, 0, keepdims=False) == 1
    later_band = jnp.where(at_end, own_band, shifted(own_band, "tm", -1))
    rim_rows = min(aspp_reach, band_rows)
    extra_rows = aspp_reach - rim_rows

    def widen(band):
        wide = padded_2(band, (("row", 1),), rim_rows)
        return jnp.pad(wide, ((0, 0), (extra_rows, extra_rows), (0, 0)))

    joined_wide = jnp.concatenate([widen(own_band), widen(later_band)], 0)
    wide_rows = joined_wide.shape[1]
    pitch = columns + aspp_reach
    front = 24
    block_rows = 8 if band_rows % 8 == 0 else band_rows
    block = block_rows * pitch
    blocks = band_rows // block_rows
    length = -(-(front + wide_rows * pitch + aspp_reach) // 8) * 8
    flat = jnp.pad(
        jnp.transpose(joined_wide, (1, 2, 0)), ((0, 0), (aspp_reach, 0), (0, 0))
    ).reshape(wide_rows * pitch, 2 * channel_count)
    flat = jnp.pad(flat, ((front, length - front - wide_rows * pitch), (0, 0))).astype(
        jnp.float32
    )

    counted = (semantic[0] >= THING_FIRST) & (instance[0] > 0)
    labels = jnp.arange(INSTANCES, dtype=jnp.int32)
    onehot = ((instance[0][None] == labels[:, None, None]) & counted[None]).astype(jnp.float32)
    row_pos = (row_index * band_rows + jnp.arange(band_rows, dtype=jnp.int32)).astype(jnp.float32)[
        :, None
    ] * jnp.ones((1, columns), jnp.float32)
    col_pos = jnp.arange(columns, dtype=jnp.float32)[None, :] * jnp.ones(
        (band_rows, 1), jnp.float32
    )
    local_stats = jnp.stack(
        [
            jnp.sum(onehot, axis=(1, 2)),
            jnp.sum(onehot * row_pos, axis=(1, 2)),
            jnp.sum(onehot * col_pos, axis=(1, 2)),
        ],
        0,
    )
    channel_sums = jnp.concatenate(
        [jnp.sum(band, axis=(1, 2), dtype=jnp.float32) for band in (own_band, later_band)]
    )
    frame_totals, inst_stats = all_sum((channel_sums, local_stats), ("row",))
    pooled = (frame_totals / (height * columns)).astype(jnp.bfloat16)
    pool_feature = relu_bf16(jnp.dot(pool_weight, pooled, preferred_element_type=jnp.float32))
    aspp_width = aspp_point.shape[0]
    pool_term = jnp.dot(
        proj_weight[:, 4 * aspp_width :], pool_feature, preferred_element_type=jnp.float32
    )[None]
    projected_flat = aspp_projected(
        flat,
        aspp_point,
        aspp_dilated,
        proj_weight,
        pool_term,
        (front, pitch, aspp_reach, block, blocks),
    )
    projected = projected_flat.reshape(band_rows, pitch, aspp_width)[:, aspp_reach:]
    rimmed = padded_2(projected, (("row", 0),), 2)
    head_kernel = head_weight.reshape(5, 5, *head_weight.shape[1:])
    head_sum = lax.conv_general_dilated(
        rimmed[None],
        head_kernel,
        window_strides=(1, 1),
        padding=((0, 0), (2, 2)),
        dimension_numbers=("NHWC", "HWOI", "NCHW"),
        preferred_element_type=jnp.float32,
    )[0]
    head_out = relu_bf16(head_sum)
    predictions = emit_heads(head_out, out_weight)
    pixel = jnp.einsum("sk,khw->shw", inst_stats, onehot, precision=lax.Precision.HIGHEST)
    counts = jnp.where(counted, pixel[0], 1.0)
    centre_row = pixel[1] / counts
    centre_col = pixel[2] / counts
    distance = (row_pos - centre_row) * (row_pos - centre_row) + (col_pos - centre_col) * (
        col_pos - centre_col
    )
    heat = jnp.where(counted, jnp.exp(-distance / (2.0 * center_sigma * center_sigma)), 0.0)
    center_err = jnp.sum(jnp.square(predictions[0] - heat))
    offset_err = jnp.sum(
        jnp.where(
            counted,
            jnp.abs(predictions[1] - (centre_row - row_pos))
            + jnp.abs(predictions[2] - (centre_col - col_pos)),
            0.0,
        )
    )
    counted_local = jnp.sum(counted.astype(jnp.float32))
    totals = all_sum(jnp.stack([center_err, offset_err, counted_local]), ("row", "tm"))
    center_total, offset_total, counted_total = totals[0], totals[1], totals[2]
    losses = jnp.stack(
        [
            center_total / (frame_count * height * columns),
            offset_weight * offset_total / jnp.maximum(counted_total, 1.0),
        ]
    )
    return (predictions[None], losses)


def solution(mesh):
    placed = (
        P(("grp", "tm"), None, "row", None),
        P("grp"),
        P(("grp", "tm"), "row", None),
        P(("grp", "tm"), "row", None),
        P(),
        P(),
        P(),
        P(),
        P(),
        P(),
    )
    return jax.shard_map(
        shards,
        mesh=mesh,
        in_specs=placed,
        out_specs=(P(("grp", "tm"), None, "row", None), P("grp")),
        check_vma=False,
    )
```

profile of v0, /device:TPU:0, one launch (start us, length us, event | category | flops | bytes accessed | tf_op | source)
XLA Modules:
  0.0 122.1 jit_solution(17372330926107890277)
XLA Ops:
  0.7 6.1 %collective-permute-start.2 = (bf16[256,32,48]{0,2,1:T(8,128)(2,1)}, bf16[256,32,48]{0,2,1:T(8,128)(2,1)S(1)}, u32[]{:S(2)}, u32[]{:S(2)}) collective-permute-start(bf16[256,32,48]{0,2,1:T(8,128)(2,1)} %bitcast.101), channel_id=1, source_target_pairs={{0,14},{2,0},{4,2},{6,4},{8,6},{10,8},{12,10},{14,12},{1,15},{3,1}... | collective-permute-start | bytes 2359304 | tf_op jit(solution)/shard_map/ppermute | solution.py:34
  6.8 2.1 %fusion.42 = (bf16[256,18,48]{0,2,1:T(8,128)(2,1)}, bf16[256,18,48]{0,2,1:T(8,128)(2,1)}) fusion(bf16[256,32,48]{0,2,1:T(8,128)(2,1)} %bitcast.102), kind=kLoop, calls=%fused_computation.64 | loop fusion | bytes 1769472 | tf_op jit(solution)/shard_map/slice | solution.py:24
  8.9 1.5 %collective-permute-start = (bf16[256,18,48]{0,2,1:T(8,128)(2,1)}, bf16[256,18,48]{0,2,1:T(8,128)(2,1)S(1)}, u32[]{:S(2)}, u32[]{:S(2)}) collective-permute-start(bf16[256,18,48]{0,2,1:T(8,128)(2,1)} %get-tuple-element.19), channel_id=1, source_target_pairs={{0,1},{2,3},{4,5},{6,7},{8,9},{10,11},{12,13},{14,15},{16,17},{18,... | collective-permute-start | bytes 1327112 | tf_op jit(solution)/shard_map/ppermute | solution.py:23
  13.8 2.0 %collective-permute-start.8 = (f32[3,64]{1,0:T(4,128)S(1)}, f32[3,64]{1,0:T(4,128)S(1)}, u32[]{:S(2)}, u32[]{:S(2)}) collective-permute-start(f32[3,64]{1,0:T(4,128)S(1)} %pad_maximum_fusion.1), channel_id=1, source_target_pairs={{0,1},{1,0},{2,3},{3,2},{4,5},{5,4},{6,7},{7,6},{8,9},{9,8},{10,11... | collective-permute-start | bytes 2312 | tf_op jit(solution)/shard_map/ppermute | solution.py:46
  17.6 2.9 %fusion.19 = f32[3,32,48]{2,0,1:T(4,128)} fusion(s32[32,48]{1,0:T(8,128)} %bitcast.108, pred[32,48]{1,0:T(8,128)(4,1)S(1)} %get-tuple-element.12, f32[3,64]{1,0:T(4,128)S(1)} %collective-permute-done.8, f32[1,64]{1,0:T(1,128)S(1)} %bitcast.118, f32[1,64]{1,0:T(1,128)S(1)} %bitcast.120, f32[1,64]{1,0:T(1,128)S(1)} %bitcast.116), kind=kOutput, calls=%fused_computation.23 | convolution fusion | flops 3736128 | bytes 27648 | tf_op jit(solution)/shard_map/sk,khw->shw/dot_general | solution.py:217
  20.5 3.4 %collective-permute-done.2 = bf16[256,32,48]{0,2,1:T(8,128)(2,1)S(1)} collective-permute-done((bf16[256,32,48]{0,2,1:T(8,128)(2,1)}, bf16[256,32,48]{0,2,1:T(8,128)(2,1)S(1)}, u32[]{:S(2)}, u32[]{:S(2)}) %collective-permute-start.2) | collective-permute-done | bytes 786464 | tf_op jit(solution)/shard_map/ppermute | solution.py:34
  23.9 1.5 %convert_reduce_fusion = (f32[256]{0:T(256)S(1)}, bf16[256,32,48]{0,2,1:T(8,128)(2,1)S(1)}, f32[256]{0:T(256)S(1)}) fusion(bf16[256,32,48]{0,2,1:T(8,128)(2,1)S(1)} %collective-permute-done.2, bf16[1,256,32,48]{1,3,2,0:T(8,128)(2,1)} %param.10, pred[]{:T(512)} %bitcast.1), kind=kLoop, calls=%fused_computation.10 | loop fusion | flops 1965568 | bytes 2361345 | tf_op jit(solution)/shard_map/reduce_sum | solution.py:187
  25.6 2.4 %collective-permute-start.3 = (bf16[256,18,48]{0,2,1:T(8,128)(2,1)S(1)}, bf16[256,18,48]{0,2,1:T(8,128)(2,1)S(1)}, u32[]{:S(2)}, u32[]{:S(2)}) collective-permute-start(bf16[256,18,48]{0,2,1:T(8,128)(2,1)S(1)} %get-tuple-element.21), channel_id=1, source_target_pairs={{0,1},{2,3},{4,5},{6,7},{8,9},{10,11},{12,13},{14,15},{16,17},{18,... | collective-permute-start | bytes 1327112 | tf_op jit(solution)/shard_map/ppermute | solution.py:23
  29.5 1.7 %fusion.26.pool_ref = f32[1,256]{1,0:T(1,128)} fusion(bf16[256,1]{0,1:T(2,128)(2,1)S(1)} %reshape.67, bf16[256,1280]{1,0:T(8,128)(2,1)} %proj_ref.1), kind=kOutput, calls=%fused_computation.32 | convolution fusion | flops 131072 | bytes 132608 | tf_op jit(solution)/shard_map/dot_general | solution.py:193
  31.7 1.4 %maximum_bitcast_fusion = bf16[68,48,512]{2,1,0:T(8,128)(2,1)S(1)} fusion(bf16[256,18,48]{0,2,1:T(8,128)(2,1)S(1)} %collective-permute-done.4, bf16[256,32,48]{0,2,1:T(8,128)(2,1)S(1)} %get-tuple-element.15, bf16[256,18,48]{0,2,1:T(8,128)(2,1)S(1)} %collective-permute-done.3, bf16[256,18,48]{0,2,1:T(8,128)(2,1)} %collective-permute-done.1, ...), kind=kLoop, calls=%fused_computation.1 | loop fusion | flops 20054016 | bytes 6684672 | tf_op jit(solution)/shard_map/transpose | solution.py:163
  33.1 4.5 %pad.8 = bf16[68,66,512]{2,1,0:T(8,128)(2,1)} pad(bf16[68,48,512]{2,1,0:T(8,128)(2,1)S(1)} %maximum_bitcast_fusion, bf16[]{:T(256)} %constant.50.clone.1), padding=0_0x18_0x0_0 | pad | bytes 7938050 | tf_op jit(solution)/shard_map/jit(_pad)/pad | solution.py:162
  37.6 7.8 %reshape.44 = bf16[4488,512]{1,0:T(8,128)(2,1)} reshape(bf16[68,66,512]{2,1,0:T(8,128)(2,1)} %pad.8) | data formatting | bytes 9191424 | tf_op jit(solution)/shard_map/reshape | solution.py:164
  45.4 7.2 %pad_convert_fusion.x_ref = f32[4536,512]{1,0:T(8,128)} fusion(bf16[4488,512]{1,0:T(8,128)(2,1)} %reshape.44), kind=kLoop, calls=%fused_computation | loop fusion | flops 2322432 | bytes 13885440 | tf_op jit(solution)/shard_map/convert_element_type | solution.py:165
  52.6 29.1 %shard_map.113 = bf16[2112,256]{1,0:T(8,128)(2,1)} custom-call(f32[4536,512]{1,0:T(8,128)} %pad_convert_fusion.x_ref, bf16[256,512]{1,0:T(8,128)(2,1)} %point_ref.1, bf16[3,9,256,512]{3,2,1,0:T(8,128)(2,1)} %dilated_ref.1, bf16[256,1280]{1,0:T(8,128)(2,1)} %proj_ref.1, f32[1,256]{1,0:T(1,128)} %fusion.26.pool_ref), custom_call_target="tpu_custom_call" | custom-call | flops 16609443840 | bytes 17448960 | tf_op jit(solution)/shard_map/pallas_call | solution.py:96
  81.7 1.4 %reshape.45 = bf16[32,66,256]{2,1,0:T(8,128)(2,1)S(1)} reshape(bf16[2112,256]{1,0:T(8,128)(2,1)} %shard_map.113) | data formatting | bytes 2162688 | tf_op jit(solution)/shard_map/reshape | solution.py:204
  83.1 2.6 %collective-permute-start.6 = (bf16[2,48,256]{2,1,0:T(8,128)(2,1)S(1)}, bf16[2,48,256]{2,1,0:T(8,128)(2,1)S(1)}, u32[]{:S(2)}, u32[]{:S(2)}) collective-permute-start(bf16[2,48,256]{2,1,0:T(8,128)(2,1)S(1)} %get-tuple-element.16), channel_id=1, source_target_pairs={{0,1},{2,3},{4,5},{6,7},{8,9},{10,11},{12,13},{14,15},{16,17},{18,... | collective-permute-start | bytes 147464 | tf_op jit(solution)/shard_map/ppermute | solution.py:23
  90.7 6.1 %fusion.14 = bf16[32,8,7,96]{3,1,2,0:T(8,128)(2,1)S(1)} fusion(bf16[5,5,96,256]{3,2,1,0:T(8,128)(2,1)S(1)} %bitcast.100, bf16[36,1,7,4,256]{4,2,3,0,1:T(8,128)(2,1)S(1)} %slice.119, bf16[36,1,8,7,256]{4,2,3,0,1:T(8,128)(2,1)S(1)} %copy.19, pred[8,7]{0,1:T(8,128)(4,1)S(1)} %copy-done.6), kind=kOutput, calls=%fused_computation.14 | convolution fusion | flops 2207391744 | bytes 3121208 | tf_op jit(solution)/shard_map/conv_general_dilated | solution.py:207
  99.8 2.0 %pad_maximum_fusion.2 = f32[3]{0:T(128)S(1)} fusion(f32[1]{0:T(128)} %bitcast.41, f32[1]{0:T(128)} %bitcast.40, f32[1]{0:T(128)} %bitcast.37), kind=kLoop, calls=%fused_computation.51 | loop fusion | flops 6 | bytes 24 | tf_op jit(solution)/shard_map/stack | solution.py:235
  103.4 2.0 %fusion.53 = f32[3]{0:T(128)S(1)} fusion(f32[3]{0:T(128)S(1)} %collective-permute-done.9, f32[1]{0:T(128)} %bitcast.41, f32[1]{0:T(128)} %bitcast.40, f32[1]{0:T(128)} %bitcast.37), kind=kLoop, calls=%fused_computation.71 | loop fusion | flops 9 | bytes 36 | tf_op jit(solution)/shard_map/add | solution.py:47
  105.6 3.3 %collective-permute-done.10 = f32[3]{0:T(128)S(1)} collective-permute-done((f32[3]{0:T(128)S(1)}, f32[3]{0:T(128)S(1)}, u32[]{:S(2)}, u32[]{:S(2)}) %collective-permute-start.10) | collective-permute-done | bytes 44 | tf_op jit(solution)/shard_map/ppermute | solution.py:46
  108.9 2.0 %fusion.54 = f32[3]{0:T(128)S(1)} fusion(f32[3]{0:T(128)S(1)} %collective-permute-done.10, f32[3]{0:T(128)S(1)} %collective-permute-done.9, f32[1]{0:T(128)} %bitcast.41, f32[1]{0:T(128)} %bitcast.40, f32[1]{0:T(128)} %bitcast.37), kind=kLoop, calls=%fused_computation.72 | loop fusion | flops 12 | bytes 48 | tf_op jit(solution)/shard_map/add | solution.py:47
  110.9 3.6 %collective-permute-done.11 = f32[3]{0:T(128)S(1)} collective-permute-done((f32[3]{0:T(128)S(1)}, f32[3]{0:T(128)S(1)}, u32[]{:S(2)}, u32[]{:S(2)}) %collective-permute-start.11) | collective-permute-done | bytes 44 | tf_op jit(solution)/shard_map/ppermute | solution.py:46
  114.5 2.2 %collective-permute-start.12 = (f32[3]{0:T(128)S(1)}, f32[3]{0:T(128)S(1)}, u32[]{:S(2)}, u32[]{:S(2)}) collective-permute-start(f32[3]{0:T(128)S(1)} %add.60), channel_id=1, source_target_pairs={{0,8},{2,10},{4,12},{6,14},{8,0},{10,2},{12,4},{14,6},{1,9},{3,11}... | collective-permute-start | bytes 44 | tf_op jit(solution)/shard_map/ppermute | solution.py:46
  116.6 2.3 %collective-permute-done.12 = f32[3]{0:T(128)S(1)} collective-permute-done((f32[3]{0:T(128)S(1)}, f32[3]{0:T(128)S(1)}, u32[]{:S(2)}, u32[]{:S(2)}) %collective-permute-start.12) | collective-permute-done | bytes 44 | tf_op jit(solution)/shard_map/ppermute | solution.py:46
  (70 shorter events, 17.7 us)
Async XLA Ops:
  0.6 90.0 %copy-start = (bf16[25,96,256]{2,1,0:T(8,128)(2,1)S(1)}, bf16[25,96,256]{2,1,0:T(8,128)(2,1)}, u32[]{:S(2)}) copy-start(bf16[25,96,256]{2,1,0:T(8,128)(2,1)} %param.18) | copy-start | bytes 3686404
  0.6 28.7 %copy-start.2 = (bf16[256,512]{1,0:T(8,128)(2,1)S(1)}, bf16[256,512]{1,0:T(8,128)(2,1)}, u32[]{:S(2)}) copy-start(bf16[256,512]{1,0:T(8,128)(2,1)} %param.16) | copy-start | bytes 786436
  0.7 31.0 %copy-start.1 = (bf16[1,256,32,48]{1,3,2,0:T(8,128)(2,1)S(1)}, bf16[1,256,32,48]{1,3,2,0:T(8,128)(2,1)}, u32[]{:S(2)}) copy-start(bf16[1,256,32,48]{1,3,2,0:T(8,128)(2,1)} %param.10) | copy-start | bytes 2359300
  0.7 23.2 %collective-permute-start.2 = (bf16[256,32,48]{0,2,1:T(8,128)(2,1)}, bf16[256,32,48]{0,2,1:T(8,128)(2,1)S(1)}, u32[]{:S(2)}, u32[]{:S(2)}) collective-permute-start(bf16[256,32,48]{0,2,1:T(8,128)(2,1)} %bitcast.101), channel_id=1, source_target_pairs={{0,14},{2,0},{4,2},{6,4},{8,6},{10,8},{12,10},{14,12},{1,15},{3,1}... | collective-permute-start | bytes 2359304 | tf_op jit(solution)/shard_map/ppermute | solution.py:34
  8.9 22.3 %collective-permute-start = (bf16[256,18,48]{0,2,1:T(8,128)(2,1)}, bf16[256,18,48]{0,2,1:T(8,128)(2,1)S(1)}, u32[]{:S(2)}, u32[]{:S(2)}) collective-permute-start(bf16[256,18,48]{0,2,1:T(8,128)(2,1)} %get-tuple-element.19), channel_id=1, source_target_pairs={{0,1},{2,3},{4,5},{6,7},{8,9},{10,11},{12,13},{14,15},{16,17},{18,... | collective-permute-start | bytes 1327112 | tf_op jit(solution)/shard_map/ppermute | solution.py:23
  10.4 20.9 %collective-permute-start.1 = (bf16[256,18,48]{0,2,1:T(8,128)(2,1)}, bf16[256,18,48]{0,2,1:T(8,128)(2,1)}, u32[]{:S(2)}, u32[]{:S(2)}) collective-permute-start(bf16[256,18,48]{0,2,1:T(8,128)(2,1)} %get-tuple-element.20), channel_id=1, source_target_pairs={{1,0},{3,2},{5,4},{7,6},{9,8},{11,10},{13,12},{15,14},{17,16},{19,... | collective-permute-start | bytes 1327112 | tf_op jit(solution)/shard_map/ppermute | solution.py:26
  13.8 3.8 %collective-permute-start.8 = (f32[3,64]{1,0:T(4,128)S(1)}, f32[3,64]{1,0:T(4,128)S(1)}, u32[]{:S(2)}, u32[]{:S(2)}) collective-permute-start(f32[3,64]{1,0:T(4,128)S(1)} %pad_maximum_fusion.1), channel_id=1, source_target_pairs={{0,1},{1,0},{2,3},{3,2},{4,5},{5,4},{6,7},{7,6},{8,9},{9,8},{10,11... | collective-permute-start | bytes 2312 | tf_op jit(solution)/shard_map/ppermute | solution.py:46
  25.4 3.9 %collective-permute-start.5 = (f32[512]{0:T(512)S(1)}, f32[512]{0:T(512)S(1)}, u32[]{:S(2)}, u32[]{:S(2)}) collective-permute-start(f32[512]{0:T(512)S(1)} %pad_maximum_fusion), channel_id=1, source_target_pairs={{0,1},{1,0},{2,3},{3,2},{4,5},{5,4},{6,7},{7,6},{8,9},{9,8},{10,11... | collective-permute-start | bytes 6152 | tf_op jit(solution)/shard_map/ppermute | solution.py:46
  25.6 5.7 %collective-permute-start.3 = (bf16[256,18,48]{0,2,1:T(8,128)(2,1)S(1)}, bf16[256,18,48]{0,2,1:T(8,128)(2,1)S(1)}, u32[]{:S(2)}, u32[]{:S(2)}) collective-permute-start(bf16[256,18,48]{0,2,1:T(8,128)(2,1)S(1)} %get-tuple-element.21), channel_id=1, source_target_pairs={{0,1},{2,3},{4,5},{6,7},{8,9},{10,11},{12,13},{14,15},{16,17},{18,... | collective-permute-start | bytes 1327112 | tf_op jit(solution)/shard_map/ppermute | solution.py:23
  28.0 3.7 %collective-permute-start.4 = (bf16[256,18,48]{0,2,1:T(8,128)(2,1)S(1)}, bf16[256,18,48]{0,2,1:T(8,128)(2,1)S(1)}, u32[]{:S(2)}, u32[]{:S(2)}) collective-permute-start(bf16[256,18,48]{0,2,1:T(8,128)(2,1)S(1)} %get-tuple-element.22), channel_id=1, source_target_pairs={{1,0},{3,2},{5,4},{7,6},{9,8},{11,10},{13,12},{15,14},{17,16},{19,... | collective-permute-start | bytes 1327112 | tf_op jit(solution)/shard_map/ppermute | solution.py:26
  52.6 34.4 %copy-start.4 = (f32[3,32,48]{2,0,1:T(4,128)S(1)}, f32[3,32,48]{2,0,1:T(4,128)}, u32[]{:S(2)}) copy-start(f32[3,32,48]{2,0,1:T(4,128)} %fusion.19) | copy-start | bytes 55300
  83.1 4.4 %collective-permute-start.6 = (bf16[2,48,256]{2,1,0:T(8,128)(2,1)S(1)}, bf16[2,48,256]{2,1,0:T(8,128)(2,1)S(1)}, u32[]{:S(2)}, u32[]{:S(2)}) collective-permute-start(bf16[2,48,256]{2,1,0:T(8,128)(2,1)S(1)} %get-tuple-element.16), channel_id=1, source_target_pairs={{0,1},{2,3},{4,5},{6,7},{8,9},{10,11},{12,13},{14,15},{16,17},{18,... | collective-permute-start | bytes 147464 | tf_op jit(solution)/shard_map/ppermute | solution.py:23
  85.7 3.1 %collective-permute-start.7 = (bf16[2,48,256]{2,1,0:T(8,128)(2,1)S(1)}, bf16[2,48,256]{2,1,0:T(8,128)(2,1)S(1)}, u32[]{:S(2)}, u32[]{:S(2)}) collective-permute-start(bf16[2,48,256]{2,1,0:T(8,128)(2,1)S(1)} %get-tuple-element.17), channel_id=1, source_target_pairs={{1,0},{3,2},{5,4},{7,6},{9,8},{11,10},{13,12},{15,14},{17,16},{19,... | collective-permute-start | bytes 147464 | tf_op jit(solution)/shard_map/ppermute | solution.py:26
  89.0 1.7 %copy-start.6 = (pred[8,7]{0,1:T(8,128)(4,1)S(1)}, pred[8,7]{0,1:T(8,128)(4,1)}, u32[]{:S(2)}) copy-start(pred[8,7]{0,1:T(8,128)(4,1)} %constant.71) | copy-start | bytes 172
  96.8 0.7 copy-start.5
  96.8 2.2 %copy-start.3 = (s32[1,32,48]{2,1,0:T(8,128)S(1)}, s32[1,32,48]{2,1,0:T(8,128)}, u32[]{:S(2)}) copy-start(s32[1,32,48]{2,1,0:T(8,128)} %param.13) | copy-start | bytes 18436
  101.7 1.7 %collective-permute-start.9 = (f32[3]{0:T(128)S(1)}, f32[3]{0:T(128)S(1)}, u32[]{:S(2)}, u32[]{:S(2)}) collective-permute-start(f32[3]{0:T(128)S(1)} %pad_maximum_fusion.2), channel_id=1, source_target_pairs={{0,1},{1,0},{2,3},{3,2},{4,5},{5,4},{6,7},{7,6},{8,9},{9,8},{10,11... | collective-permute-start | bytes 44 | tf_op jit(solution)/shard_map/ppermute | solution.py:46
  105.3 3.6 %collective-permute-start.10 = (f32[3]{0:T(128)S(1)}, f32[3]{0:T(128)S(1)}, u32[]{:S(2)}, u32[]{:S(2)}) collective-permute-start(f32[3]{0:T(128)S(1)} %fusion.53), channel_id=1, source_target_pairs={{0,2},{2,0},{4,6},{6,4},{8,10},{10,8},{12,14},{14,12},{1,3},{3,1},... | collective-permute-start | bytes 44 | tf_op jit(solution)/shard_map/ppermute | solution.py:46
  110.9 3.6 %collective-permute-start.11 = (f32[3]{0:T(128)S(1)}, f32[3]{0:T(128)S(1)}, u32[]{:S(2)}, u32[]{:S(2)}) collective-permute-start(f32[3]{0:T(128)S(1)} %fusion.54), channel_id=1, source_target_pairs={{0,4},{2,6},{4,0},{6,2},{8,12},{10,14},{12,8},{14,10},{1,5},{3,7},... | collective-permute-start | bytes 44 | tf_op jit(solution)/shard_map/ppermute | solution.py:46
  114.5 4.5 %collective-permute-start.12 = (f32[3]{0:T(128)S(1)}, f32[3]{0:T(128)S(1)}, u32[]{:S(2)}, u32[]{:S(2)}) collective-permute-start(f32[3]{0:T(128)S(1)} %add.60), channel_id=1, source_target_pairs={{0,8},{2,10},{4,12},{6,14},{8,0},{10,2},{12,4},{14,6},{1,9},{3,11}... | collective-permute-start | bytes 44 | tf_op jit(solution)/shard_map/ppermute | solution.py:46
where the time goes:
time: 123 us; the launch traced here: 122 us
  Pallas kernels  29.1 us (24%)
  local copies, waits for them, and re-layouts  22.2 us (18%)
  starting transfers between devices  21.1 us (17%)
  other arithmetic  19.7 us (16%)
  waiting for transfers between devices  14.4 us (12%)
  matrix products  12.1 us (10%)
  between operations  3.59 us (3%)
    pallas_call x1, Pallas kernels, aspp_projected(): pl.pallas_call(body, out_shape=jax.ShapeDtypeStruct((blocks * block, widt...  29.1 us
    ppermute x6, waiting for transfers between devices, all_sum(): other = lax.ppermute(value, axis, pairs)  9.21 us
    reshape x1, local copies, waits for them, and re-layouts, shards(): flat = jnp.pad(jnp.transpose(joined_wide, (1, 2, 0)), ((0, 0), (aspp_reac...  7.78 us
    convert_element_type x1, other arithmetic, shards(): jnp.pad(flat, ((front, length - front - wide_rows * pitch), (0, 0)))  7.21 us
    ppermute x3, starting transfers between devices, padded_2(): lax.ppermute(lax.slice_in_dim(block, block.shape[dim] - width, None, axis...  6.54 us
    conv_general_dilated x1, matrix products, shards(): lax.conv_general_dilated(rimmed[None], head_kernel, window_strides=(1, 1)...  6.1 us
    ppermute x1, starting transfers between devices, shifted(): return lax.ppermute(value, axis, pairs)  6.09 us
    ppermute x6, starting transfers between devices, all_sum(): other = lax.ppermute(value, axis, pairs)  4.6 us
  transfers between devices with their start and end apart: 13, of which 6 were waited for; matrix products, arithmetic and copies ran while one was open for 11% of the time, Pallas kernels for 0%

commit v1 on v0

--- a/solution.py
+++ b/solution.py
@@ -153,18 +153,15 @@
 
     joined_wide = jnp.concatenate([widen(own_band), widen(later_band)], 0)
     wide_rows = joined_wide.shape[1]
-    pitch = columns + aspp_reach
-    front = 24
+    pitch = -(-(columns + aspp_reach) // 8) * 8
+    front = pitch
     block_rows = 8 if band_rows % 8 == 0 else band_rows
     block = block_rows * pitch
     blocks = band_rows // block_rows
-    length = -(-(front + wide_rows * pitch + aspp_reach) // 8) * 8
     flat = jnp.pad(
-        jnp.transpose(joined_wide, (1, 2, 0)), ((0, 0), (aspp_reach, 0), (0, 0))
-    ).reshape(wide_rows * pitch, 2 * channel_count)
-    flat = jnp.pad(flat, ((front, length - front - wide_rows * pitch), (0, 0))).astype(
-        jnp.float32
-    )
+        jnp.transpose(joined_wide, (1, 2, 0)).astype(jnp.float32),
+        ((1, 1), (pitch - columns, 0), (0, 0)),
+    ).reshape((wide_rows + 2) * pitch, 2 * channel_count)
 
     counted = (semantic[0] >= THING_FIRST) & (instance[0] > 0)
     labels = jnp.arange(INSTANCES, dtype=jnp.int32)
@@ -201,7 +198,7 @@
         pool_term,
         (front, pitch, aspp_reach, block, blocks),
     )
-    projected = projected_flat.reshape(band_rows, pitch, aspp_width)[:, aspp_reach:]
+    projected = projected_flat.reshape(band_rows, pitch, aspp_width)[:, pitch - columns :]
     rimmed = padded_2(projected, (("row", 0),), 2)
     head_kernel = head_weight.reshape(5, 5, *head_weight.shape[1:])
     head_sum = lax.conv_general_dilated(
@@ -232,7 +229,8 @@
         )
     )
     counted_local = jnp.sum(counted.astype(jnp.float32))
-    totals = all_sum(jnp.stack([center_err, offset_err, counted_local]), ("row", "tm"))
+    local_totals = lax.optimization_barrier(jnp.stack([center_err, offset_err, counted_local]))
+    totals = all_sum(local_totals, ("row", "tm"))
     center_total, offset_total, counted_total = totals[0], totals[1], totals[2]
     losses = jnp.stack(
         [

time: 123 us -> 108 us (0.88)
  local copies, waits for them, and re-layouts: 22.2 us -> 10.4 us
  other arithmetic: 19.7 us -> 14.6 us
  Pallas kernels: 29.1 us -> 31.3 us
    reshape x2 -> x0, local copies, waits for them, and re-layouts: 9.14 us -> none  [the longest x1 7.78 us: shards(): flat = jnp.pad(jnp.transpose(joined_wide, (1, 2, 0)), ((0, 0), (aspp_reac...]
    reshape x0 -> x1, other arithmetic: none -> 5.93 us  [shards(): flat = jnp.pad(jnp.transpose(joined_wide, (1, 2, 0)).astype(jnp.float32),...]
    convert_element_type x1, other arithmetic: 7.21 us -> 1.4 us  [shards(): jnp.transpose(joined_wide, (1, 2, 0)).astype(jnp.float32)]
    pad x1, local copies, waits for them, and re-layouts: 4.54 us -> 0.35 us  [shards(): jnp.pad(jnp.transpose(joined_wide, (1, 2, 0)).astype(jnp.float32), ((1, 1...]
    add x4, other arithmetic: 3.93 us -> 0.01 us  [all_sum(): value = jax.tree.map(jnp.add, value, other)]
    pallas_call x1, Pallas kernels: 29.1 us -> 31.3 us  [aspp_projected(): pl.pallas_call(body, out_shape=jax.ShapeDtypeStruct((blocks * block, widt...]
    transpose x1 -> x0, other arithmetic: 1.4 us -> none  [shards(): jnp.transpose(joined_wide, (1, 2, 0))]
  transfers between devices with their start and end apart: 13 -> 13, of which waited for: 6 -> 6; matrix products, arithmetic and copies ran while one was open for 11% -> 13% of each run, Pallas kernels for 0% -> 0%
where the time goes in v1:
time: 108 us; the launch traced here: 107 us
  Pallas kernels  31.3 us (29%)
  starting transfers between devices  21.4 us (20%)
  other arithmetic  14.6 us (14%)
  waiting for transfers between devices  14.3 us (13%)
  matrix products  11.5 us (11%)
  local copies, waits for them, and re-layouts  10.4 us (10%)
  between operations  3.57 us (3%)
    pallas_call x1, Pallas kernels, aspp_projected(): pl.pallas_call(body, out_shape=jax.ShapeDtypeStruct((blocks * block, widt...  31.3 us
    ppermute x6, waiting for transfers between devices, all_sum(): other = lax.ppermute(value, axis, pairs)  9.22 us
    ppermute x3, starting transfers between devices, padded_2(): lax.ppermute(lax.slice_in_dim(block, block.shape[dim] - width, None, axis...  6.5 us
    conv_general_dilated x1, matrix products, shards(): lax.conv_general_dilated(rimmed[None], head_kernel, window_strides=(1, 1)...  6.1 us
    ppermute x1, starting transfers between devices, shifted(): return lax.ppermute(value, axis, pairs)  6.09 us
    reshape x1, other arithmetic, shards(): flat = jnp.pad(jnp.transpose(joined_wide, (1, 2, 0)).astype(jnp.float32),...  5.93 us
    ppermute x6, starting transfers between devices, all_sum(): other = lax.ppermute(value, axis, pairs)  4.97 us
    ppermute x1, waiting for transfers between devices, shifted(): return lax.ppermute(value, axis, pairs)  4.03 us
  transfers between devices with their start and end apart: 13, of which 6 were waited for; matrix products, arithmetic and copies ran while one was open for 13% of the time, Pallas kernels for 0%

profile of v1, /device:TPU:0, one launch (start us, length us, event | category | flops | bytes accessed | tf_op | source)
XLA Modules:
  0.0 107.1 jit_solution(14636993458684565173)
XLA Ops:
  0.7 6.1 %collective-permute-start.2 = (bf16[256,32,48]{0,2,1:T(8,128)(2,1)}, bf16[256,32,48]{0,2,1:T(8,128)(2,1)S(1)}, u32[]{:S(2)}, u32[]{:S(2)}) collective-permute-start(bf16[256,32,48]{0,2,1:T(8,128)(2,1)} %bitcast.105), channel_id=1, source_target_pairs={{0,14},{2,0},{4,2},{6,4},{8,6},{10,8},{12,10},{14,12},{1,15},{3,1}... | collective-permute-start | bytes 2359304 | tf_op jit(solution)/shard_map/ppermute | solution.py:34
  6.8 2.1 %fusion.42 = (bf16[256,18,48]{0,2,1:T(8,128)(2,1)}, bf16[256,18,48]{0,2,1:T(8,128)(2,1)}) fusion(bf16[256,32,48]{0,2,1:T(8,128)(2,1)} %bitcast.106), kind=kLoop, calls=%fused_computation.64 | loop fusion | bytes 1769472 | tf_op jit(solution)/shard_map/slice | solution.py:24
  8.9 1.5 %collective-permute-start = (bf16[256,18,48]{0,2,1:T(8,128)(2,1)}, bf16[256,18,48]{0,2,1:T(8,128)(2,1)S(1)}, u32[]{:S(2)}, u32[]{:S(2)}) collective-permute-start(bf16[256,18,48]{0,2,1:T(8,128)(2,1)} %get-tuple-element.19), channel_id=1, source_target_pairs={{0,1},{2,3},{4,5},{6,7},{8,9},{10,11},{12,13},{14,15},{16,17},{18,... | collective-permute-start | bytes 1327112 | tf_op jit(solution)/shard_map/ppermute | solution.py:23
  10.4 1.3 %collective-permute-start.1 = (bf16[256,18,48]{0,2,1:T(8,128)(2,1)}, bf16[256,18,48]{0,2,1:T(8,128)(2,1)}, u32[]{:S(2)}, u32[]{:S(2)}) collective-permute-start(bf16[256,18,48]{0,2,1:T(8,128)(2,1)} %get-tuple-element.20), channel_id=1, source_target_pairs={{1,0},{3,2},{5,4},{7,6},{9,8},{11,10},{13,12},{15,14},{17,16},{19,... | collective-permute-start | bytes 1327112 | tf_op jit(solution)/shard_map/ppermute | solution.py:26
  12.4 1.3 %convert_reduce_fusion.2 = (f32[64]{0:T(128)S(1)}, f32[64]{0:T(128)S(1)}, f32[64]{0:T(128)S(1)}) fusion(s32[32,48]{1,0:T(8,128)} %bitcast.113, pred[32,48]{1,0:T(8,128)(4,1)S(1)} %get-tuple-element.12, f32[32]{0:T(128)S(1)} %add_convert_fusion), kind=kLoop, calls=%fused_computation.20 | loop fusion | flops 786240 | bytes 8576 | tf_op jit(solution)/shard_map/reduce_sum | solution.py:177
  13.8 1.9 %collective-permute-start.8 = (f32[3,64]{1,0:T(4,128)S(1)}, f32[3,64]{1,0:T(4,128)S(1)}, u32[]{:S(2)}, u32[]{:S(2)}) collective-permute-start(f32[3,64]{1,0:T(4,128)S(1)} %pad_maximum_fusion.1), channel_id=1, source_target_pairs={{0,1},{1,0},{2,3},{3,2},{4,5},{5,4},{6,7},{7,6},{8,9},{9,8},{10,11... | collective-permute-start | bytes 2312 | tf_op jit(solution)/shard_map/ppermute | solution.py:46
  15.7 1.2 %dynamic_slice.4 = s32[1]{0:T(128)} dynamic-slice(s32[8]{0:T(128)} %param.11, s32[]{:T(128)S(6)} %select_n.30), dynamic_slice_sizes={1} | dynamic-slice | bytes 12 | tf_op jit(solution)/shard_map/jit(dynamic_index_in_dim)/dynamic_slice | solution.py:145
  17.6 2.2 %fusion.19 = f32[3,32,48]{2,0,1:T(4,128)S(1)} fusion(s32[32,48]{1,0:T(8,128)} %bitcast.114, pred[32,48]{1,0:T(8,128)(4,1)S(1)} %get-tuple-element.12, f32[3,64]{1,0:T(4,128)S(1)} %collective-permute-done.8, f32[1,64]{1,0:T(1,128)S(1)} %bitcast.124, f32[1,64]{1,0:T(1,128)S(1)} %bitcast.126, f32[1,64]{1,0:T(1,128)S(1)} %bitcast.122), kind=kOutput, calls=%fused_computation.23 | convolution fusion | flops 3736128 | bytes 27648 | tf_op jit(solution)/shard_map/sk,khw->shw/dot_general | solution.py:214
  19.8 4.0 %collective-permute-done.2 = bf16[256,32,48]{0,2,1:T(8,128)(2,1)S(1)} collective-permute-done((bf16[256,32,48]{0,2,1:T(8,128)(2,1)}, bf16[256,32,48]{0,2,1:T(8,128)(2,1)S(1)}, u32[]{:S(2)}, u32[]{:S(2)}) %collective-permute-start.2) | collective-permute-done | bytes 786464 | tf_op jit(solution)/shard_map/ppermute | solution.py:34
  23.9 1.5 %convert_reduce_fusion = (f32[256]{0:T(256)S(1)}, bf16[256,32,48]{0,2,1:T(8,128)(2,1)S(1)}, f32[256]{0:T(256)S(1)}) fusion(bf16[256,32,48]{0,2,1:T(8,128)(2,1)S(1)} %collective-permute-done.2, bf16[1,256,32,48]{1,3,2,0:T(8,128)(2,1)} %param.10, pred[]{:T(512)} %bitcast.1), kind=kLoop, calls=%fused_computation.10 | loop fusion | flops 1965568 | bytes 2361345 | tf_op jit(solution)/shard_map/reduce_sum | solution.py:184
  25.6 2.4 %collective-permute-start.3 = (bf16[256,18,48]{0,2,1:T(8,128)(2,1)S(1)}, bf16[256,18,48]{0,2,1:T(8,128)(2,1)S(1)}, u32[]{:S(2)}, u32[]{:S(2)}) collective-permute-start(bf16[256,18,48]{0,2,1:T(8,128)(2,1)S(1)} %get-tuple-element.21), channel_id=1, source_target_pairs={{0,1},{2,3},{4,5},{6,7},{8,9},{10,11},{12,13},{14,15},{16,17},{18,... | collective-permute-start | bytes 1327112 | tf_op jit(solution)/shard_map/ppermute | solution.py:23
  28.0 1.3 %collective-permute-start.4 = (bf16[256,18,48]{0,2,1:T(8,128)(2,1)S(1)}, bf16[256,18,48]{0,2,1:T(8,128)(2,1)S(1)}, u32[]{:S(2)}, u32[]{:S(2)}) collective-permute-start(bf16[256,18,48]{0,2,1:T(8,128)(2,1)S(1)} %get-tuple-element.22), channel_id=1, source_target_pairs={{1,0},{3,2},{5,4},{7,6},{9,8},{11,10},{13,12},{15,14},{17,16},{19,... | collective-permute-start | bytes 1327112 | tf_op jit(solution)/shard_map/ppermute | solution.py:26
  29.5 1.7 %fusion.26.pool_ref = f32[1,256]{1,0:T(1,128)} fusion(bf16[256,1]{0,1:T(2,128)(2,1)S(1)} %reshape.72, bf16[256,1280]{1,0:T(8,128)(2,1)} %proj_ref.1), kind=kOutput, calls=%fused_computation.32 | convolution fusion | flops 131072 | bytes 132608 | tf_op jit(solution)/shard_map/dot_general | solution.py:190
  31.7 1.4 %maximum_bitcast_fusion = bf16[68,48,512]{2,1,0:T(8,128)(2,1)S(1)} fusion(bf16[256,18,48]{0,2,1:T(8,128)(2,1)S(1)} %collective-permute-done.4, bf16[256,32,48]{0,2,1:T(8,128)(2,1)S(1)} %get-tuple-element.15, bf16[256,18,48]{0,2,1:T(8,128)(2,1)S(1)} %collective-permute-done.3, bf16[256,18,48]{0,2,1:T(8,128)(2,1)} %collective-permute-done.1, ...), kind=kLoop, calls=%fused_computation.1 | loop fusion | flops 20054016 | bytes 6684672 | tf_op jit(solution)/shard_map/convert_element_type | solution.py:162
  33.5 5.9 %bitcast_convert_fusion.x_ref = f32[5040,512]{1,0:T(8,128)} fusion(bf16[70,72,512]{2,1,0:T(8,128)(2,1)S(1)} %pad.5), kind=kLoop, calls=%fused_computation | loop fusion | flops 2580480 | bytes 15482880 | tf_op jit(solution)/shard_map/reshape | solution.py:164
  39.4 31.3 %shard_map.113 = bf16[2304,256]{1,0:T(8,128)(2,1)} custom-call(f32[5040,512]{1,0:T(8,128)} %bitcast_convert_fusion.x_ref, bf16[256,512]{1,0:T(8,128)(2,1)} %point_ref.1, bf16[3,9,256,512]{3,2,1,0:T(8,128)(2,1)} %dilated_ref.1, bf16[256,1280]{1,0:T(8,128)(2,1)} %proj_ref.1, f32[1,256]{1,0:T(1,128)} %fusion.26.pool_ref), custom_call_target="tpu_custom_call" | custom-call | flops 18119393280 | bytes 18579456 | tf_op jit(solution)/shard_map/pallas_call | solution.py:96
  71.5 2.6 %collective-permute-start.6 = (bf16[2,48,256]{2,1,0:T(8,128)(2,1)S(1)}, bf16[2,48,256]{2,1,0:T(8,128)(2,1)S(1)}, u32[]{:S(2)}, u32[]{:S(2)}) collective-permute-start(bf16[2,48,256]{2,1,0:T(8,128)(2,1)S(1)} %get-tuple-element.16), channel_id=1, source_target_pairs={{0,1},{2,3},{4,5},{6,7},{8,9},{10,11},{12,13},{14,15},{16,17},{18,... | collective-permute-start | bytes 147464 | tf_op jit(solution)/shard_map/ppermute | solution.py:23
  74.1 1.3 %collective-permute-start.7 = (bf16[2,48,256]{2,1,0:T(8,128)(2,1)S(1)}, bf16[2,48,256]{2,1,0:T(8,128)(2,1)S(1)}, u32[]{:S(2)}, u32[]{:S(2)}) collective-permute-start(bf16[2,48,256]{2,1,0:T(8,128)(2,1)S(1)} %get-tuple-element.17), channel_id=1, source_target_pairs={{1,0},{3,2},{5,4},{7,6},{9,8},{11,10},{13,12},{15,14},{17,16},{19,... | collective-permute-start | bytes 147464 | tf_op jit(solution)/shard_map/ppermute | solution.py:26
  79.1 6.1 %fusion.14 = bf16[32,8,7,96]{3,1,2,0:T(8,128)(2,1)S(1)} fusion(bf16[5,5,96,256]{3,2,1,0:T(8,128)(2,1)S(1)} %bitcast.104, bf16[36,1,7,4,256]{4,2,3,0,1:T(8,128)(2,1)S(1)} %slice.119, bf16[36,1,8,7,256]{4,2,3,0,1:T(8,128)(2,1)S(1)} %copy.19, pred[8,7]{0,1:T(8,128)(4,1)S(1)} %copy-done.5), kind=kOutput, calls=%fused_computation.14 | convolution fusion | flops 2207391744 | bytes 3121208 | tf_op jit(solution)/shard_map/conv_general_dilated | solution.py:204
  88.2 2.1 %pad_maximum_fusion.2 = f32[3]{0:T(128)S(1)} fusion(f32[1]{0:T(128)} %bitcast.43, f32[1]{0:T(128)} %bitcast.42, f32[1]{0:T(128)} %bitcast.39), kind=kLoop, calls=%fused_computation.51 | loop fusion | flops 6 | bytes 24 | tf_op jit(solution)/shard_map/stack | solution.py:232
  92.5 3.3 %collective-permute-done.10 = f32[3]{0:T(128)S(1)} collective-permute-done((f32[3]{0:T(128)S(1)}, f32[3]{0:T(128)S(1)}, u32[]{:S(2)}, u32[]{:S(2)}) %collective-permute-start.10) | collective-permute-done | bytes 44 | tf_op jit(solution)/shard_map/ppermute | solution.py:46
  95.9 3.6 %collective-permute-done.11 = f32[3]{0:T(128)S(1)} collective-permute-done((f32[3]{0:T(128)S(1)}, f32[3]{0:T(128)S(1)}, u32[]{:S(2)}, u32[]{:S(2)}) %collective-permute-start.11) | collective-permute-done | bytes 44 | tf_op jit(solution)/shard_map/ppermute | solution.py:46
  99.4 2.2 %collective-permute-start.12 = (f32[3]{0:T(128)S(1)}, f32[3]{0:T(128)S(1)}, u32[]{:S(2)}, u32[]{:S(2)}) collective-permute-start(f32[3]{0:T(128)S(1)} %add.58), channel_id=1, source_target_pairs={{0,8},{2,10},{4,12},{6,14},{8,0},{10,2},{12,4},{14,6},{1,9},{3,11}... | collective-permute-start | bytes 44 | tf_op jit(solution)/shard_map/ppermute | solution.py:46
  101.6 2.3 %collective-permute-done.12 = f32[3]{0:T(128)S(1)} collective-permute-done((f32[3]{0:T(128)S(1)}, f32[3]{0:T(128)S(1)}, u32[]{:S(2)}, u32[]{:S(2)}) %collective-permute-start.12) | collective-permute-done | bytes 44 | tf_op jit(solution)/shard_map/ppermute | solution.py:46
  (66 shorter events, 12.8 us)
Async XLA Ops:
  0.6 78.4 %copy-start = (bf16[25,96,256]{2,1,0:T(8,128)(2,1)S(1)}, bf16[25,96,256]{2,1,0:T(8,128)(2,1)}, u32[]{:S(2)}) copy-start(bf16[25,96,256]{2,1,0:T(8,128)(2,1)} %param.18) | copy-start | bytes 3686404
  0.6 28.7 %copy-start.2 = (bf16[256,512]{1,0:T(8,128)(2,1)S(1)}, bf16[256,512]{1,0:T(8,128)(2,1)}, u32[]{:S(2)}) copy-start(bf16[256,512]{1,0:T(8,128)(2,1)} %param.16) | copy-start | bytes 786436
  0.7 31.0 %copy-start.1 = (bf16[1,256,32,48]{1,3,2,0:T(8,128)(2,1)S(1)}, bf16[1,256,32,48]{1,3,2,0:T(8,128)(2,1)}, u32[]{:S(2)}) copy-start(bf16[1,256,32,48]{1,3,2,0:T(8,128)(2,1)} %param.10) | copy-start | bytes 2359300
  0.7 23.2 %collective-permute-start.2 = (bf16[256,32,48]{0,2,1:T(8,128)(2,1)}, bf16[256,32,48]{0,2,1:T(8,128)(2,1)S(1)}, u32[]{:S(2)}, u32[]{:S(2)}) collective-permute-start(bf16[256,32,48]{0,2,1:T(8,128)(2,1)} %bitcast.105), channel_id=1, source_target_pairs={{0,14},{2,0},{4,2},{6,4},{8,6},{10,8},{12,10},{14,12},{1,15},{3,1}... | collective-permute-start | bytes 2359304 | tf_op jit(solution)/shard_map/ppermute | solution.py:34
  8.9 22.3 %collective-permute-start = (bf16[256,18,48]{0,2,1:T(8,128)(2,1)}, bf16[256,18,48]{0,2,1:T(8,128)(2,1)S(1)}, u32[]{:S(2)}, u32[]{:S(2)}) collective-permute-start(bf16[256,18,48]{0,2,1:T(8,128)(2,1)} %get-tuple-element.19), channel_id=1, source_target_pairs={{0,1},{2,3},{4,5},{6,7},{8,9},{10,11},{12,13},{14,15},{16,17},{18,... | collective-permute-start | bytes 1327112 | tf_op jit(solution)/shard_map/ppermute | solution.py:23
  10.4 20.8 %collective-permute-start.1 = (bf16[256,18,48]{0,2,1:T(8,128)(2,1)}, bf16[256,18,48]{0,2,1:T(8,128)(2,1)}, u32[]{:S(2)}, u32[]{:S(2)}) collective-permute-start(bf16[256,18,48]{0,2,1:T(8,128)(2,1)} %get-tuple-element.20), channel_id=1, source_target_pairs={{1,0},{3,2},{5,4},{7,6},{9,8},{11,10},{13,12},{15,14},{17,16},{19,... | collective-permute-start | bytes 1327112 | tf_op jit(solution)/shard_map/ppermute | solution.py:26
  13.8 3.8 %collective-permute-start.8 = (f32[3,64]{1,0:T(4,128)S(1)}, f32[3,64]{1,0:T(4,128)S(1)}, u32[]{:S(2)}, u32[]{:S(2)}) collective-permute-start(f32[3,64]{1,0:T(4,128)S(1)} %pad_maximum_fusion.1), channel_id=1, source_target_pairs={{0,1},{1,0},{2,3},{3,2},{4,5},{5,4},{6,7},{7,6},{8,9},{9,8},{10,11... | collective-permute-start | bytes 2312 | tf_op jit(solution)/shard_map/ppermute | solution.py:46
  25.4 3.9 %collective-permute-start.5 = (f32[512]{0:T(512)S(1)}, f32[512]{0:T(512)S(1)}, u32[]{:S(2)}, u32[]{:S(2)}) collective-permute-start(f32[512]{0:T(512)S(1)} %pad_maximum_fusion), channel_id=1, source_target_pairs={{0,1},{1,0},{2,3},{3,2},{4,5},{5,4},{6,7},{7,6},{8,9},{9,8},{10,11... | collective-permute-start | bytes 6152 | tf_op jit(solution)/shard_map/ppermute | solution.py:46
  25.6 5.6 %collective-permute-start.3 = (bf16[256,18,48]{0,2,1:T(8,128)(2,1)S(1)}, bf16[256,18,48]{0,2,1:T(8,128)(2,1)S(1)}, u32[]{:S(2)}, u32[]{:S(2)}) collective-permute-start(bf16[256,18,48]{0,2,1:T(8,128)(2,1)S(1)} %get-tuple-element.21), channel_id=1, source_target_pairs={{0,1},{2,3},{4,5},{6,7},{8,9},{10,11},{12,13},{14,15},{16,17},{18,... | collective-permute-start | bytes 1327112 | tf_op jit(solution)/shard_map/ppermute | solution.py:23
  28.0 3.7 %collective-permute-start.4 = (bf16[256,18,48]{0,2,1:T(8,128)(2,1)S(1)}, bf16[256,18,48]{0,2,1:T(8,128)(2,1)S(1)}, u32[]{:S(2)}, u32[]{:S(2)}) collective-permute-start(bf16[256,18,48]{0,2,1:T(8,128)(2,1)S(1)} %get-tuple-element.22), channel_id=1, source_target_pairs={{1,0},{3,2},{5,4},{7,6},{9,8},{11,10},{13,12},{15,14},{17,16},{19,... | collective-permute-start | bytes 1327112 | tf_op jit(solution)/shard_map/ppermute | solution.py:26
  71.5 5.1 %collective-permute-start.6 = (bf16[2,48,256]{2,1,0:T(8,128)(2,1)S(1)}, bf16[2,48,256]{2,1,0:T(8,128)(2,1)S(1)}, u32[]{:S(2)}, u32[]{:S(2)}) collective-permute-start(bf16[2,48,256]{2,1,0:T(8,128)(2,1)S(1)} %get-tuple-element.16), channel_id=1, source_target_pairs={{0,1},{2,3},{4,5},{6,7},{8,9},{10,11},{12,13},{14,15},{16,17},{18,... | collective-permute-start | bytes 147464 | tf_op jit(solution)/shard_map/ppermute | solution.py:23
  74.1 3.1 %collective-permute-start.7 = (bf16[2,48,256]{2,1,0:T(8,128)(2,1)S(1)}, bf16[2,48,256]{2,1,0:T(8,128)(2,1)S(1)}, u32[]{:S(2)}, u32[]{:S(2)}) collective-permute-start(bf16[2,48,256]{2,1,0:T(8,128)(2,1)S(1)} %get-tuple-element.17), channel_id=1, source_target_pairs={{1,0},{3,2},{5,4},{7,6},{9,8},{11,10},{13,12},{15,14},{17,16},{19,... | collective-permute-start | bytes 147464 | tf_op jit(solution)/shard_map/ppermute | solution.py:26
  77.4 1.7 %copy-start.5 = (pred[8,7]{0,1:T(8,128)(4,1)S(1)}, pred[8,7]{0,1:T(8,128)(4,1)}, u32[]{:S(2)}) copy-start(pred[8,7]{0,1:T(8,128)(4,1)} %constant.70) | copy-start | bytes 172
  85.2 0.7 copy-start.4
  85.2 2.2 %copy-start.3 = (s32[1,32,48]{2,1,0:T(8,128)S(1)}, s32[1,32,48]{2,1,0:T(8,128)}, u32[]{:S(2)}) copy-start(s32[1,32,48]{2,1,0:T(8,128)} %param.13) | copy-start | bytes 18436
  90.2 2.1 %collective-permute-start.9 = (f32[3]{0:T(128)S(1)}, f32[3]{0:T(128)S(1)}, u32[]{:S(2)}, u32[]{:S(2)}) collective-permute-start(f32[3]{0:T(128)S(1)} %pad_maximum_fusion.2), channel_id=1, source_target_pairs={{0,1},{1,0},{2,3},{3,2},{4,5},{5,4},{6,7},{7,6},{8,9},{9,8},{10,11... | collective-permute-start | bytes 44 | tf_op jit(solution)/shard_map/ppermute | solution.py:46
  92.3 3.6 %collective-permute-start.10 = (f32[3]{0:T(128)S(1)}, f32[3]{0:T(128)S(1)}, u32[]{:S(2)}, u32[]{:S(2)}) collective-permute-start(f32[3]{0:T(128)S(1)} %add.56), channel_id=1, source_target_pairs={{0,2},{2,0},{4,6},{6,4},{8,10},{10,8},{12,14},{14,12},{1,3},{3,1},... | collective-permute-start | bytes 44 | tf_op jit(solution)/shard_map/ppermute | solution.py:46
  95.9 3.6 %collective-permute-start.11 = (f32[3]{0:T(128)S(1)}, f32[3]{0:T(128)S(1)}, u32[]{:S(2)}, u32[]{:S(2)}) collective-permute-start(f32[3]{0:T(128)S(1)} %add.57), channel_id=1, source_target_pairs={{0,4},{2,6},{4,0},{6,2},{8,12},{10,14},{12,8},{14,10},{1,5},{3,7},... | collective-permute-start | bytes 44 | tf_op jit(solution)/shard_map/ppermute | solution.py:46
  99.4 4.5 %collective-permute-start.12 = (f32[3]{0:T(128)S(1)}, f32[3]{0:T(128)S(1)}, u32[]{:S(2)}, u32[]{:S(2)}) collective-permute-start(f32[3]{0:T(128)S(1)} %add.58), channel_id=1, source_target_pairs={{0,8},{2,10},{4,12},{6,14},{8,0},{10,2},{12,4},{14,6},{1,9},{3,11}... | collective-permute-start | bytes 44 | tf_op jit(solution)/shard_map/ppermute | solution.py:46

commit v2 on v1

--- a/solution.py
+++ b/solution.py
@@ -26,6 +26,23 @@
         high = lax.ppermute(lax.slice_in_dim(block, 0, width, axis=dim), axis, backward)
         block = jnp.concatenate([low, block, high], axis=dim)
     return block
+
+
+def with_rims(block, axis, dim, width):
+    if lax.axis_size(axis) != 2:
+        return padded_2(block, ((axis, dim),), width)
+    first = lax.axis_index(axis) == 0
+    size = block.shape[dim]
+    sent = jnp.where(
+        first,
+        lax.slice_in_dim(block, size - width, None, axis=dim),
+        lax.slice_in_dim(block, 0, width, axis=dim),
+    )
+    got = lax.ppermute(sent, axis, [(0, 1), (1, 0)])
+    empty = jnp.zeros_like(got)
+    low = jnp.where(first, empty, got)
+    high = jnp.where(first, got, empty)
+    return jnp.concatenate([low, block, high], axis=dim)
 
 
 def shifted(value, axis, steps):
@@ -49,12 +66,12 @@
     return value
 
 
-def aspp_projected(x, aspp_point, aspp_dilated, proj_weight, pool_term, geometry):
+def aspp_projected(x, aspp_point, aspp_dilated, proj_weight, pool_term, keep, geometry):
     front, pitch, margin, block, blocks = geometry
     width = aspp_point.shape[0]
     contract = (((1,), (1,)), ((), ()))
 
-    def body(x_ref, point_ref, dilated_ref, proj_ref, pool_ref, out_ref):
+    def body(x_ref, point_ref, dilated_ref, proj_ref, pool_ref, keep_ref, out_ref):
         for index in range(blocks):
             base = front + margin * pitch + index * block
 
@@ -89,20 +106,55 @@
                 )
                 mixed = term if mixed is None else mixed + term
             mixed = mixed + pool_ref[...]
-            out_ref[pl.ds(index * block, block), :] = relu_bf16(mixed)
+            rounded = relu_bf16(mixed).astype(jnp.float32)
+            out_ref[pl.ds(index * block, block), :] = jnp.where(keep_ref[...] > 0.5, rounded, 0.0)
 
     taps = 1 + 9 * len(DILATIONS)
     flops = 2 * blocks * block * x.shape[1] * width * taps + 2 * blocks * block * 4 * width * width
     return pl.pallas_call(
         body,
-        out_shape=jax.ShapeDtypeStruct((blocks * block, width), jnp.bfloat16),
+        out_shape=jax.ShapeDtypeStruct((blocks * block, width), jnp.float32),
         compiler_params=pltpu.CompilerParams(vmem_limit_bytes=56 * 1024 * 1024),
         cost_estimate=pl.CostEstimate(
             flops=flops,
             transcendentals=0,
             bytes_accessed=x.size * 4 + aspp_dilated.size * 2 + blocks * block * width * 2,
         ),
-    )(x, aspp_point, aspp_dilated, proj_weight, pool_term)
+    )(x, aspp_point, aspp_dilated, proj_weight, pool_term, keep)
+
+
+def head_kernel_call(x, head_weight, geometry):
+    front, pitch, reach, block, blocks = geometry
+    outputs = head_weight.shape[1]
+    side = 2 * reach + 1
+    contract = (((1,), (1,)), ((), ()))
+
+    def body(x_ref, weight_ref, out_ref):
+        for index in range(blocks):
+            base = front + reach * pitch + index * block
+            total = None
+            for vertical in range(side):
+                for lateral in range(side):
+                    shift = (vertical - reach) * pitch + (lateral - reach)
+                    term = lax.dot_general(
+                        x_ref[pl.ds(base + shift, block), :].astype(jnp.bfloat16),
+                        weight_ref[side * vertical + lateral],
+                        contract,
+                        preferred_element_type=jnp.float32,
+                    )
+                    total = term if total is None else total + term
+            out_ref[pl.ds(index * block, block), :] = relu_bf16(total)
+
+    return pl.pallas_call(
+        body,
+        out_shape=jax.ShapeDtypeStruct((blocks * block, outputs), jnp.bfloat16),
+        compiler_params=pltpu.CompilerParams(vmem_limit_bytes=32 * 1024 * 1024),
+        cost_estimate=pl.CostEstimate(
+            flops=2 * blocks * block * x.shape[1] * outputs * side * side,
+            transcendentals=0,
+            bytes_accessed=x.size * 4 + head_weight.size * 2 + blocks * block * outputs * 2,
+        ),
+    )(x, head_weight)
 
 
 def relu_bf16(values):
@@ -147,11 +199,10 @@
     rim_rows = min(aspp_reach, band_rows)
     extra_rows = aspp_reach - rim_rows
 
-    def widen(band):
-        wide = padded_2(band, (("row", 1),), rim_rows)
-        return jnp.pad(wide, ((0, 0), (extra_rows, extra_rows), (0, 0)))
-
-    joined_wide = jnp.concatenate([widen(own_band), widen(later_band)], 0)
+    joined_wide = jnp.pad(
+        with_rims(jnp.concatenate([own_band, later_band], 0), "row", 1, rim_rows),
+        ((0, 0), (extra_rows, extra_rows), (0, 0)),
+    )
     wide_rows = joined_wide.shape[1]
     pitch = -(-(columns + aspp_reach) // 8) * 8
     front = pitch
@@ -190,26 +241,25 @@
     pool_term = jnp.dot(
         proj_weight[:, 4 * aspp_width :], pool_feature, preferred_element_type=jnp.float32
     )[None]
+    pad_columns = pitch - columns
+    keep = (jnp.arange(block) % pitch >= pad_columns).astype(jnp.float32)[:, None]
     projected_flat = aspp_projected(
         flat,
         aspp_point,
         aspp_dilated,
         proj_weight,
         pool_term,
+        keep,
         (front, pitch, aspp_reach, block, blocks),
     )
-    projected = projected_flat.reshape(band_rows, pitch, aspp_width)[:, pitch - columns :]
-    rimmed = padded_2(projected, (("row", 0),), 2)
-    head_kernel = head_weight.reshape(5, 5, *head_weight.shape[1:])
-    head_sum = lax.conv_general_dilated(
-        rimmed[None],
-        head_kernel,
-        window_strides=(1, 1),
-        padding=((0, 0), (2, 2)),
-        dimension_numbers=("NHWC", "HWOI", "NCHW"),
-        preferred_element_type=jnp.float32,
-    )[0]
-    head_out = relu_bf16(head_sum)
+    head_reach = 2
+    head_in = jnp.pad(
+        with_rims(projected_flat, "row", 0, head_reach * pitch), ((pitch, pitch), (0, 0))
+    )
+    head_flat = head_kernel_call(head_in, head_weight, (pitch, pitch, head_reach, block, blocks))
+    head_out = jnp.transpose(
+        head_flat.reshape(band_rows, pitch, head_weight.shape[1])[:, pad_columns:], (2, 0, 1)
+    )
     predictions = emit_heads(head_out, out_weight)
     pixel = jnp.einsum("sk,khw->shw", inst_stats, onehot, precision=lax.Precision.HIGHEST)
     counts = jnp.where(counted, pixel[0], 1.0)

time: 108 us -> 99.7 us (0.923)
  starting transfers between devices: 21.4 us -> 9.6 us
  Pallas kernels: 31.3 us -> 39.8 us
  matrix products: 11.5 us -> 4.49 us
  local copies, waits for them, and re-layouts: 10.4 us -> 3.44 us
  waiting for transfers between devices: 14.3 us -> 20.9 us
  other arithmetic: 14.6 us -> 17.6 us
    ppermute x6 -> x2, starting transfers between devices: 10.4 us -> 0.81 us  [with_rims(): got = lax.ppermute(sent, axis, [(0, 1), (1, 0)])]
    pallas_call x0 -> x1, Pallas kernels: none -> 8.04 us  [head_kernel_call(): pl.pallas_call(body, out_shape=jax.ShapeDtypeStruct((blocks * block, outp...]
    conv_general_dilated x1 -> x0, matrix products: 6.1 us -> none  [shards(): lax.conv_general_dilated(rimmed[None], head_kernel, window_strides=(1, 1)...]
    ppermute x1, waiting for transfers between devices: 4.03 us -> 9.94 us  [shifted(): return lax.ppermute(value, axis, pairs)]
    slice x4 -> x1, local copies, waits for them, and re-layouts: 4.2 us -> 0.03 us  [shards(): head_flat.reshape(band_rows, pitch, head_weight.shape[1])[:, pad_columns:]]
    ppermute x6, starting transfers between devices: 4.97 us -> 2.71 us  [all_sum(): other = lax.ppermute(value, axis, pairs)]
    concatenate x0 -> x1, other arithmetic: none -> 1.95 us  [with_rims(): return jnp.concatenate([low, block, high], axis=dim)]
    select_n x0 -> x4, other arithmetic: none -> 1.37 us  [the longest x2 1.23 us: with_rims(): jnp.where(first, lax.slice_in_dim(block, size - width, None, axis=dim), l...]
  transfers between devices with their start and end apart: 13 -> 9, of which waited for: 6 -> 7; matrix products, arithmetic and copies ran while one was open for 13% -> 9% of each run, Pallas kernels for 0% -> 0%
where the time goes in v2:
time: 99.7 us; the launch traced here: 99.3 us
  Pallas kernels  39.8 us (40%)
  waiting for transfers between devices  20.9 us (21%)
  other arithmetic  17.6 us (18%)
  starting transfers between devices  9.6 us (10%)
  matrix products  4.49 us (5%)
  local copies, waits for them, and re-layouts  3.44 us (3%)
  between operations  3.43 us (3%)
    pallas_call x1, Pallas kernels, aspp_projected(): pl.pallas_call(body, out_shape=jax.ShapeDtypeStruct((blocks * block, widt...  31.7 us
    ppermute x1, waiting for transfers between devices, shifted(): return lax.ppermute(value, axis, pairs)  9.94 us
    ppermute x6, waiting for transfers between devices, all_sum(): other = lax.ppermute(value, axis, pairs)  9.85 us
    pallas_call x1, Pallas kernels, head_kernel_call(): pl.pallas_call(body, out_shape=jax.ShapeDtypeStruct((blocks * block, outp...  8.04 us
    ppermute x1, starting transfers between devices, shifted(): return lax.ppermute(value, axis, pairs)  6.09 us
    reshape x1, other arithmetic, shards(): flat = jnp.pad(jnp.transpose(joined_wide, (1, 2, 0)).astype(jnp.float32),...  5.91 us
    ppermute x6, starting transfers between devices, all_sum(): other = lax.ppermute(value, axis, pairs)  2.71 us
    dot_general x1, matrix products, shards(): jnp.einsum('sk,khw->shw', inst_stats, onehot, precision=lax.Precision.HIG...  2.23 us
  transfers between devices with their start and end apart: 9, of which 7 were waited for; matrix products, arithmetic and copies ran while one was open for 9% of the time, Pallas kernels for 0%

profile of v2, /device:TPU:0, one launch (start us, length us, event | category | flops | bytes accessed | tf_op | source)
XLA Modules:
  0.0 99.3 jit_solution(4320507379668612348)
XLA Ops:
  0.7 6.1 %collective-permute-start = (bf16[256,32,48]{0,2,1:T(8,128)(2,1)}, bf16[256,32,48]{0,2,1:T(8,128)(2,1)S(1)}, u32[]{:S(2)}, u32[]{:S(2)}) collective-permute-start(bf16[256,32,48]{0,2,1:T(8,128)(2,1)} %bitcast.70), channel_id=1, source_target_pairs={{0,14},{2,0},{4,2},{6,4},{8,6},{10,8},{12,10},{14,12},{1,15},{3,1}... | collective-permute-start | bytes 2359304 | tf_op jit(solution)/shard_map/ppermute | solution.py:51
  6.7 0.7 and_bitcast_fusion
  7.5 1.3 %convert_reduce_fusion.2 = (f32[64]{0:T(128)S(1)}, f32[64]{0:T(128)S(1)}, f32[64]{0:T(128)S(1)}) fusion(s32[32,48]{1,0:T(8,128)} %bitcast.76, pred[32,48]{1,0:T(8,128)(4,1)S(1)} %get-tuple-element.10, f32[32]{0:T(128)S(1)} %add_convert_fusion), kind=kLoop, calls=%fused_computation.19 | loop fusion | flops 786240 | bytes 8576 | tf_op jit(solution)/shard_map/reduce_sum | solution.py:228
  8.9 0.9 fusion.12.keep_ref
  9.8 1.2 %dynamic_slice.4 = s32[1]{0:T(128)} dynamic-slice(s32[8]{0:T(128)} %param.11, s32[]{:T(128)S(6)} %select_n.77), dynamic_slice_sizes={1} | dynamic-slice | bytes 12 | tf_op jit(solution)/shard_map/jit(dynamic_index_in_dim)/dynamic_slice | solution.py:197
  11.7 2.2 %fusion.4 = f32[3,32,48]{2,0,1:T(4,128)S(1)} fusion(s32[32,48]{1,0:T(8,128)} %bitcast.77, pred[32,48]{1,0:T(8,128)(4,1)S(1)} %get-tuple-element.10, f32[3,64]{1,0:T(4,128)S(1)} %collective-permute-done.4, f32[1,64]{1,0:T(1,128)S(1)} %bitcast.87, f32[1,64]{1,0:T(1,128)S(1)} %bitcast.89, f32[1,64]{1,0:T(1,128)S(1)} %bitcast.85), kind=kOutput, calls=%fused_computation.22 | convolution fusion | flops 3736128 | bytes 27648 | tf_op jit(solution)/shard_map/sk,khw->shw/dot_general | solution.py:264
  13.9 9.9 %collective-permute-done = bf16[256,32,48]{0,2,1:T(8,128)(2,1)S(1)} collective-permute-done((bf16[256,32,48]{0,2,1:T(8,128)(2,1)}, bf16[256,32,48]{0,2,1:T(8,128)(2,1)S(1)}, u32[]{:S(2)}, u32[]{:S(2)}) %collective-permute-start) | collective-permute-done | bytes 786464 | tf_op jit(solution)/shard_map/ppermute | solution.py:51
  23.9 1.5 %convert_reduce_fusion = (f32[256]{0:T(256)S(1)}, bf16[256,32,48]{0,2,1:T(8,128)(2,1)S(1)}, f32[256]{0:T(256)S(1)}) fusion(bf16[256,32,48]{0,2,1:T(8,128)(2,1)S(1)} %collective-permute-done, bf16[1,256,32,48]{1,3,2,0:T(8,128)(2,1)} %param.10, pred[]{:T(512)} %bitcast.1), kind=kLoop, calls=%fused_computation.9 | loop fusion | flops 1965568 | bytes 2361345 | tf_op jit(solution)/shard_map/reduce_sum | solution.py:235
  26.9 1.7 %fusion.18.pool_ref = f32[1,256]{1,0:T(1,128)} fusion(bf16[256,1]{0,1:T(2,128)(2,1)S(1)} %reshape.72, bf16[256,1280]{1,0:T(8,128)(2,1)} %proj_ref.1), kind=kOutput, calls=%fused_computation.39 | convolution fusion | flops 131072 | bytes 132608 | tf_op jit(solution)/shard_map/dot_general | solution.py:241
  29.4 5.9 %bitcast_convert_fusion.x_ref = f32[5040,512]{1,0:T(8,128)} fusion(bf16[70,72,512]{2,1,0:T(8,128)(2,1)S(1)} %pad.9), kind=kLoop, calls=%fused_computation | loop fusion | flops 2580480 | bytes 15482880 | tf_op jit(solution)/shard_map/reshape | solution.py:215
  35.3 31.7 %shard_map.113 = f32[2304,256]{1,0:T(8,128)} custom-call(f32[5040,512]{1,0:T(8,128)} %bitcast_convert_fusion.x_ref, bf16[256,512]{1,0:T(8,128)(2,1)} %point_ref.1, bf16[3,9,256,512]{3,2,1,0:T(8,128)(2,1)} %dilated_ref.1, bf16[256,1280]{1,0:T(8,128)(2,1)} %proj_ref.1, f32[1,256]{1,0:T(1,128)} %fusion.18.pool_ref, f32[576,1]{1,0:T(8,128)} %fusion.12.keep_ref), custom_call_target="tpu_custom_call" | custom-call | flops 18119393280 | bytes 18579456 | tf_op jit(solution)/shard_map/pallas_call | solution.py:114
  67.0 1.0 %slice_select_fusion = f32[144,256]{1,0:T(8,128)S(1)} fusion(f32[2304,256]{1,0:T(8,128)} %shard_map.113, pred[]{:T(512)S(6)} %eq.27), kind=kLoop, calls=%fused_computation.38 | loop fusion | flops 36864 | bytes 442369 | tf_op jit(solution)/shard_map/jit(_where)/select_n | solution.py:36
  68.3 1.1 %collective-permute-done.3 = f32[144,256]{1,0:T(8,128)S(1)} collective-permute-done((f32[144,256]{1,0:T(8,128)S(1)}, f32[144,256]{1,0:T(8,128)S(1)}, u32[]{:S(2)}, u32[]{:S(2)}) %collective-permute-start.3) | collective-permute-done | bytes 147488 | tf_op jit(solution)/shard_map/ppermute | solution.py:41
  69.5 1.9 %select_maximum_fusion.x_ref = f32[2736,256]{1,0:T(8,128)S(1)} fusion(f32[144,256]{1,0:T(8,128)S(1)} %get-tuple-element.18, f32[2304,256]{1,0:T(8,128)} %shard_map.113, f32[144,256]{1,0:T(8,128)S(1)} %get-tuple-element.17), kind=kLoop, calls=%fused_computation.4 | loop fusion | flops 5603328 | bytes 5455872 | tf_op jit(solution)/shard_map/concatenate | solution.py:45
  71.5 8.0 %shard_map.114 = bf16[2304,96]{1,0:T(8,128)(2,1)S(1)} custom-call(f32[2736,256]{1,0:T(8,128)S(1)} %select_maximum_fusion.x_ref, bf16[25,96,256]{2,1,0:T(8,128)(2,1)S(1)} %copy-done.1), custom_call_target="tpu_custom_call" | custom-call | flops 2831155200 | bytes 4472832 | tf_op jit(solution)/shard_map/pallas_call | solution.py:148
  80.5 0.8 multiply_reduce_fusion
  81.2 2.1 %pad_maximum_fusion.3 = f32[3]{0:T(128)S(1)} fusion(f32[1]{0:T(128)} %bitcast.35, f32[1]{0:T(128)} %bitcast.34, f32[1]{0:T(128)} %bitcast.31), kind=kLoop, calls=%fused_computation.58 | loop fusion | flops 6 | bytes 24 | tf_op jit(solution)/shard_map/stack | solution.py:282
  83.5 0.6 copy.18
  84.7 3.4 %collective-permute-done.6 = f32[3]{0:T(128)S(1)} collective-permute-done((f32[3]{0:T(128)S(1)}, f32[3]{0:T(128)S(1)}, u32[]{:S(2)}, u32[]{:S(2)}) %collective-permute-start.6) | collective-permute-done | bytes 44 | tf_op jit(solution)/shard_map/ppermute | solution.py:63
  88.0 3.6 %collective-permute-done.7 = f32[3]{0:T(128)S(1)} collective-permute-done((f32[3]{0:T(128)S(1)}, f32[3]{0:T(128)S(1)}, u32[]{:S(2)}, u32[]{:S(2)}) %collective-permute-start.7) | collective-permute-done | bytes 44 | tf_op jit(solution)/shard_map/ppermute | solution.py:63
  91.6 2.2 %collective-permute-start.8 = (f32[3]{0:T(128)S(1)}, f32[3]{0:T(128)S(1)}, u32[]{:S(2)}, u32[]{:S(2)}) collective-permute-start(f32[3]{0:T(128)S(1)} %add.74), channel_id=1, source_target_pairs={{0,8},{2,10},{4,12},{6,14},{8,0},{10,2},{12,4},{14,6},{1,9},{3,11}... | collective-permute-start | bytes 44 | tf_op jit(solution)/shard_map/ppermute | solution.py:63
  93.8 2.3 %collective-permute-done.8 = f32[3]{0:T(128)S(1)} collective-permute-done((f32[3]{0:T(128)S(1)}, f32[3]{0:T(128)S(1)}, u32[]{:S(2)}, u32[]{:S(2)}) %collective-permute-start.8) | collective-permute-done | bytes 44 | tf_op jit(solution)/shard_map/ppermute | solution.py:63
  96.1 0.7 fusion.30
  98.7 0.6 pad_maximum_fusion.4
  (46 shorter events, 4.4 us)
Async XLA Ops:
  0.6 26.0 %copy-start = (bf16[256,512]{1,0:T(8,128)(2,1)S(1)}, bf16[256,512]{1,0:T(8,128)(2,1)}, u32[]{:S(2)}) copy-start(bf16[256,512]{1,0:T(8,128)(2,1)} %param.16) | copy-start | bytes 786436
  0.6 24.8 %copy-start.2 = (bf16[1,256,32,48]{1,3,2,0:T(8,128)(2,1)S(1)}, bf16[1,256,32,48]{1,3,2,0:T(8,128)(2,1)}, u32[]{:S(2)}) copy-start(bf16[1,256,32,48]{1,3,2,0:T(8,128)(2,1)} %param.10) | copy-start | bytes 2359300
  0.7 23.2 %collective-permute-start = (bf16[256,32,48]{0,2,1:T(8,128)(2,1)}, bf16[256,32,48]{0,2,1:T(8,128)(2,1)S(1)}, u32[]{:S(2)}, u32[]{:S(2)}) collective-permute-start(bf16[256,32,48]{0,2,1:T(8,128)(2,1)} %bitcast.70), channel_id=1, source_target_pairs={{0,14},{2,0},{4,2},{6,4},{8,6},{10,8},{12,10},{14,12},{1,15},{3,1}... | collective-permute-start | bytes 2359304 | tf_op jit(solution)/shard_map/ppermute | solution.py:51
  8.8 2.8 %collective-permute-start.4 = (f32[3,64]{1,0:T(4,128)S(1)}, f32[3,64]{1,0:T(4,128)S(1)}, u32[]{:S(2)}, u32[]{:S(2)}) collective-permute-start(f32[3,64]{1,0:T(4,128)S(1)} %pad_maximum_fusion.2), channel_id=1, source_target_pairs={{0,1},{1,0},{2,3},{3,2},{4,5},{5,4},{6,7},{7,6},{8,9},{9,8},{10,11... | collective-permute-start | bytes 2312 | tf_op jit(solution)/shard_map/ppermute | solution.py:63
  25.4 1.2 %collective-permute-start.2 = (f32[512]{0:T(512)S(1)}, f32[512]{0:T(512)S(1)}, u32[]{:S(2)}, u32[]{:S(2)}) collective-permute-start(f32[512]{0:T(512)S(1)} %pad_maximum_fusion.1), channel_id=1, source_target_pairs={{0,1},{1,0},{2,3},{3,2},{4,5},{5,4},{6,7},{7,6},{8,9},{9,8},{10,11... | collective-permute-start | bytes 6152 | tf_op jit(solution)/shard_map/ppermute | solution.py:63
  25.7 2.8 %collective-permute-start.1 = (bf16[512,18,48]{0,2,1:T(8,128)(2,1)S(1)}, bf16[512,18,48]{0,2,1:T(8,128)(2,1)S(1)}, u32[]{:S(2)}, u32[]{:S(2)}) collective-permute-start(bf16[512,18,48]{0,2,1:T(8,128)(2,1)S(1)} %fusion.2), channel_id=1, source_target_pairs={{0,1},{1,0},{2,3},{3,2},{4,5},{5,4},{6,7},{7,6},{8,9},{9,8},{10,11... | collective-permute-start | bytes 2654216 | tf_op jit(solution)/shard_map/ppermute | solution.py:41
  68.0 1.4 %collective-permute-start.3 = (f32[144,256]{1,0:T(8,128)S(1)}, f32[144,256]{1,0:T(8,128)S(1)}, u32[]{:S(2)}, u32[]{:S(2)}) collective-permute-start(f32[144,256]{1,0:T(8,128)S(1)} %slice_select_fusion), channel_id=1, source_target_pairs={{0,1},{1,0},{2,3},{3,2},{4,5},{5,4},{6,7},{7,6},{8,9},{9,8},{10,11... | collective-permute-start | bytes 442376 | tf_op jit(solution)/shard_map/ppermute | solution.py:41
  69.5 2.0 %copy-start.1 = (bf16[25,96,256]{2,1,0:T(8,128)(2,1)S(1)}, bf16[25,96,256]{2,1,0:T(8,128)(2,1)}, u32[]{:S(2)}) copy-start(bf16[25,96,256]{2,1,0:T(8,128)(2,1)} %weight_ref.1) | copy-start | bytes 3686404
  71.5 8.5 %copy-start.4 = (bf16[4,32]{1,0:T(4,128)(2,1)S(1)}, bf16[4,32]{1,0:T(4,128)(2,1)}, u32[]{:S(2)}) copy-start(bf16[4,32]{1,0:T(4,128)(2,1)} %param.19) | copy-start | bytes 772
  79.5 0.9 copy-start.3
  83.3 1.2 %collective-permute-start.5 = (f32[3]{0:T(128)S(1)}, f32[3]{0:T(128)S(1)}, u32[]{:S(2)}, u32[]{:S(2)}) collective-permute-start(f32[3]{0:T(128)S(1)} %pad_maximum_fusion.3), channel_id=1, source_target_pairs={{0,1},{1,0},{2,3},{3,2},{4,5},{5,4},{6,7},{7,6},{8,9},{9,8},{10,11... | collective-permute-start | bytes 44 | tf_op jit(solution)/shard_map/ppermute | solution.py:63
  84.5 3.6 %collective-permute-start.6 = (f32[3]{0:T(128)S(1)}, f32[3]{0:T(128)S(1)}, u32[]{:S(2)}, u32[]{:S(2)}) collective-permute-start(f32[3]{0:T(128)S(1)} %add.72), channel_id=1, source_target_pairs={{0,2},{2,0},{4,6},{6,4},{8,10},{10,8},{12,14},{14,12},{1,3},{3,1},... | collective-permute-start | bytes 44 | tf_op jit(solution)/shard_map/ppermute | solution.py:63
  88.0 3.6 %collective-permute-start.7 = (f32[3]{0:T(128)S(1)}, f32[3]{0:T(128)S(1)}, u32[]{:S(2)}, u32[]{:S(2)}) collective-permute-start(f32[3]{0:T(128)S(1)} %add.73), channel_id=1, source_target_pairs={{0,4},{2,6},{4,0},{6,2},{8,12},{10,14},{12,8},{14,10},{1,5},{3,7},... | collective-permute-start | bytes 44 | tf_op jit(solution)/shard_map/ppermute | solution.py:63
  91.6 4.5 %collective-permute-start.8 = (f32[3]{0:T(128)S(1)}, f32[3]{0:T(128)S(1)}, u32[]{:S(2)}, u32[]{:S(2)}) collective-permute-start(f32[3]{0:T(128)S(1)} %add.74), channel_id=1, source_target_pairs={{0,8},{2,10},{4,12},{6,14},{8,0},{10,2},{12,4},{14,6},{1,9},{3,11}... | collective-permute-start | bytes 44 | tf_op jit(solution)/shard_map/ppermute | solution.py:63

commit v3 on v2

--- a/solution.py
+++ b/solution.py
@@ -66,21 +66,29 @@
     return value
 
 
-def aspp_projected(x, aspp_point, aspp_dilated, proj_weight, pool_term, keep, geometry):
+def aspp_pass(x, aspp_point, aspp_dilated, extra, geometry, part, finish):
     front, pitch, margin, block, blocks = geometry
     width = aspp_point.shape[0]
+    channels = x.shape[1]
+    lanes = pl.ds(part * channels, channels)
     contract = (((1,), (1,)), ((), ()))
-
-    def body(x_ref, point_ref, dilated_ref, proj_ref, pool_ref, keep_ref, out_ref):
+    branches = 1 + len(DILATIONS)
+
+    def body(x_ref, point_ref, dilated_ref, *rest):
+        if finish:
+            earlier_ref, proj_ref, pool_ref, keep_ref, out_ref = rest
+        else:
+            (out_ref,) = rest
         for index in range(blocks):
             base = front + margin * pitch + index * block
+            rows = pl.ds(index * block, block)
 
             def window(shift):
                 return x_ref[pl.ds(base + shift, block), :].astype(jnp.bfloat16)
 
             sums = [
                 lax.dot_general(
-                    window(0), point_ref[...], contract, preferred_element_type=jnp.float32
+                    window(0), point_ref[:, lanes], contract, preferred_element_type=jnp.float32
                 )
             ]
             for branch, spread in enumerate(DILATIONS):
@@ -90,16 +98,20 @@
                         shift = (vertical - 1) * spread * pitch + (lateral - 1) * spread
                         term = lax.dot_general(
                             window(shift),
-                            dilated_ref[branch, 3 * vertical + lateral],
+                            dilated_ref[branch, 3 * vertical + lateral, :, lanes],
                             contract,
                             preferred_element_type=jnp.float32,
                         )
                         total = term if total is None else total + term
                 sums.append(total)
+            if not finish:
+                for branch, total in enumerate(sums):
+                    out_ref[branch, rows, :] = total
+                continue
             mixed = None
             for branch, total in enumerate(sums):
                 term = lax.dot_general(
-                    relu_bf16(total),
+                    relu_bf16(earlier_ref[branch, rows, :] + total),
                     proj_ref[:, branch * width : (branch + 1) * width],
                     contract,
                     preferred_element_type=jnp.float32,
@@ -107,20 +119,27 @@
                 mixed = term if mixed is None else mixed + term
             mixed = mixed + pool_ref[...]
             rounded = relu_bf16(mixed).astype(jnp.float32)
-            out_ref[pl.ds(index * block, block), :] = jnp.where(keep_ref[...] > 0.5, rounded, 0.0)
+            out_ref[rows, :] = jnp.where(keep_ref[...] > 0.5, rounded, 0.0)
 
     taps = 1 + 9 * len(DILATIONS)
-    flops = 2 * blocks * block * x.shape[1] * width * taps + 2 * blocks * block * 4 * width * width
+    flops = 2 * blocks * block * channels * width * taps
+    if finish:
+        flops += 2 * blocks * block * branches * width * width
+        out_shape = jax.ShapeDtypeStruct((blocks * block, width), jnp.float32)
+    else:
+        out_shape = jax.ShapeDtypeStruct((branches, blocks * block, width), jnp.float32)
     return pl.pallas_call(
         body,
-        out_shape=jax.ShapeDtypeStruct((blocks * block, width), jnp.float32),
+        out_shape=out_shape,
         compiler_params=pltpu.CompilerParams(vmem_limit_bytes=56 * 1024 * 1024),
         cost_estimate=pl.CostEstimate(
             flops=flops,
             transcendentals=0,
-            bytes_accessed=x.size * 4 + aspp_dilated.size * 2 + blocks * block * width * 2,
+            bytes_accessed=x.size * 4
+            + aspp_dilated.size
+            + branches * blocks * block * width * 4,
         ),
-    )(x, aspp_point, aspp_dilated, proj_weight, pool_term, keep)
+    )(x, aspp_point, aspp_dilated, *extra)
 
 
 def head_kernel_call(x, head_weight, geometry):
@@ -199,20 +218,26 @@
     rim_rows = min(aspp_reach, band_rows)
     extra_rows = aspp_reach - rim_rows
 
-    joined_wide = jnp.pad(
-        with_rims(jnp.concatenate([own_band, later_band], 0), "row", 1, rim_rows),
-        ((0, 0), (extra_rows, extra_rows), (0, 0)),
-    )
-    wide_rows = joined_wide.shape[1]
+    wide_rows = band_rows + 2 * aspp_reach
     pitch = -(-(columns + aspp_reach) // 8) * 8
     front = pitch
     block_rows = 8 if band_rows % 8 == 0 else band_rows
     block = block_rows * pitch
     blocks = band_rows // block_rows
-    flat = jnp.pad(
-        jnp.transpose(joined_wide, (1, 2, 0)).astype(jnp.float32),
-        ((1, 1), (pitch - columns, 0), (0, 0)),
-    ).reshape((wide_rows + 2) * pitch, 2 * channel_count)
+
+    def flat_of(band):
+        wide = jnp.pad(
+            with_rims(band, "row", 1, rim_rows), ((0, 0), (extra_rows, extra_rows), (0, 0))
+        )
+        return jnp.pad(
+            jnp.transpose(wide, (1, 2, 0)).astype(jnp.float32),
+            ((1, 1), (pitch - columns, 0), (0, 0)),
+        ).reshape((wide_rows + 2) * pitch, channel_count)
+
+    geometry = (front, pitch, aspp_reach, block, blocks)
+    own_sums = aspp_pass(
+        flat_of(own_band), aspp_point, aspp_dilated, (), geometry, 0, False
+    )
 
     counted = (semantic[0] >= THING_FIRST) & (instance[0] > 0)
     labels = jnp.arange(INSTANCES, dtype=jnp.int32)
@@ -243,14 +268,14 @@
     )[None]
     pad_columns = pitch - columns
     keep = (jnp.arange(block) % pitch >= pad_columns).astype(jnp.float32)[:, None]
-    projected_flat = aspp_projected(
-        flat,
+    projected_flat = aspp_pass(
+        flat_of(later_band),
         aspp_point,
         aspp_dilated,
-        proj_weight,
-        pool_term,
-        keep,
-        (front, pitch, aspp_reach, block, blocks),
+        (own_sums, proj_weight, pool_term, keep),
+        geometry,
+        1,
+        True,
     )
     head_reach = 2
     head_in = jnp.pad(

time: 99.7 us -> 96.8 us (0.971)
  waiting for transfers between devices: 20.9 us -> 13.6 us
  Pallas kernels: 39.8 us -> 46.2 us
  starting transfers between devices: 9.6 us -> 7.75 us
    ppermute x1, waiting for transfers between devices: 9.94 us -> 0.01 us  [shifted(): return lax.ppermute(value, axis, pairs)]
    pallas_call x1 -> x2, Pallas kernels: 31.7 us -> 38.2 us  [aspp_pass(): pl.pallas_call(body, out_shape=out_shape, compiler_params=pltpu.CompilerP...]
    ppermute x6, waiting for transfers between devices: 9.85 us -> 12.4 us  [all_sum(): other = lax.ppermute(value, axis, pairs)]
    ppermute x6, starting transfers between devices: 2.71 us -> 0.82 us  [all_sum(): other = lax.ppermute(value, axis, pairs)]
    reduce_sum x1, other arithmetic: 1.54 us -> 0.43 us  [shards(): jnp.sum(band, axis=(1, 2), dtype=jnp.float32)]
    select_n x2 -> x3, other arithmetic: 1.23 us -> 2.24 us  [with_rims(): jnp.where(first, lax.slice_in_dim(block, size - width, None, axis=dim), l...]
    reshape x1 -> x2, other arithmetic: 5.91 us -> 5.85 us  [flat_of(): return jnp.pad(jnp.transpose(wide, (1, 2, 0)).astype(jnp.float32), ((1, 1...]
  transfers between devices with their start and end apart: 9 -> 10, of which waited for: 7 -> 6; matrix products, arithmetic and copies ran while one was open for 9% -> 14% of each run, Pallas kernels for 0% -> 18%
where the time goes in v3:
time: 96.8 us; the launch traced here: 96.3 us
  Pallas kernels  46.2 us (48%)
  other arithmetic  17.4 us (18%)
  waiting for transfers between devices  13.6 us (14%)
  starting transfers between devices  7.75 us (8%)
  matrix products  4.48 us (5%)
  between operations  3.47 us (4%)
  local copies, waits for them, and re-layouts  3.42 us (4%)
    pallas_call x2, Pallas kernels, aspp_pass(): pl.pallas_call(body, out_shape=out_shape, compiler_params=pltpu.CompilerP...  38.2 us
    ppermute x6, waiting for transfers between devices, all_sum(): other = lax.ppermute(value, axis, pairs)  12.4 us
    pallas_call x1, Pallas kernels, head_kernel_call(): pl.pallas_call(body, out_shape=jax.ShapeDtypeStruct((blocks * block, outp...  8 us
    ppermute x1, starting transfers between devices, shifted(): return lax.ppermute(value, axis, pairs)  6.09 us
    reshape x2, other arithmetic, flat_of(): return jnp.pad(jnp.transpose(wide, (1, 2, 0)).astype(jnp.float32), ((1, 1...  5.85 us
    select_n x3, other arithmetic, with_rims(): jnp.where(first, lax.slice_in_dim(block, size - width, None, axis=dim), l...  2.24 us
    dot_general x1, matrix products, shards(): jnp.einsum('sk,khw->shw', inst_stats, onehot, precision=lax.Precision.HIG...  2.23 us
    another operation x1, other arithmetic, shards(): jnp.stack([center_err, offset_err, counted_local])  2 us
  transfers between devices with their start and end apart: 10, of which 6 were waited for; matrix products, arithmetic and copies ran while one was open for 14% of the time, Pallas kernels for 18%

profile of v3, /device:TPU:0, one launch (start us, length us, event | category | flops | bytes accessed | tf_op | source)
XLA Modules:
  0.0 96.3 jit_solution(5852713475177111967)
XLA Ops:
  0.7 6.1 %collective-permute-start = (bf16[256,32,48]{0,2,1:T(8,128)(2,1)}, bf16[256,32,48]{0,2,1:T(8,128)(2,1)S(1)}, u32[]{:S(2)}, u32[]{:S(2)}) collective-permute-start(bf16[256,32,48]{0,2,1:T(8,128)(2,1)} %bitcast.75), channel_id=1, source_target_pairs={{0,14},{2,0},{4,2},{6,4},{8,6},{10,8},{12,10},{14,12},{1,15},{3,1}... | collective-permute-start | bytes 2359304 | tf_op jit(solution)/shard_map/ppermute | solution.py:51
  6.7 1.2 %slice_select_fusion = bf16[256,18,48]{0,2,1:T(8,128)(2,1)S(1)} fusion(bf16[256,32,48]{0,2,1:T(8,128)(2,1)} %bitcast.76, pred[]{:T(512)S(6)} %eq.28), kind=kLoop, calls=%fused_computation.19 | loop fusion | flops 221184 | bytes 1327105 | tf_op jit(solution)/shard_map/jit(_where)/select_n | solution.py:36
  8.0 0.7 and_bitcast_fusion
  8.8 1.3 %convert_reduce_fusion.2 = (f32[64]{0:T(128)S(1)}, f32[64]{0:T(128)S(1)}, f32[64]{0:T(128)S(1)}) fusion(s32[32,48]{1,0:T(8,128)} %bitcast.81, pred[32,48]{1,0:T(8,128)(4,1)S(1)} %get-tuple-element.10, f32[32]{0:T(128)S(1)} %add_convert_fusion), kind=kLoop, calls=%fused_computation.14 | loop fusion | flops 786240 | bytes 8576 | tf_op jit(solution)/shard_map/reduce_sum | solution.py:253
  10.7 0.9 fusion.10.rest_3_
  11.5 1.2 %dynamic_slice.4 = s32[1]{0:T(128)} dynamic-slice(s32[8]{0:T(128)} %param.11, s32[]{:T(128)S(6)} %select_n.89), dynamic_slice_sizes={1} | dynamic-slice | bytes 12 | tf_op jit(solution)/shard_map/jit(dynamic_index_in_dim)/dynamic_slice | solution.py:216
  13.4 2.2 %fusion.2 = f32[3,32,48]{2,0,1:T(4,128)S(1)} fusion(s32[32,48]{1,0:T(8,128)} %bitcast.82, pred[32,48]{1,0:T(8,128)(4,1)S(1)} %get-tuple-element.10, f32[3,64]{1,0:T(4,128)S(1)} %collective-permute-done.5, f32[1,64]{1,0:T(1,128)S(1)} %bitcast.92, f32[1,64]{1,0:T(1,128)S(1)} %bitcast.94, f32[1,64]{1,0:T(1,128)S(1)} %bitcast.90), kind=kOutput, calls=%fused_computation.17 | convolution fusion | flops 3736128 | bytes 27648 | tf_op jit(solution)/shard_map/sk,khw->shw/dot_general | solution.py:289
  16.1 2.9 %bitcast_convert_fusion.x_ref = f32[5040,256]{1,0:T(8,128)} fusion(bf16[70,72,256]{2,1,0:T(8,128)(2,1)S(1)} %pad.14), kind=kLoop, calls=%fused_computation.5 | loop fusion | flops 1290240 | bytes 7741440 | tf_op jit(solution)/shard_map/reshape | solution.py:235
  19.1 17.0 %shard_map.113.rest_0_ = f32[4,2304,256]{2,1,0:T(8,128)} custom-call(f32[5040,256]{1,0:T(8,128)} %bitcast_convert_fusion.x_ref, bf16[256,512]{1,0:T(8,128)(2,1)} %point_ref.3, bf16[3,9,256,512]{3,2,1,0:T(8,128)(2,1)} %dilated_ref.3), custom_call_target="tpu_custom_call" | custom-call | flops 8455716864 | bytes 18137088 | tf_op jit(solution)/shard_map/pallas_call | solution.py:131
  37.9 1.7 %fusion.16.rest_2_ = f32[1,256]{1,0:T(1,128)} fusion(bf16[256,1]{0,1:T(2,128)(2,1)S(1)} %reshape.81, bf16[256,1280]{1,0:T(8,128)(2,1)} %rest_1_.1), kind=kOutput, calls=%fused_computation.40 | convolution fusion | flops 131072 | bytes 132608 | tf_op jit(solution)/shard_map/dot_general | solution.py:266
  40.0 2.9 %bitcast_convert_fusion.1.x_ref = f32[5040,256]{1,0:T(8,128)} fusion(bf16[70,72,256]{2,1,0:T(8,128)(2,1)S(1)} %pad.13), kind=kLoop, calls=%fused_computation.6 | loop fusion | flops 1290240 | bytes 7741440 | tf_op jit(solution)/shard_map/reshape | solution.py:235
  42.9 21.3 %shard_map.114 = f32[2304,256]{1,0:T(8,128)} custom-call(f32[5040,256]{1,0:T(8,128)} %bitcast_convert_fusion.1.x_ref, bf16[256,512]{1,0:T(8,128)(2,1)} %point_ref.3, bf16[3,9,256,512]{3,2,1,0:T(8,128)(2,1)} %dilated_ref.3, f32[4,2304,256]{2,1,0:T(8,128)} %shard_map.113.rest_0_, bf16[256,1280]{1,0:T(8,128)(2,1)} %rest_1_.1, f32[1,256]{1,0:T(1,128)} %fusion.16.rest_2_, ...), custom_call_target="tpu_custom_call" | custom-call | flops 9663676416 | bytes 18137088 | tf_op jit(solution)/shard_map/pallas_call | solution.py:131
  64.2 1.0 %slice_select_fusion.2 = f32[144,256]{1,0:T(8,128)S(1)} fusion(f32[2304,256]{1,0:T(8,128)} %shard_map.114, pred[]{:T(512)S(6)} %eq.28), kind=kLoop, calls=%fused_computation.39 | loop fusion | flops 36864 | bytes 442369 | tf_op jit(solution)/shard_map/jit(_where)/select_n | solution.py:36
  65.5 1.2 %collective-permute-done.4 = f32[144,256]{1,0:T(8,128)S(1)} collective-permute-done((f32[144,256]{1,0:T(8,128)S(1)}, f32[144,256]{1,0:T(8,128)S(1)}, u32[]{:S(2)}, u32[]{:S(2)}) %collective-permute-start.4) | collective-permute-done | bytes 147488 | tf_op jit(solution)/shard_map/ppermute | solution.py:41
  66.7 1.9 %select_maximum_fusion.x_ref = f32[2736,256]{1,0:T(8,128)S(1)} fusion(f32[144,256]{1,0:T(8,128)S(1)} %get-tuple-element.20, f32[2304,256]{1,0:T(8,128)} %shard_map.114, f32[144,256]{1,0:T(8,128)S(1)} %get-tuple-element.19), kind=kLoop, calls=%fused_computation.2 | loop fusion | flops 5603328 | bytes 5455872 | tf_op jit(solution)/shard_map/concatenate | solution.py:45
  68.7 8.0 %shard_map.115 = bf16[2304,96]{1,0:T(8,128)(2,1)S(1)} custom-call(f32[2736,256]{1,0:T(8,128)S(1)} %select_maximum_fusion.x_ref, bf16[25,96,256]{2,1,0:T(8,128)(2,1)S(1)} %copy-done.1), custom_call_target="tpu_custom_call" | custom-call | flops 2831155200 | bytes 4472832 | tf_op jit(solution)/shard_map/pallas_call | solution.py:167
  77.6 0.7 multiply_reduce_fusion
  78.3 2.0 %pad_maximum_fusion.2 = f32[3]{0:T(128)S(1)} fusion(f32[1]{0:T(128)} %bitcast.37, f32[1]{0:T(128)} %bitcast.36, f32[1]{0:T(128)} %bitcast.33), kind=kLoop, calls=%fused_computation.59 | loop fusion | flops 6 | bytes 24 | tf_op jit(solution)/shard_map/stack | solution.py:307
  80.6 0.6 copy.18
  81.5 3.6 %collective-permute-done.7 = f32[3]{0:T(128)S(1)} collective-permute-done((f32[3]{0:T(128)S(1)}, f32[3]{0:T(128)S(1)}, u32[]{:S(2)}, u32[]{:S(2)}) %collective-permute-start.7) | collective-permute-done | bytes 44 | tf_op jit(solution)/shard_map/ppermute | solution.py:63
  85.1 3.6 %collective-permute-done.8 = f32[3]{0:T(128)S(1)} collective-permute-done((f32[3]{0:T(128)S(1)}, f32[3]{0:T(128)S(1)}, u32[]{:S(2)}, u32[]{:S(2)}) %collective-permute-start.8) | collective-permute-done | bytes 44 | tf_op jit(solution)/shard_map/ppermute | solution.py:63
  88.7 4.5 %collective-permute-done.9 = f32[3]{0:T(128)S(1)} collective-permute-done((f32[3]{0:T(128)S(1)}, f32[3]{0:T(128)S(1)}, u32[]{:S(2)}, u32[]{:S(2)}) %collective-permute-start.9) | collective-permute-done | bytes 44 | tf_op jit(solution)/shard_map/ppermute | solution.py:63
  93.1 0.7 fusion.28
  95.7 0.6 pad_maximum_fusion.3
  (54 shorter events, 5.1 us)
Async XLA Ops:
  0.6 37.1 %copy-start = (bf16[256,512]{1,0:T(8,128)(2,1)S(1)}, bf16[256,512]{1,0:T(8,128)(2,1)}, u32[]{:S(2)}) copy-start(bf16[256,512]{1,0:T(8,128)(2,1)} %param.16) | copy-start | bytes 786436
  0.6 15.1 %copy-start.2 = (bf16[1,256,32,48]{1,3,2,0:T(8,128)(2,1)S(1)}, bf16[1,256,32,48]{1,3,2,0:T(8,128)(2,1)}, u32[]{:S(2)}) copy-start(bf16[1,256,32,48]{1,3,2,0:T(8,128)(2,1)} %param.10) | copy-start | bytes 2359300
  0.7 35.4 %collective-permute-start = (bf16[256,32,48]{0,2,1:T(8,128)(2,1)}, bf16[256,32,48]{0,2,1:T(8,128)(2,1)S(1)}, u32[]{:S(2)}, u32[]{:S(2)}) collective-permute-start(bf16[256,32,48]{0,2,1:T(8,128)(2,1)} %bitcast.75), channel_id=1, source_target_pairs={{0,14},{2,0},{4,2},{6,4},{8,6},{10,8},{12,10},{14,12},{1,15},{3,1}... | collective-permute-start | bytes 2359304 | tf_op jit(solution)/shard_map/ppermute | solution.py:51
  7.9 7.7 %collective-permute-start.2 = (bf16[256,18,48]{0,2,1:T(8,128)(2,1)S(1)}, bf16[256,18,48]{0,2,1:T(8,128)(2,1)S(1)}, u32[]{:S(2)}, u32[]{:S(2)}) collective-permute-start(bf16[256,18,48]{0,2,1:T(8,128)(2,1)S(1)} %slice_select_fusion), channel_id=1, source_target_pairs={{0,1},{1,0},{2,3},{3,2},{4,5},{5,4},{6,7},{7,6},{8,9},{9,8},{10,11... | collective-permute-start | bytes 1327112 | tf_op jit(solution)/shard_map/ppermute | solution.py:41
  10.1 3.3 %collective-permute-start.5 = (f32[3,64]{1,0:T(4,128)S(1)}, f32[3,64]{1,0:T(4,128)S(1)}, u32[]{:S(2)}, u32[]{:S(2)}) collective-permute-start(f32[3,64]{1,0:T(4,128)S(1)} %pad_maximum_fusion.1), channel_id=1, source_target_pairs={{0,1},{1,0},{2,3},{3,2},{4,5},{5,4},{6,7},{7,6},{8,9},{9,8},{10,11... | collective-permute-start | bytes 2312 | tf_op jit(solution)/shard_map/ppermute | solution.py:63
  36.5 1.2 %collective-permute-start.3 = (f32[512]{0:T(512)S(1)}, f32[512]{0:T(512)S(1)}, u32[]{:S(2)}, u32[]{:S(2)}) collective-permute-start(f32[512]{0:T(512)S(1)} %pad_maximum_fusion), channel_id=1, source_target_pairs={{0,1},{1,0},{2,3},{3,2},{4,5},{5,4},{6,7},{7,6},{8,9},{9,8},{10,11... | collective-permute-start | bytes 6152 | tf_op jit(solution)/shard_map/ppermute | solution.py:63
  36.6 3.0 %collective-permute-start.1 = (bf16[256,18,48]{0,2,1:T(8,128)(2,1)S(1)}, bf16[256,18,48]{0,2,1:T(8,128)(2,1)S(1)}, u32[]{:S(2)}, u32[]{:S(2)}) collective-permute-start(bf16[256,18,48]{0,2,1:T(8,128)(2,1)S(1)} %slice_select_fusion.1), channel_id=1, source_target_pairs={{0,1},{1,0},{2,3},{3,2},{4,5},{5,4},{6,7},{7,6},{8,9},{9,8},{10,11... | collective-permute-start | bytes 1327112 | tf_op jit(solution)/shard_map/ppermute | solution.py:41
  65.2 1.4 %collective-permute-start.4 = (f32[144,256]{1,0:T(8,128)S(1)}, f32[144,256]{1,0:T(8,128)S(1)}, u32[]{:S(2)}, u32[]{:S(2)}) collective-permute-start(f32[144,256]{1,0:T(8,128)S(1)} %slice_select_fusion.2), channel_id=1, source_target_pairs={{0,1},{1,0},{2,3},{3,2},{4,5},{5,4},{6,7},{7,6},{8,9},{9,8},{10,11... | collective-permute-start | bytes 442376 | tf_op jit(solution)/shard_map/ppermute | solution.py:41
  66.7 2.0 %copy-start.1 = (bf16[25,96,256]{2,1,0:T(8,128)(2,1)S(1)}, bf16[25,96,256]{2,1,0:T(8,128)(2,1)}, u32[]{:S(2)}) copy-start(bf16[25,96,256]{2,1,0:T(8,128)(2,1)} %weight_ref.1) | copy-start | bytes 3686404
  68.7 8.4 %copy-start.4 = (bf16[4,32]{1,0:T(4,128)(2,1)S(1)}, bf16[4,32]{1,0:T(4,128)(2,1)}, u32[]{:S(2)}) copy-start(bf16[4,32]{1,0:T(4,128)(2,1)} %param.19) | copy-start | bytes 772
  76.7 0.9 copy-start.3
  80.3 1.2 %collective-permute-start.6 = (f32[3]{0:T(128)S(1)}, f32[3]{0:T(128)S(1)}, u32[]{:S(2)}, u32[]{:S(2)}) collective-permute-start(f32[3]{0:T(128)S(1)} %pad_maximum_fusion.2), channel_id=1, source_target_pairs={{0,1},{1,0},{2,3},{3,2},{4,5},{5,4},{6,7},{7,6},{8,9},{9,8},{10,11... | collective-permute-start | bytes 44 | tf_op jit(solution)/shard_map/ppermute | solution.py:63
  81.5 3.6 %collective-permute-start.7 = (f32[3]{0:T(128)S(1)}, f32[3]{0:T(128)S(1)}, u32[]{:S(2)}, u32[]{:S(2)}) collective-permute-start(f32[3]{0:T(128)S(1)} %add.74), channel_id=1, source_target_pairs={{0,2},{2,0},{4,6},{6,4},{8,10},{10,8},{12,14},{14,12},{1,3},{3,1},... | collective-permute-start | bytes 44 | tf_op jit(solution)/shard_map/ppermute | solution.py:63
  85.1 3.6 %collective-permute-start.8 = (f32[3]{0:T(128)S(1)}, f32[3]{0:T(128)S(1)}, u32[]{:S(2)}, u32[]{:S(2)}) collective-permute-start(f32[3]{0:T(128)S(1)} %add.75), channel_id=1, source_target_pairs={{0,4},{2,6},{4,0},{6,2},{8,12},{10,14},{12,8},{14,10},{1,5},{3,7},... | collective-permute-start | bytes 44 | tf_op jit(solution)/shard_map/ppermute | solution.py:63
  88.7 4.5 %collective-permute-start.9 = (f32[3]{0:T(128)S(1)}, f32[3]{0:T(128)S(1)}, u32[]{:S(2)}, u32[]{:S(2)}) collective-permute-start(f32[3]{0:T(128)S(1)} %add.76), channel_id=1, source_target_pairs={{0,8},{2,10},{4,12},{6,14},{8,0},{10,2},{12,4},{14,6},{1,9},{3,11}... | collective-permute-start | bytes 44 | tf_op jit(solution)/shard_map/ppermute | solution.py:63

commit v4 on v3

--- a/solution.py
+++ b/solution.py
@@ -56,6 +56,18 @@
         count = lax.axis_size(axis)
         if count & (count - 1):
             value = jax.tree.map(lambda v: lax.psum(v, axis), value)
+            continue
+        if 2 < count <= 8 and not isinstance(value, tuple):
+            index = lax.axis_index(axis)
+            copies = [value] + [
+                lax.ppermute(value, axis, [(i, (i + k) % count) for i in range(count)])
+                for k in range(1, count)
+            ]
+            stacked = jnp.stack(copies)
+            ordered = jnp.take(stacked, (index - jnp.arange(count)) % count, axis=0)
+            value = ordered[0]
+            for source in range(1, count):
+                value = value + ordered[source]
             continue
         step = 1
         while step < count:

time: 96.8 us -> 97.6 us (level)
  starting transfers between devices: 7.75 us -> 16.6 us
  waiting for transfers between devices: 13.6 us -> 4.93 us
    ppermute x6 -> x3, waiting for transfers between devices: 12.4 us -> 0.84 us  [all_sum(): other = lax.ppermute(value, axis, pairs)]
    ppermute x0 -> x7, starting transfers between devices: none -> 8.86 us  [all_sum(): lax.ppermute(value, axis, [(i, (i + k) % count) for i in range(count)])]
    ppermute x0 -> x7, waiting for transfers between devices: none -> 2.92 us  [all_sum(): lax.ppermute(value, axis, [(i, (i + k) % count) for i in range(count)])]
  transfers between devices with their start and end apart: 10 -> 14, of which waited for: 6 -> 7; matrix products, arithmetic and copies ran while one was open for 14% -> 14% of each run, Pallas kernels for 18% -> 17%
where the time goes in v4:
time: 97.6 us; the launch traced here: 97.1 us
  Pallas kernels  46.2 us (47%)
  other arithmetic  17.4 us (18%)
  starting transfers between devices  16.6 us (17%)
  waiting for transfers between devices  4.93 us (5%)
  matrix products  4.48 us (5%)
  local copies, waits for them, and re-layouts  4.01 us (4%)
  between operations  3.48 us (4%)
    pallas_call x2, Pallas kernels, aspp_pass(): pl.pallas_call(body, out_shape=out_shape, compiler_params=pltpu.CompilerP...  38.2 us
    ppermute x7, starting transfers between devices, all_sum(): lax.ppermute(value, axis, [(i, (i + k) % count) for i in range(count)])  8.86 us
    pallas_call x1, Pallas kernels, head_kernel_call(): pl.pallas_call(body, out_shape=jax.ShapeDtypeStruct((blocks * block, outp...  8 us
    ppermute x1, starting transfers between devices, shifted(): return lax.ppermute(value, axis, pairs)  6.09 us
    reshape x2, other arithmetic, flat_of(): return jnp.pad(jnp.transpose(wide, (1, 2, 0)).astype(jnp.float32), ((1, 1...  5.88 us
    ppermute x7, waiting for transfers between devices, all_sum(): lax.ppermute(value, axis, [(i, (i + k) % count) for i in range(count)])  2.92 us
    select_n x3, other arithmetic, with_rims(): jnp.where(first, lax.slice_in_dim(block, size - width, None, axis=dim), l...  2.24 us
    dot_general x1, matrix products, shards(): jnp.einsum('sk,khw->shw', inst_stats, onehot, precision=lax.Precision.HIG...  2.23 us
  transfers between devices with their start and end apart: 14, of which 7 were waited for; matrix products, arithmetic and copies ran while one was open for 14% of the time, Pallas kernels for 17%

profile of v4, /device:TPU:0, one launch (start us, length us, event | category | flops | bytes accessed | tf_op | source)
XLA Modules:
  0.0 97.1 jit_solution(12599102750918106432)
XLA Ops:
  0.7 6.1 %collective-permute-start = (bf16[256,32,48]{0,2,1:T(8,128)(2,1)}, bf16[256,32,48]{0,2,1:T(8,128)(2,1)S(1)}, u32[]{:S(2)}, u32[]{:S(2)}) collective-permute-start(bf16[256,32,48]{0,2,1:T(8,128)(2,1)} %bitcast.87), channel_id=1, source_target_pairs={{0,14},{2,0},{4,2},{6,4},{8,6},{10,8},{12,10},{14,12},{1,15},{3,1}... | collective-permute-start | bytes 2359304 | tf_op jit(solution)/shard_map/ppermute | solution.py:51
  6.7 1.2 %slice_select_fusion = bf16[256,18,48]{0,2,1:T(8,128)(2,1)S(1)} fusion(bf16[256,32,48]{0,2,1:T(8,128)(2,1)} %bitcast.88, pred[]{:T(512)S(6)} %eq.30), kind=kLoop, calls=%fused_computation.20 | loop fusion | flops 221184 | bytes 1327105 | tf_op jit(solution)/shard_map/jit(_where)/select_n | solution.py:36
  8.0 0.7 and_bitcast_fusion
  8.8 1.3 %convert_reduce_fusion.2 = (f32[64]{0:T(128)S(1)}, f32[64]{0:T(128)S(1)}, f32[64]{0:T(128)S(1)}) fusion(s32[32,48]{1,0:T(8,128)} %bitcast.93, pred[32,48]{1,0:T(8,128)(4,1)S(1)} %get-tuple-element.10, f32[32]{0:T(128)S(1)} %add_convert_fusion), kind=kLoop, calls=%fused_computation.15 | loop fusion | flops 786240 | bytes 8576 | tf_op jit(solution)/shard_map/reduce_sum | solution.py:265
  10.7 0.8 fusion.10.rest_3_
  11.6 1.2 %dynamic_slice.4 = s32[1]{0:T(128)} dynamic-slice(s32[8]{0:T(128)} %param.11, s32[]{:T(128)S(6)} %select_n.126), dynamic_slice_sizes={1} | dynamic-slice | bytes 12 | tf_op jit(solution)/shard_map/jit(dynamic_index_in_dim)/dynamic_slice | solution.py:228
  13.5 2.2 %fusion.2 = f32[3,32,48]{2,0,1:T(4,128)S(1)} fusion(s32[32,48]{1,0:T(8,128)} %bitcast.94, pred[32,48]{1,0:T(8,128)(4,1)S(1)} %get-tuple-element.10, f32[3,64]{1,0:T(4,128)S(1)} %collective-permute-done.5, f32[1,64]{1,0:T(1,128)S(1)} %bitcast.104, f32[1,64]{1,0:T(1,128)S(1)} %bitcast.106, f32[1,64]{1,0:T(1,128)S(1)} %bitcast.102), kind=kOutput, calls=%fused_computation.18 | convolution fusion | flops 3736128 | bytes 27648 | tf_op jit(solution)/shard_map/sk,khw->shw/dot_general | solution.py:301
  16.2 2.9 %bitcast_convert_fusion.x_ref = f32[5040,256]{1,0:T(8,128)} fusion(bf16[70,72,256]{2,1,0:T(8,128)(2,1)S(1)} %pad.14), kind=kLoop, calls=%fused_computation.6 | loop fusion | flops 1290240 | bytes 7741440 | tf_op jit(solution)/shard_map/reshape | solution.py:247
  19.1 17.0 %shard_map.113.rest_0_ = f32[4,2304,256]{2,1,0:T(8,128)} custom-call(f32[5040,256]{1,0:T(8,128)} %bitcast_convert_fusion.x_ref, bf16[256,512]{1,0:T(8,128)(2,1)} %point_ref.3, bf16[3,9,256,512]{3,2,1,0:T(8,128)(2,1)} %dilated_ref.3), custom_call_target="tpu_custom_call" | custom-call | flops 8455716864 | bytes 18137088 | tf_op jit(solution)/shard_map/pallas_call | solution.py:143
  38.0 1.7 %fusion.16.rest_2_ = f32[1,256]{1,0:T(1,128)} fusion(bf16[256,1]{0,1:T(2,128)(2,1)S(1)} %reshape.160, bf16[256,1280]{1,0:T(8,128)(2,1)} %rest_1_.1), kind=kOutput, calls=%fused_computation.41 | convolution fusion | flops 131072 | bytes 132608 | tf_op jit(solution)/shard_map/dot_general | solution.py:278
  40.1 2.9 %bitcast_convert_fusion.1.x_ref = f32[5040,256]{1,0:T(8,128)} fusion(bf16[70,72,256]{2,1,0:T(8,128)(2,1)S(1)} %pad.13), kind=kLoop, calls=%fused_computation.7 | loop fusion | flops 1290240 | bytes 7741440 | tf_op jit(solution)/shard_map/reshape | solution.py:247
  43.0 21.3 %shard_map.114 = f32[2304,256]{1,0:T(8,128)} custom-call(f32[5040,256]{1,0:T(8,128)} %bitcast_convert_fusion.1.x_ref, bf16[256,512]{1,0:T(8,128)(2,1)} %point_ref.3, bf16[3,9,256,512]{3,2,1,0:T(8,128)(2,1)} %dilated_ref.3, f32[4,2304,256]{2,1,0:T(8,128)} %shard_map.113.rest_0_, bf16[256,1280]{1,0:T(8,128)(2,1)} %rest_1_.1, f32[1,256]{1,0:T(1,128)} %fusion.16.rest_2_, ...), custom_call_target="tpu_custom_call" | custom-call | flops 9663676416 | bytes 18137088 | tf_op jit(solution)/shard_map/pallas_call | solution.py:143
  64.3 1.0 %slice_select_fusion.2 = f32[144,256]{1,0:T(8,128)S(1)} fusion(f32[2304,256]{1,0:T(8,128)} %shard_map.114, pred[]{:T(512)S(6)} %eq.30), kind=kLoop, calls=%fused_computation.40 | loop fusion | flops 36864 | bytes 442369 | tf_op jit(solution)/shard_map/jit(_where)/select_n | solution.py:36
  65.6 1.2 %collective-permute-done.4 = f32[144,256]{1,0:T(8,128)S(1)} collective-permute-done((f32[144,256]{1,0:T(8,128)S(1)}, f32[144,256]{1,0:T(8,128)S(1)}, u32[]{:S(2)}, u32[]{:S(2)}) %collective-permute-start.4) | collective-permute-done | bytes 147488 | tf_op jit(solution)/shard_map/ppermute | solution.py:41
  66.8 1.9 %select_maximum_fusion.x_ref = f32[2736,256]{1,0:T(8,128)S(1)} fusion(f32[144,256]{1,0:T(8,128)S(1)} %get-tuple-element.20, f32[2304,256]{1,0:T(8,128)} %shard_map.114, f32[144,256]{1,0:T(8,128)S(1)} %get-tuple-element.19), kind=kLoop, calls=%fused_computation.3 | loop fusion | flops 5603328 | bytes 5455872 | tf_op jit(solution)/shard_map/concatenate | solution.py:45
  68.8 8.0 %shard_map.115 = bf16[2304,96]{1,0:T(8,128)(2,1)S(1)} custom-call(f32[2736,256]{1,0:T(8,128)S(1)} %select_maximum_fusion.x_ref, bf16[25,96,256]{2,1,0:T(8,128)(2,1)S(1)} %copy-done.1), custom_call_target="tpu_custom_call" | custom-call | flops 2831155200 | bytes 4472832 | tf_op jit(solution)/shard_map/pallas_call | solution.py:179
  77.7 0.7 multiply_reduce_fusion
  78.4 1.9 %pad_maximum_fusion.2 = f32[3]{0:T(128)S(1)} fusion(f32[1]{0:T(128)} %bitcast.37, f32[1]{0:T(128)} %bitcast.36, f32[1]{0:T(128)} %bitcast.33), kind=kLoop, calls=%fused_computation.74 | loop fusion | flops 6 | bytes 24 | tf_op jit(solution)/shard_map/stack | solution.py:319
  81.5 2.5 %collective-permute-start.9 = (f32[3]{0:T(128)S(1)}, f32[3]{0:T(128)S(1)}, u32[]{:S(2)}, u32[]{:S(2)}) collective-permute-start(f32[3]{0:T(128)S(1)} %add.126), channel_id=1, source_target_pairs={{0,6},{2,8},{4,10},{6,12},{8,14},{10,0},{12,2},{14,4},{1,7},{3,9},... | collective-permute-start | bytes 44 | tf_op jit(solution)/shard_map/ppermute | solution.py:63
  84.0 2.8 %collective-permute-start.10 = (f32[3]{0:T(128)S(1)}, f32[3]{0:T(128)S(1)}, u32[]{:S(2)}, u32[]{:S(2)}) collective-permute-start(f32[3]{0:T(128)S(1)} %add.126), channel_id=1, source_target_pairs={{0,8},{2,10},{4,12},{6,14},{8,0},{10,2},{12,4},{14,6},{1,9},{3,11}... | collective-permute-start | bytes 44 | tf_op jit(solution)/shard_map/ppermute | solution.py:63
  86.9 0.8 collective-permute-done.7
  87.7 2.0 %collective-permute-start.12 = (f32[3]{0:T(128)S(1)}, f32[3]{0:T(128)S(1)}, u32[]{:S(2)}, u32[]{:S(2)}) collective-permute-start(f32[3]{0:T(128)S(1)} %add.126), channel_id=1, source_target_pairs={{0,12},{2,14},{4,0},{6,2},{8,4},{10,6},{12,8},{14,10},{1,13},{3,15... | collective-permute-start | bytes 44 | tf_op jit(solution)/shard_map/ppermute | solution.py:63
  89.7 1.5 %collective-permute-start.13 = (f32[3]{0:T(128)S(1)}, f32[3]{0:T(128)S(1)}, u32[]{:S(2)}, u32[]{:S(2)}) collective-permute-start(f32[3]{0:T(128)S(1)} %add.126), channel_id=1, source_target_pairs={{0,14},{2,0},{4,2},{6,4},{8,6},{10,8},{12,10},{14,12},{1,15},{3,1}... | collective-permute-start | bytes 44 | tf_op jit(solution)/shard_map/ppermute | solution.py:63
  91.3 2.0 %collective-permute-done.13 = f32[3]{0:T(128)S(1)} collective-permute-done((f32[3]{0:T(128)S(1)}, f32[3]{0:T(128)S(1)}, u32[]{:S(2)}, u32[]{:S(2)}) %collective-permute-start.13) | collective-permute-done | bytes 44 | tf_op jit(solution)/shard_map/ppermute | solution.py:63
  (66 shorter events, 8.0 us)
Async XLA Ops:
  0.6 37.1 %copy-start = (bf16[256,512]{1,0:T(8,128)(2,1)S(1)}, bf16[256,512]{1,0:T(8,128)(2,1)}, u32[]{:S(2)}) copy-start(bf16[256,512]{1,0:T(8,128)(2,1)} %param.16) | copy-start | bytes 786436
  0.6 15.1 %copy-start.2 = (bf16[1,256,32,48]{1,3,2,0:T(8,128)(2,1)S(1)}, bf16[1,256,32,48]{1,3,2,0:T(8,128)(2,1)}, u32[]{:S(2)}) copy-start(bf16[1,256,32,48]{1,3,2,0:T(8,128)(2,1)} %param.10) | copy-start | bytes 2359300
  0.7 35.4 %collective-permute-start = (bf16[256,32,48]{0,2,1:T(8,128)(2,1)}, bf16[256,32,48]{0,2,1:T(8,128)(2,1)S(1)}, u32[]{:S(2)}, u32[]{:S(2)}) collective-permute-start(bf16[256,32,48]{0,2,1:T(8,128)(2,1)} %bitcast.87), channel_id=1, source_target_pairs={{0,14},{2,0},{4,2},{6,4},{8,6},{10,8},{12,10},{14,12},{1,15},{3,1}... | collective-permute-start | bytes 2359304 | tf_op jit(solution)/shard_map/ppermute | solution.py:51
  7.9 7.8 %collective-permute-start.2 = (bf16[256,18,48]{0,2,1:T(8,128)(2,1)S(1)}, bf16[256,18,48]{0,2,1:T(8,128)(2,1)S(1)}, u32[]{:S(2)}, u32[]{:S(2)}) collective-permute-start(bf16[256,18,48]{0,2,1:T(8,128)(2,1)S(1)} %slice_select_fusion), channel_id=1, source_target_pairs={{0,1},{1,0},{2,3},{3,2},{4,5},{5,4},{6,7},{7,6},{8,9},{9,8},{10,11... | collective-permute-start | bytes 1327112 | tf_op jit(solution)/shard_map/ppermute | solution.py:41
  10.1 3.3 %collective-permute-start.5 = (f32[3,64]{1,0:T(4,128)S(1)}, f32[3,64]{1,0:T(4,128)S(1)}, u32[]{:S(2)}, u32[]{:S(2)}) collective-permute-start(f32[3,64]{1,0:T(4,128)S(1)} %pad_maximum_fusion.1), channel_id=1, source_target_pairs={{0,1},{1,0},{2,3},{3,2},{4,5},{5,4},{6,7},{7,6},{8,9},{9,8},{10,11... | collective-permute-start | bytes 2312 | tf_op jit(solution)/shard_map/ppermute | solution.py:75
  36.5 1.2 %collective-permute-start.3 = (f32[512]{0:T(512)S(1)}, f32[512]{0:T(512)S(1)}, u32[]{:S(2)}, u32[]{:S(2)}) collective-permute-start(f32[512]{0:T(512)S(1)} %pad_maximum_fusion), channel_id=1, source_target_pairs={{0,1},{1,0},{2,3},{3,2},{4,5},{5,4},{6,7},{7,6},{8,9},{9,8},{10,11... | collective-permute-start | bytes 6152 | tf_op jit(solution)/shard_map/ppermute | solution.py:75
  36.7 3.0 %collective-permute-start.1 = (bf16[256,18,48]{0,2,1:T(8,128)(2,1)S(1)}, bf16[256,18,48]{0,2,1:T(8,128)(2,1)S(1)}, u32[]{:S(2)}, u32[]{:S(2)}) collective-permute-start(bf16[256,18,48]{0,2,1:T(8,128)(2,1)S(1)} %slice_select_fusion.1), channel_id=1, source_target_pairs={{0,1},{1,0},{2,3},{3,2},{4,5},{5,4},{6,7},{7,6},{8,9},{9,8},{10,11... | collective-permute-start | bytes 1327112 | tf_op jit(solution)/shard_map/ppermute | solution.py:41
  65.3 1.4 %collective-permute-start.4 = (f32[144,256]{1,0:T(8,128)S(1)}, f32[144,256]{1,0:T(8,128)S(1)}, u32[]{:S(2)}, u32[]{:S(2)}) collective-permute-start(f32[144,256]{1,0:T(8,128)S(1)} %slice_select_fusion.2), channel_id=1, source_target_pairs={{0,1},{1,0},{2,3},{3,2},{4,5},{5,4},{6,7},{7,6},{8,9},{9,8},{10,11... | collective-permute-start | bytes 442376 | tf_op jit(solution)/shard_map/ppermute | solution.py:41
  66.8 2.0 %copy-start.1 = (bf16[25,96,256]{2,1,0:T(8,128)(2,1)S(1)}, bf16[25,96,256]{2,1,0:T(8,128)(2,1)}, u32[]{:S(2)}) copy-start(bf16[25,96,256]{2,1,0:T(8,128)(2,1)} %weight_ref.1) | copy-start | bytes 3686404
  68.8 8.4 %copy-start.4 = (bf16[4,32]{1,0:T(4,128)(2,1)S(1)}, bf16[4,32]{1,0:T(4,128)(2,1)}, u32[]{:S(2)}) copy-start(bf16[4,32]{1,0:T(4,128)(2,1)} %param.19) | copy-start | bytes 772
  76.8 0.9 copy-start.3
  80.3 1.2 %collective-permute-start.6 = (f32[3]{0:T(128)S(1)}, f32[3]{0:T(128)S(1)}, u32[]{:S(2)}, u32[]{:S(2)}) collective-permute-start(f32[3]{0:T(128)S(1)} %pad_maximum_fusion.2), channel_id=1, source_target_pairs={{0,1},{1,0},{2,3},{3,2},{4,5},{5,4},{6,7},{7,6},{8,9},{9,8},{10,11... | collective-permute-start | bytes 44 | tf_op jit(solution)/shard_map/ppermute | solution.py:75
  81.5 6.3 %collective-permute-start.7 = (f32[3]{0:T(128)S(1)}, f32[3]{0:T(128)S(1)}, u32[]{:S(2)}, u32[]{:S(2)}) collective-permute-start(f32[3]{0:T(128)S(1)} %add.126), channel_id=1, source_target_pairs={{0,2},{2,4},{4,6},{6,8},{8,10},{10,12},{12,14},{14,0},{1,3},{3,5},... | collective-permute-start | bytes 44 | tf_op jit(solution)/shard_map/ppermute | solution.py:63
  81.5 8.2 %collective-permute-start.8 = (f32[3]{0:T(128)S(1)}, f32[3]{0:T(128)S(1)}, u32[]{:S(2)}, u32[]{:S(2)}) collective-permute-start(f32[3]{0:T(128)S(1)} %add.126), channel_id=1, source_target_pairs={{0,4},{2,6},{4,8},{6,10},{8,12},{10,14},{12,0},{14,2},{1,5},{3,7},... | collective-permute-start | bytes 44 | tf_op jit(solution)/shard_map/ppermute | solution.py:63
  81.5 9.7 %collective-permute-start.9 = (f32[3]{0:T(128)S(1)}, f32[3]{0:T(128)S(1)}, u32[]{:S(2)}, u32[]{:S(2)}) collective-permute-start(f32[3]{0:T(128)S(1)} %add.126), channel_id=1, source_target_pairs={{0,6},{2,8},{4,10},{6,12},{8,14},{10,0},{12,2},{14,4},{1,7},{3,9},... | collective-permute-start | bytes 44 | tf_op jit(solution)/shard_map/ppermute | solution.py:63
  84.0 7.2 %collective-permute-start.10 = (f32[3]{0:T(128)S(1)}, f32[3]{0:T(128)S(1)}, u32[]{:S(2)}, u32[]{:S(2)}) collective-permute-start(f32[3]{0:T(128)S(1)} %add.126), channel_id=1, source_target_pairs={{0,8},{2,10},{4,12},{6,14},{8,0},{10,2},{12,4},{14,6},{1,9},{3,11}... | collective-permute-start | bytes 44 | tf_op jit(solution)/shard_map/ppermute | solution.py:63
  86.8 4.5 %collective-permute-start.11 = (f32[3]{0:T(128)S(1)}, f32[3]{0:T(128)S(1)}, u32[]{:S(2)}, u32[]{:S(2)}) collective-permute-start(f32[3]{0:T(128)S(1)} %add.126), channel_id=1, source_target_pairs={{0,10},{2,12},{4,14},{6,0},{8,2},{10,4},{12,6},{14,8},{1,11},{3,13... | collective-permute-start | bytes 44 | tf_op jit(solution)/shard_map/ppermute | solution.py:63
  87.7 3.6 %collective-permute-start.12 = (f32[3]{0:T(128)S(1)}, f32[3]{0:T(128)S(1)}, u32[]{:S(2)}, u32[]{:S(2)}) collective-permute-start(f32[3]{0:T(128)S(1)} %add.126), channel_id=1, source_target_pairs={{0,12},{2,14},{4,0},{6,2},{8,4},{10,6},{12,8},{14,10},{1,13},{3,15... | collective-permute-start | bytes 44 | tf_op jit(solution)/shard_map/ppermute | solution.py:63
  89.7 3.6 %collective-permute-start.13 = (f32[3]{0:T(128)S(1)}, f32[3]{0:T(128)S(1)}, u32[]{:S(2)}, u32[]{:S(2)}) collective-permute-start(f32[3]{0:T(128)S(1)} %add.126), channel_id=1, source_target_pairs={{0,14},{2,0},{4,2},{6,4},{8,6},{10,8},{12,10},{14,12},{1,15},{3,1}... | collective-permute-start | bytes 44 | tf_op jit(solution)/shard_map/ppermute | solution.py:63

commit v5 on v3

--- a/solution.py
+++ b/solution.py
@@ -76,12 +76,28 @@
 
     def body(x_ref, point_ref, dilated_ref, *rest):
         if finish:
-            earlier_ref, proj_ref, pool_ref, keep_ref, out_ref = rest
+            earlier_hbm, proj_ref, pool_ref, keep_ref, out_ref, earlier_ref, sems = rest
         else:
-            (out_ref,) = rest
+            out_hbm, out_ref, sems = rest
+
+        def block_copy(index):
+            rows = pl.ds(index * block, block)
+            if finish:
+                return pltpu.make_async_copy(
+                    earlier_hbm.at[:, rows, :], earlier_ref.at[:, rows, :], sems.at[index]
+                )
+            return pltpu.make_async_copy(
+                out_ref.at[:, rows, :], out_hbm.at[:, rows, :], sems.at[index]
+            )
+
+        if finish:
+            for index in range(blocks):
+                block_copy(index).start()
         for index in range(blocks):
             base = front + margin * pitch + index * block
             rows = pl.ds(index * block, block)
+            if finish:
+                block_copy(index).wait()
 
             def window(shift):
                 return x_ref[pl.ds(base + shift, block), :].astype(jnp.bfloat16)
@@ -107,6 +123,7 @@
             if not finish:
                 for branch, total in enumerate(sums):
                     out_ref[branch, rows, :] = total
+                block_copy(index).start()
                 continue
             mixed = None
             for branch, total in enumerate(sums):
@@ -120,17 +137,31 @@
             mixed = mixed + pool_ref[...]
             rounded = relu_bf16(mixed).astype(jnp.float32)
             out_ref[rows, :] = jnp.where(keep_ref[...] > 0.5, rounded, 0.0)
+        if not finish:
+            for index in range(blocks):
+                block_copy(index).wait()
 
     taps = 1 + 9 * len(DILATIONS)
     flops = 2 * blocks * block * channels * width * taps
+    sums_shape = (branches, blocks * block, width)
+    vmem = pl.BlockSpec(memory_space=pltpu.VMEM)
+    hbm = pl.BlockSpec(memory_space=pl.ANY)
+    scratch = [pltpu.VMEM(sums_shape, jnp.float32), pltpu.SemaphoreType.DMA((blocks,))]
     if finish:
         flops += 2 * blocks * block * branches * width * width
         out_shape = jax.ShapeDtypeStruct((blocks * block, width), jnp.float32)
+        in_specs = [vmem, vmem, vmem, hbm, vmem, vmem, vmem]
+        out_specs = vmem
     else:
-        out_shape = jax.ShapeDtypeStruct((branches, blocks * block, width), jnp.float32)
+        out_shape = jax.ShapeDtypeStruct(sums_shape, jnp.float32)
+        in_specs = [vmem, vmem, vmem]
+        out_specs = hbm
     return pl.pallas_call(
         body,
         out_shape=out_shape,
+        in_specs=in_specs,
+        out_specs=out_specs,
+        scratch_shapes=scratch,
         compiler_params=pltpu.CompilerParams(vmem_limit_bytes=56 * 1024 * 1024),
         cost_estimate=pl.CostEstimate(
             flops=flops,

time: 96.8 us -> 94.7 us (0.978)
  Pallas kernels: 46.2 us -> 44 us
    pallas_call x2, Pallas kernels: 38.2 us -> 36 us  [aspp_pass(): pl.pallas_call(body, out_shape=out_shape, in_specs=in_specs, out_specs=ou...]
  transfers between devices with their start and end apart: 10 -> 10, of which waited for: 6 -> 6; matrix products, arithmetic and copies ran while one was open for 14% -> 14% of each run, Pallas kernels for 18% -> 16%
where the time goes in v5:
time: 94.7 us; the launch traced here: 94.1 us
  Pallas kernels  44 us (46%)
  other arithmetic  17.4 us (18%)
  waiting for transfers between devices  13.6 us (14%)
  starting transfers between devices  7.74 us (8%)
  matrix products  4.49 us (5%)
  between operations  3.5 us (4%)
  local copies, waits for them, and re-layouts  3.42 us (4%)
    pallas_call x2, Pallas kernels, aspp_pass(): pl.pallas_call(body, out_shape=out_shape, in_specs=in_specs, out_specs=ou...  36 us
    ppermute x6, waiting for transfers between devices, all_sum(): other = lax.ppermute(value, axis, pairs)  12.4 us
    pallas_call x1, Pallas kernels, head_kernel_call(): pl.pallas_call(body, out_shape=jax.ShapeDtypeStruct((blocks * block, outp...  8.01 us
    ppermute x1, starting transfers between devices, shifted(): return lax.ppermute(value, axis, pairs)  6.09 us
    reshape x2, other arithmetic, flat_of(): return jnp.pad(jnp.transpose(wide, (1, 2, 0)).astype(jnp.float32), ((1, 1...  5.85 us
    select_n x3, other arithmetic, with_rims(): jnp.where(first, lax.slice_in_dim(block, size - width, None, axis=dim), l...  2.24 us
    dot_general x1, matrix products, shards(): jnp.einsum('sk,khw->shw', inst_stats, onehot, precision=lax.Precision.HIG...  2.23 us
    another operation x1, other arithmetic, shards(): jnp.stack([center_err, offset_err, counted_local])  2 us
  transfers between devices with their start and end apart: 10, of which 6 were waited for; matrix products, arithmetic and copies ran while one was open for 14% of the time, Pallas kernels for 16%

profile of v5, /device:TPU:0, one launch (start us, length us, event | category | flops | bytes accessed | tf_op | source)
XLA Modules:
  0.0 94.1 jit_solution(9963441298509768473)
XLA Ops:
  0.7 6.1 %collective-permute-start = (bf16[256,32,48]{0,2,1:T(8,128)(2,1)}, bf16[256,32,48]{0,2,1:T(8,128)(2,1)S(1)}, u32[]{:S(2)}, u32[]{:S(2)}) collective-permute-start(bf16[256,32,48]{0,2,1:T(8,128)(2,1)} %bitcast.75), channel_id=1, source_target_pairs={{0,14},{2,0},{4,2},{6,4},{8,6},{10,8},{12,10},{14,12},{1,15},{3,1}... | collective-permute-start | bytes 2359304 | tf_op jit(solution)/shard_map/ppermute | solution.py:51
  6.7 1.2 %slice_select_fusion = bf16[256,18,48]{0,2,1:T(8,128)(2,1)S(1)} fusion(bf16[256,32,48]{0,2,1:T(8,128)(2,1)} %bitcast.76, pred[]{:T(512)S(6)} %eq.28), kind=kLoop, calls=%fused_computation.19 | loop fusion | flops 221184 | bytes 1327105 | tf_op jit(solution)/shard_map/jit(_where)/select_n | solution.py:36
  8.0 0.7 and_bitcast_fusion
  8.8 1.3 %convert_reduce_fusion.2 = (f32[64]{0:T(128)S(1)}, f32[64]{0:T(128)S(1)}, f32[64]{0:T(128)S(1)}) fusion(s32[32,48]{1,0:T(8,128)} %bitcast.81, pred[32,48]{1,0:T(8,128)(4,1)S(1)} %get-tuple-element.10, f32[32]{0:T(128)S(1)} %add_convert_fusion), kind=kLoop, calls=%fused_computation.14 | loop fusion | flops 786240 | bytes 8576 | tf_op jit(solution)/shard_map/reduce_sum | solution.py:284
  10.7 0.9 fusion.10.rest_3_
  11.5 1.2 %dynamic_slice.4 = s32[1]{0:T(128)} dynamic-slice(s32[8]{0:T(128)} %param.11, s32[]{:T(128)S(6)} %select_n.89), dynamic_slice_sizes={1} | dynamic-slice | bytes 12 | tf_op jit(solution)/shard_map/jit(dynamic_index_in_dim)/dynamic_slice | solution.py:247
  13.4 2.2 %fusion.2 = f32[3,32,48]{2,0,1:T(4,128)S(1)} fusion(s32[32,48]{1,0:T(8,128)} %bitcast.82, pred[32,48]{1,0:T(8,128)(4,1)S(1)} %get-tuple-element.10, f32[3,64]{1,0:T(4,128)S(1)} %collective-permute-done.5, f32[1,64]{1,0:T(1,128)S(1)} %bitcast.92, f32[1,64]{1,0:T(1,128)S(1)} %bitcast.94, f32[1,64]{1,0:T(1,128)S(1)} %bitcast.90), kind=kOutput, calls=%fused_computation.17 | convolution fusion | flops 3736128 | bytes 27648 | tf_op jit(solution)/shard_map/sk,khw->shw/dot_general | solution.py:320
  16.1 2.9 %bitcast_convert_fusion.x_ref = f32[5040,256]{1,0:T(8,128)} fusion(bf16[70,72,256]{2,1,0:T(8,128)(2,1)S(1)} %pad.14), kind=kLoop, calls=%fused_computation.5 | loop fusion | flops 1290240 | bytes 7741440 | tf_op jit(solution)/shard_map/reshape | solution.py:266
  19.1 15.0 %shard_map.113.rest_0_ = f32[4,2304,256]{2,1,0:T(8,128)} custom-call(f32[5040,256]{1,0:T(8,128)} %bitcast_convert_fusion.x_ref, bf16[256,512]{1,0:T(8,128)(2,1)} %point_ref.3, bf16[3,9,256,512]{3,2,1,0:T(8,128)(2,1)} %dilated_ref.3), custom_call_target="tpu_custom_call" | custom-call | flops 8455716864 | bytes 18137088 | tf_op jit(solution)/shard_map/pallas_call | solution.py:159
  36.0 1.7 %fusion.16.rest_2_ = f32[1,256]{1,0:T(1,128)} fusion(bf16[256,1]{0,1:T(2,128)(2,1)S(1)} %reshape.81, bf16[256,1280]{1,0:T(8,128)(2,1)} %rest_1_.1), kind=kOutput, calls=%fused_computation.40 | convolution fusion | flops 131072 | bytes 132608 | tf_op jit(solution)/shard_map/dot_general | solution.py:297
  38.1 2.9 %bitcast_convert_fusion.1.x_ref = f32[5040,256]{1,0:T(8,128)} fusion(bf16[70,72,256]{2,1,0:T(8,128)(2,1)S(1)} %pad.13), kind=kLoop, calls=%fused_computation.6 | loop fusion | flops 1290240 | bytes 7741440 | tf_op jit(solution)/shard_map/reshape | solution.py:266
  41.0 21.0 %shard_map.114 = f32[2304,256]{1,0:T(8,128)} custom-call(f32[5040,256]{1,0:T(8,128)} %bitcast_convert_fusion.1.x_ref, bf16[256,512]{1,0:T(8,128)(2,1)} %point_ref.3, bf16[3,9,256,512]{3,2,1,0:T(8,128)(2,1)} %dilated_ref.3, f32[4,2304,256]{2,1,0:T(8,128)} %shard_map.113.rest_0_, bf16[256,1280]{1,0:T(8,128)(2,1)} %rest_1_.1, f32[1,256]{1,0:T(1,128)} %fusion.16.rest_2_, ...), custom_call_target="tpu_custom_call" | custom-call | flops 9663676416 | bytes 18137088 | tf_op jit(solution)/shard_map/pallas_call | solution.py:159
  62.0 1.0 %slice_select_fusion.2 = f32[144,256]{1,0:T(8,128)S(1)} fusion(f32[2304,256]{1,0:T(8,128)} %shard_map.114, pred[]{:T(512)S(6)} %eq.28), kind=kLoop, calls=%fused_computation.39 | loop fusion | flops 36864 | bytes 442369 | tf_op jit(solution)/shard_map/jit(_where)/select_n | solution.py:36
  63.3 1.2 %collective-permute-done.4 = f32[144,256]{1,0:T(8,128)S(1)} collective-permute-done((f32[144,256]{1,0:T(8,128)S(1)}, f32[144,256]{1,0:T(8,128)S(1)}, u32[]{:S(2)}, u32[]{:S(2)}) %collective-permute-start.4) | collective-permute-done | bytes 147488 | tf_op jit(solution)/shard_map/ppermute | solution.py:41
  64.5 1.9 %select_maximum_fusion.x_ref = f32[2736,256]{1,0:T(8,128)S(1)} fusion(f32[144,256]{1,0:T(8,128)S(1)} %get-tuple-element.20, f32[2304,256]{1,0:T(8,128)} %shard_map.114, f32[144,256]{1,0:T(8,128)S(1)} %get-tuple-element.19), kind=kLoop, calls=%fused_computation.2 | loop fusion | flops 5603328 | bytes 5455872 | tf_op jit(solution)/shard_map/concatenate | solution.py:45
  66.5 8.0 %shard_map.115 = bf16[2304,96]{1,0:T(8,128)(2,1)S(1)} custom-call(f32[2736,256]{1,0:T(8,128)S(1)} %select_maximum_fusion.x_ref, bf16[25,96,256]{2,1,0:T(8,128)(2,1)S(1)} %copy-done.1), custom_call_target="tpu_custom_call" | custom-call | flops 2831155200 | bytes 4472832 | tf_op jit(solution)/shard_map/pallas_call | solution.py:198
  75.4 0.7 multiply_reduce_fusion
  76.1 2.0 %pad_maximum_fusion.2 = f32[3]{0:T(128)S(1)} fusion(f32[1]{0:T(128)} %bitcast.37, f32[1]{0:T(128)} %bitcast.36, f32[1]{0:T(128)} %bitcast.33), kind=kLoop, calls=%fused_computation.59 | loop fusion | flops 6 | bytes 24 | tf_op jit(solution)/shard_map/stack | solution.py:338
  78.4 0.6 copy.18
  79.3 3.6 %collective-permute-done.7 = f32[3]{0:T(128)S(1)} collective-permute-done((f32[3]{0:T(128)S(1)}, f32[3]{0:T(128)S(1)}, u32[]{:S(2)}, u32[]{:S(2)}) %collective-permute-start.7) | collective-permute-done | bytes 44 | tf_op jit(solution)/shard_map/ppermute | solution.py:63
  82.9 3.6 %collective-permute-done.8 = f32[3]{0:T(128)S(1)} collective-permute-done((f32[3]{0:T(128)S(1)}, f32[3]{0:T(128)S(1)}, u32[]{:S(2)}, u32[]{:S(2)}) %collective-permute-start.8) | collective-permute-done | bytes 44 | tf_op jit(solution)/shard_map/ppermute | solution.py:63
  86.5 4.5 %collective-permute-done.9 = f32[3]{0:T(128)S(1)} collective-permute-done((f32[3]{0:T(128)S(1)}, f32[3]{0:T(128)S(1)}, u32[]{:S(2)}, u32[]{:S(2)}) %collective-permute-start.9) | collective-permute-done | bytes 44 | tf_op jit(solution)/shard_map/ppermute | solution.py:63
  90.9 0.7 fusion.28
  93.6 0.6 pad_maximum_fusion.3
  (54 shorter events, 5.1 us)
Async XLA Ops:
  0.6 35.2 %copy-start = (bf16[256,512]{1,0:T(8,128)(2,1)S(1)}, bf16[256,512]{1,0:T(8,128)(2,1)}, u32[]{:S(2)}) copy-start(bf16[256,512]{1,0:T(8,128)(2,1)} %param.16) | copy-start | bytes 786436
  0.6 15.1 %copy-start.2 = (bf16[1,256,32,48]{1,3,2,0:T(8,128)(2,1)S(1)}, bf16[1,256,32,48]{1,3,2,0:T(8,128)(2,1)}, u32[]{:S(2)}) copy-start(bf16[1,256,32,48]{1,3,2,0:T(8,128)(2,1)} %param.10) | copy-start | bytes 2359300
  0.7 33.5 %collective-permute-start = (bf16[256,32,48]{0,2,1:T(8,128)(2,1)}, bf16[256,32,48]{0,2,1:T(8,128)(2,1)S(1)}, u32[]{:S(2)}, u32[]{:S(2)}) collective-permute-start(bf16[256,32,48]{0,2,1:T(8,128)(2,1)} %bitcast.75), channel_id=1, source_target_pairs={{0,14},{2,0},{4,2},{6,4},{8,6},{10,8},{12,10},{14,12},{1,15},{3,1}... | collective-permute-start | bytes 2359304 | tf_op jit(solution)/shard_map/ppermute | solution.py:51
  7.9 7.7 %collective-permute-start.2 = (bf16[256,18,48]{0,2,1:T(8,128)(2,1)S(1)}, bf16[256,18,48]{0,2,1:T(8,128)(2,1)S(1)}, u32[]{:S(2)}, u32[]{:S(2)}) collective-permute-start(bf16[256,18,48]{0,2,1:T(8,128)(2,1)S(1)} %slice_select_fusion), channel_id=1, source_target_pairs={{0,1},{1,0},{2,3},{3,2},{4,5},{5,4},{6,7},{7,6},{8,9},{9,8},{10,11... | collective-permute-start | bytes 1327112 | tf_op jit(solution)/shard_map/ppermute | solution.py:41
  10.1 3.3 %collective-permute-start.5 = (f32[3,64]{1,0:T(4,128)S(1)}, f32[3,64]{1,0:T(4,128)S(1)}, u32[]{:S(2)}, u32[]{:S(2)}) collective-permute-start(f32[3,64]{1,0:T(4,128)S(1)} %pad_maximum_fusion.1), channel_id=1, source_target_pairs={{0,1},{1,0},{2,3},{3,2},{4,5},{5,4},{6,7},{7,6},{8,9},{9,8},{10,11... | collective-permute-start | bytes 2312 | tf_op jit(solution)/shard_map/ppermute | solution.py:63
  34.6 1.2 %collective-permute-start.3 = (f32[512]{0:T(512)S(1)}, f32[512]{0:T(512)S(1)}, u32[]{:S(2)}, u32[]{:S(2)}) collective-permute-start(f32[512]{0:T(512)S(1)} %pad_maximum_fusion), channel_id=1, source_target_pairs={{0,1},{1,0},{2,3},{3,2},{4,5},{5,4},{6,7},{7,6},{8,9},{9,8},{10,11... | collective-permute-start | bytes 6152 | tf_op jit(solution)/shard_map/ppermute | solution.py:63
  34.7 3.0 %collective-permute-start.1 = (bf16[256,18,48]{0,2,1:T(8,128)(2,1)S(1)}, bf16[256,18,48]{0,2,1:T(8,128)(2,1)S(1)}, u32[]{:S(2)}, u32[]{:S(2)}) collective-permute-start(bf16[256,18,48]{0,2,1:T(8,128)(2,1)S(1)} %slice_select_fusion.1), channel_id=1, source_target_pairs={{0,1},{1,0},{2,3},{3,2},{4,5},{5,4},{6,7},{7,6},{8,9},{9,8},{10,11... | collective-permute-start | bytes 1327112 | tf_op jit(solution)/shard_map/ppermute | solution.py:41
  63.0 1.4 %collective-permute-start.4 = (f32[144,256]{1,0:T(8,128)S(1)}, f32[144,256]{1,0:T(8,128)S(1)}, u32[]{:S(2)}, u32[]{:S(2)}) collective-permute-start(f32[144,256]{1,0:T(8,128)S(1)} %slice_select_fusion.2), channel_id=1, source_target_pairs={{0,1},{1,0},{2,3},{3,2},{4,5},{5,4},{6,7},{7,6},{8,9},{9,8},{10,11... | collective-permute-start | bytes 442376 | tf_op jit(solution)/shard_map/ppermute | solution.py:41
  64.5 2.0 %copy-start.1 = (bf16[25,96,256]{2,1,0:T(8,128)(2,1)S(1)}, bf16[25,96,256]{2,1,0:T(8,128)(2,1)}, u32[]{:S(2)}) copy-start(bf16[25,96,256]{2,1,0:T(8,128)(2,1)} %weight_ref.1) | copy-start | bytes 3686404
  66.5 8.4 %copy-start.4 = (bf16[4,32]{1,0:T(4,128)(2,1)S(1)}, bf16[4,32]{1,0:T(4,128)(2,1)}, u32[]{:S(2)}) copy-start(bf16[4,32]{1,0:T(4,128)(2,1)} %param.19) | copy-start | bytes 772
  74.5 0.9 copy-start.3
  78.1 1.2 %collective-permute-start.6 = (f32[3]{0:T(128)S(1)}, f32[3]{0:T(128)S(1)}, u32[]{:S(2)}, u32[]{:S(2)}) collective-permute-start(f32[3]{0:T(128)S(1)} %pad_maximum_fusion.2), channel_id=1, source_target_pairs={{0,1},{1,0},{2,3},{3,2},{4,5},{5,4},{6,7},{7,6},{8,9},{9,8},{10,11... | collective-permute-start | bytes 44 | tf_op jit(solution)/shard_map/ppermute | solution.py:63
  79.3 3.6 %collective-permute-start.7 = (f32[3]{0:T(128)S(1)}, f32[3]{0:T(128)S(1)}, u32[]{:S(2)}, u32[]{:S(2)}) collective-permute-start(f32[3]{0:T(128)S(1)} %add.74), channel_id=1, source_target_pairs={{0,2},{2,0},{4,6},{6,4},{8,10},{10,8},{12,14},{14,12},{1,3},{3,1},... | collective-permute-start | bytes 44 | tf_op jit(solution)/shard_map/ppermute | solution.py:63
  82.9 3.6 %collective-permute-start.8 = (f32[3]{0:T(128)S(1)}, f32[3]{0:T(128)S(1)}, u32[]{:S(2)}, u32[]{:S(2)}) collective-permute-start(f32[3]{0:T(128)S(1)} %add.75), channel_id=1, source_target_pairs={{0,4},{2,6},{4,0},{6,2},{8,12},{10,14},{12,8},{14,10},{1,5},{3,7},... | collective-permute-start | bytes 44 | tf_op jit(solution)/shard_map/ppermute | solution.py:63
  86.5 4.5 %collective-permute-start.9 = (f32[3]{0:T(128)S(1)}, f32[3]{0:T(128)S(1)}, u32[]{:S(2)}, u32[]{:S(2)}) collective-permute-start(f32[3]{0:T(128)S(1)} %add.76), channel_id=1, source_target_pairs={{0,8},{2,10},{4,12},{6,14},{8,0},{10,2},{12,4},{14,6},{1,9},{3,11}... | collective-permute-start | bytes 44 | tf_op jit(solution)/shard_map/ppermute | solution.py:63

commit v6 on v5

--- a/solution.py
+++ b/solution.py
@@ -76,9 +76,18 @@
 
     def body(x_ref, point_ref, dilated_ref, *rest):
         if finish:
-            earlier_hbm, proj_ref, pool_ref, keep_ref, out_ref, earlier_ref, sems = rest
+            (earlier_hbm, proj_ref, pool_ref, keep_ref, out_ref, earlier_ref, sems,
+             weight_ref, weight_sems) = rest
         else:
-            out_hbm, out_ref, sems = rest
+            out_hbm, out_ref, sems, weight_ref, weight_sems = rest
+
+        def weight_copy(branch):
+            return pltpu.make_async_copy(
+                dilated_ref.at[branch, :, :, lanes], weight_ref.at[branch], weight_sems.at[branch]
+            )
+
+        for branch in range(len(DILATIONS)):
+            weight_copy(branch).start()
 
         def block_copy(index):
             rows = pl.ds(index * block, block)
@@ -108,13 +117,15 @@
                 )
             ]
             for branch, spread in enumerate(DILATIONS):
+                if index == 0:
+                    weight_copy(branch).wait()
                 total = None
                 for vertical in range(3):
                     for lateral in range(3):
                         shift = (vertical - 1) * spread * pitch + (lateral - 1) * spread
                         term = lax.dot_general(
                             window(shift),
-                            dilated_ref[branch, 3 * vertical + lateral, :, lanes],
+                            weight_ref[branch, 3 * vertical + lateral],
                             contract,
                             preferred_element_type=jnp.float32,
                         )
@@ -146,15 +157,20 @@
     sums_shape = (branches, blocks * block, width)
     vmem = pl.BlockSpec(memory_space=pltpu.VMEM)
     hbm = pl.BlockSpec(memory_space=pl.ANY)
-    scratch = [pltpu.VMEM(sums_shape, jnp.float32), pltpu.SemaphoreType.DMA((blocks,))]
+    scratch = [
+        pltpu.VMEM(sums_shape, jnp.float32),
+        pltpu.SemaphoreType.DMA((blocks,)),
+        pltpu.VMEM(aspp_dilated.shape[:3] + (channels,), aspp_dilated.dtype),
+        pltpu.SemaphoreType.DMA((len(DILATIONS),)),
+    ]
     if finish:
         flops += 2 * blocks * block * branches * width * width
         out_shape = jax.ShapeDtypeStruct((blocks * block, width), jnp.float32)
-        in_specs = [vmem, vmem, vmem, hbm, vmem, vmem, vmem]
+        in_specs = [vmem, vmem, hbm, hbm, vmem, vmem, vmem]
         out_specs = vmem
     else:
         out_shape = jax.ShapeDtypeStruct(sums_shape, jnp.float32)
-        in_specs = [vmem, vmem, vmem]
+        in_specs = [vmem, vmem, hbm]
         out_specs = hbm
     return pl.pallas_call(
         body,

time: 94.7 us -> 95.5 us (level)
  transfers between devices with their start and end apart: 10 -> 10, of which waited for: 6 -> 6; matrix products, arithmetic and copies ran while one was open for 14% -> 14% of each run, Pallas kernels for 16% -> 17%
where the time goes in v6:
time: 95.5 us; the launch traced here: 94.9 us
  Pallas kernels  44.8 us (47%)
  other arithmetic  17.4 us (18%)
  waiting for transfers between devices  13.6 us (14%)
  starting transfers between devices  7.73 us (8%)
  matrix products  4.49 us (5%)
  between operations  3.5 us (4%)
  local copies, waits for them, and re-layouts  3.42 us (4%)
    pallas_call x2, Pallas kernels, aspp_pass(): pl.pallas_call(body, out_shape=out_shape, in_specs=in_specs, out_specs=ou...  36.8 us
    ppermute x6, waiting for transfers between devices, all_sum(): other = lax.ppermute(value, axis, pairs)  12.4 us
    pallas_call x1, Pallas kernels, head_kernel_call(): pl.pallas_call(body, out_shape=jax.ShapeDtypeStruct((blocks * block, outp...  8 us
    ppermute x1, starting transfers between devices, shifted(): return lax.ppermute(value, axis, pairs)  6.09 us
    reshape x2, other arithmetic, flat_of(): return jnp.pad(jnp.transpose(wide, (1, 2, 0)).astype(jnp.float32), ((1, 1...  5.85 us
    select_n x3, other arithmetic, with_rims(): jnp.where(first, lax.slice_in_dim(block, size - width, None, axis=dim), l...  2.24 us
    dot_general x1, matrix products, shards(): jnp.einsum('sk,khw->shw', inst_stats, onehot, precision=lax.Precision.HIG...  2.23 us
    another operation x1, other arithmetic, shards(): jnp.stack([center_err, offset_err, counted_local])  2 us
  transfers between devices with their start and end apart: 10, of which 6 were waited for; matrix products, arithmetic and copies ran while one was open for 14% of the time, Pallas kernels for 17%

profile of v6, /device:TPU:0, one launch (start us, length us, event | category | flops | bytes accessed | tf_op | source)
XLA Modules:
  0.0 94.9 jit_solution(13116844549637970905)
XLA Ops:
  0.7 6.1 %collective-permute-start = (bf16[256,32,48]{0,2,1:T(8,128)(2,1)}, bf16[256,32,48]{0,2,1:T(8,128)(2,1)S(1)}, u32[]{:S(2)}, u32[]{:S(2)}) collective-permute-start(bf16[256,32,48]{0,2,1:T(8,128)(2,1)} %bitcast.75), channel_id=1, source_target_pairs={{0,14},{2,0},{4,2},{6,4},{8,6},{10,8},{12,10},{14,12},{1,15},{3,1}... | collective-permute-start | bytes 2359304 | tf_op jit(solution)/shard_map/ppermute | solution.py:51
  6.7 1.2 %slice_select_fusion = bf16[256,18,48]{0,2,1:T(8,128)(2,1)S(1)} fusion(bf16[256,32,48]{0,2,1:T(8,128)(2,1)} %bitcast.76, pred[]{:T(512)S(6)} %eq.28), kind=kLoop, calls=%fused_computation.19 | loop fusion | flops 221184 | bytes 1327105 | tf_op jit(solution)/shard_map/jit(_where)/select_n | solution.py:36
  8.0 0.7 and_bitcast_fusion
  8.8 1.3 %convert_reduce_fusion.2 = (f32[64]{0:T(128)S(1)}, f32[64]{0:T(128)S(1)}, f32[64]{0:T(128)S(1)}) fusion(s32[32,48]{1,0:T(8,128)} %bitcast.81, pred[32,48]{1,0:T(8,128)(4,1)S(1)} %get-tuple-element.10, f32[32]{0:T(128)S(1)} %add_convert_fusion), kind=kLoop, calls=%fused_computation.14 | loop fusion | flops 786240 | bytes 8576 | tf_op jit(solution)/shard_map/reduce_sum | solution.py:300
  10.7 0.9 fusion.10.rest_3_
  11.5 1.2 %dynamic_slice.4 = s32[1]{0:T(128)} dynamic-slice(s32[8]{0:T(128)} %param.11, s32[]{:T(128)S(6)} %select_n.89), dynamic_slice_sizes={1} | dynamic-slice | bytes 12 | tf_op jit(solution)/shard_map/jit(dynamic_index_in_dim)/dynamic_slice | solution.py:263
  13.4 2.2 %fusion.2 = f32[3,32,48]{2,0,1:T(4,128)S(1)} fusion(s32[32,48]{1,0:T(8,128)} %bitcast.82, pred[32,48]{1,0:T(8,128)(4,1)S(1)} %get-tuple-element.10, f32[3,64]{1,0:T(4,128)S(1)} %collective-permute-done.5, f32[1,64]{1,0:T(1,128)S(1)} %bitcast.92, f32[1,64]{1,0:T(1,128)S(1)} %bitcast.94, f32[1,64]{1,0:T(1,128)S(1)} %bitcast.90), kind=kOutput, calls=%fused_computation.17 | convolution fusion | flops 3736128 | bytes 27648 | tf_op jit(solution)/shard_map/sk,khw->shw/dot_general | solution.py:336
  16.1 2.9 %bitcast_convert_fusion.x_ref = f32[5040,256]{1,0:T(8,128)} fusion(bf16[70,72,256]{2,1,0:T(8,128)(2,1)S(1)} %pad.14), kind=kLoop, calls=%fused_computation.5 | loop fusion | flops 1290240 | bytes 7741440 | tf_op jit(solution)/shard_map/reshape | solution.py:282
  19.1 16.0 %shard_map.113.rest_0_ = f32[4,2304,256]{2,1,0:T(8,128)} custom-call(f32[5040,256]{1,0:T(8,128)} %bitcast_convert_fusion.x_ref, bf16[256,512]{1,0:T(8,128)(2,1)} %point_ref.3, bf16[3,9,256,512]{3,2,1,0:T(8,128)(2,1)} %dilated_ref.3), custom_call_target="tpu_custom_call" | custom-call | flops 8455716864 | bytes 18137088 | tf_op jit(solution)/shard_map/pallas_call | solution.py:175
  37.0 1.7 %fusion.16.rest_2_ = f32[1,256]{1,0:T(1,128)} fusion(bf16[256,1]{0,1:T(2,128)(2,1)S(1)} %reshape.81, bf16[256,1280]{1,0:T(8,128)(2,1)} %rest_1_.1), kind=kOutput, calls=%fused_computation.40 | convolution fusion | flops 131072 | bytes 132608 | tf_op jit(solution)/shard_map/dot_general | solution.py:313
  39.1 2.9 %bitcast_convert_fusion.1.x_ref = f32[5040,256]{1,0:T(8,128)} fusion(bf16[70,72,256]{2,1,0:T(8,128)(2,1)S(1)} %pad.13), kind=kLoop, calls=%fused_computation.6 | loop fusion | flops 1290240 | bytes 7741440 | tf_op jit(solution)/shard_map/reshape | solution.py:282
  42.0 20.8 %shard_map.114 = f32[2304,256]{1,0:T(8,128)} custom-call(f32[5040,256]{1,0:T(8,128)} %bitcast_convert_fusion.1.x_ref, bf16[256,512]{1,0:T(8,128)(2,1)} %point_ref.3, bf16[3,9,256,512]{3,2,1,0:T(8,128)(2,1)} %dilated_ref.3, f32[4,2304,256]{2,1,0:T(8,128)} %shard_map.113.rest_0_, bf16[256,1280]{1,0:T(8,128)(2,1)} %rest_1_.1, f32[1,256]{1,0:T(1,128)} %fusion.16.rest_2_, ...), custom_call_target="tpu_custom_call" | custom-call | flops 9663676416 | bytes 18137088 | tf_op jit(solution)/shard_map/pallas_call | solution.py:175
  62.8 1.0 %slice_select_fusion.2 = f32[144,256]{1,0:T(8,128)S(1)} fusion(f32[2304,256]{1,0:T(8,128)} %shard_map.114, pred[]{:T(512)S(6)} %eq.28), kind=kLoop, calls=%fused_computation.39 | loop fusion | flops 36864 | bytes 442369 | tf_op jit(solution)/shard_map/jit(_where)/select_n | solution.py:36
  64.1 1.2 %collective-permute-done.4 = f32[144,256]{1,0:T(8,128)S(1)} collective-permute-done((f32[144,256]{1,0:T(8,128)S(1)}, f32[144,256]{1,0:T(8,128)S(1)}, u32[]{:S(2)}, u32[]{:S(2)}) %collective-permute-start.4) | collective-permute-done | bytes 147488 | tf_op jit(solution)/shard_map/ppermute | solution.py:41
  65.3 1.9 %select_maximum_fusion.x_ref = f32[2736,256]{1,0:T(8,128)S(1)} fusion(f32[144,256]{1,0:T(8,128)S(1)} %get-tuple-element.20, f32[2304,256]{1,0:T(8,128)} %shard_map.114, f32[144,256]{1,0:T(8,128)S(1)} %get-tuple-element.19), kind=kLoop, calls=%fused_computation.2 | loop fusion | flops 5603328 | bytes 5455872 | tf_op jit(solution)/shard_map/concatenate | solution.py:45
  67.3 8.0 %shard_map.115 = bf16[2304,96]{1,0:T(8,128)(2,1)S(1)} custom-call(f32[2736,256]{1,0:T(8,128)S(1)} %select_maximum_fusion.x_ref, bf16[25,96,256]{2,1,0:T(8,128)(2,1)S(1)} %copy-done.1), custom_call_target="tpu_custom_call" | custom-call | flops 2831155200 | bytes 4472832 | tf_op jit(solution)/shard_map/pallas_call | solution.py:214
  76.2 0.7 multiply_reduce_fusion
  76.9 2.0 %pad_maximum_fusion.2 = f32[3]{0:T(128)S(1)} fusion(f32[1]{0:T(128)} %bitcast.37, f32[1]{0:T(128)} %bitcast.36, f32[1]{0:T(128)} %bitcast.33), kind=kLoop, calls=%fused_computation.59 | loop fusion | flops 6 | bytes 24 | tf_op jit(solution)/shard_map/stack | solution.py:354
  79.2 0.6 copy.18
  80.1 3.6 %collective-permute-done.7 = f32[3]{0:T(128)S(1)} collective-permute-done((f32[3]{0:T(128)S(1)}, f32[3]{0:T(128)S(1)}, u32[]{:S(2)}, u32[]{:S(2)}) %collective-permute-start.7) | collective-permute-done | bytes 44 | tf_op jit(solution)/shard_map/ppermute | solution.py:63
  83.7 3.6 %collective-permute-done.8 = f32[3]{0:T(128)S(1)} collective-permute-done((f32[3]{0:T(128)S(1)}, f32[3]{0:T(128)S(1)}, u32[]{:S(2)}, u32[]{:S(2)}) %collective-permute-start.8) | collective-permute-done | bytes 44 | tf_op jit(solution)/shard_map/ppermute | solution.py:63
  87.3 4.5 %collective-permute-done.9 = f32[3]{0:T(128)S(1)} collective-permute-done((f32[3]{0:T(128)S(1)}, f32[3]{0:T(128)S(1)}, u32[]{:S(2)}, u32[]{:S(2)}) %collective-permute-start.9) | collective-permute-done | bytes 44 | tf_op jit(solution)/shard_map/ppermute | solution.py:63
  91.7 0.7 fusion.28
  94.3 0.6 pad_maximum_fusion.3
  (54 shorter events, 5.1 us)
Async XLA Ops:
  0.6 36.1 %copy-start = (bf16[256,512]{1,0:T(8,128)(2,1)S(1)}, bf16[256,512]{1,0:T(8,128)(2,1)}, u32[]{:S(2)}) copy-start(bf16[256,512]{1,0:T(8,128)(2,1)} %param.16) | copy-start | bytes 786436
  0.6 15.1 %copy-start.2 = (bf16[1,256,32,48]{1,3,2,0:T(8,128)(2,1)S(1)}, bf16[1,256,32,48]{1,3,2,0:T(8,128)(2,1)}, u32[]{:S(2)}) copy-start(bf16[1,256,32,48]{1,3,2,0:T(8,128)(2,1)} %param.10) | copy-start | bytes 2359300
  0.7 34.4 %collective-permute-start = (bf16[256,32,48]{0,2,1:T(8,128)(2,1)}, bf16[256,32,48]{0,2,1:T(8,128)(2,1)S(1)}, u32[]{:S(2)}, u32[]{:S(2)}) collective-permute-start(bf16[256,32,48]{0,2,1:T(8,128)(2,1)} %bitcast.75), channel_id=1, source_target_pairs={{0,14},{2,0},{4,2},{6,4},{8,6},{10,8},{12,10},{14,12},{1,15},{3,1}... | collective-permute-start | bytes 2359304 | tf_op jit(solution)/shard_map/ppermute | solution.py:51
  7.9 7.7 %collective-permute-start.2 = (bf16[256,18,48]{0,2,1:T(8,128)(2,1)S(1)}, bf16[256,18,48]{0,2,1:T(8,128)(2,1)S(1)}, u32[]{:S(2)}, u32[]{:S(2)}) collective-permute-start(bf16[256,18,48]{0,2,1:T(8,128)(2,1)S(1)} %slice_select_fusion), channel_id=1, source_target_pairs={{0,1},{1,0},{2,3},{3,2},{4,5},{5,4},{6,7},{7,6},{8,9},{9,8},{10,11... | collective-permute-start | bytes 1327112 | tf_op jit(solution)/shard_map/ppermute | solution.py:41
  10.1 3.3 %collective-permute-start.5 = (f32[3,64]{1,0:T(4,128)S(1)}, f32[3,64]{1,0:T(4,128)S(1)}, u32[]{:S(2)}, u32[]{:S(2)}) collective-permute-start(f32[3,64]{1,0:T(4,128)S(1)} %pad_maximum_fusion.1), channel_id=1, source_target_pairs={{0,1},{1,0},{2,3},{3,2},{4,5},{5,4},{6,7},{7,6},{8,9},{9,8},{10,11... | collective-permute-start | bytes 2312 | tf_op jit(solution)/shard_map/ppermute | solution.py:63
  35.5 1.2 %collective-permute-start.3 = (f32[512]{0:T(512)S(1)}, f32[512]{0:T(512)S(1)}, u32[]{:S(2)}, u32[]{:S(2)}) collective-permute-start(f32[512]{0:T(512)S(1)} %pad_maximum_fusion), channel_id=1, source_target_pairs={{0,1},{1,0},{2,3},{3,2},{4,5},{5,4},{6,7},{7,6},{8,9},{9,8},{10,11... | collective-permute-start | bytes 6152 | tf_op jit(solution)/shard_map/ppermute | solution.py:63
  35.7 3.0 %collective-permute-start.1 = (bf16[256,18,48]{0,2,1:T(8,128)(2,1)S(1)}, bf16[256,18,48]{0,2,1:T(8,128)(2,1)S(1)}, u32[]{:S(2)}, u32[]{:S(2)}) collective-permute-start(bf16[256,18,48]{0,2,1:T(8,128)(2,1)S(1)} %slice_select_fusion.1), channel_id=1, source_target_pairs={{0,1},{1,0},{2,3},{3,2},{4,5},{5,4},{6,7},{7,6},{8,9},{9,8},{10,11... | collective-permute-start | bytes 1327112 | tf_op jit(solution)/shard_map/ppermute | solution.py:41
  63.8 1.4 %collective-permute-start.4 = (f32[144,256]{1,0:T(8,128)S(1)}, f32[144,256]{1,0:T(8,128)S(1)}, u32[]{:S(2)}, u32[]{:S(2)}) collective-permute-start(f32[144,256]{1,0:T(8,128)S(1)} %slice_select_fusion.2), channel_id=1, source_target_pairs={{0,1},{1,0},{2,3},{3,2},{4,5},{5,4},{6,7},{7,6},{8,9},{9,8},{10,11... | collective-permute-start | bytes 442376 | tf_op jit(solution)/shard_map/ppermute | solution.py:41
  65.3 2.0 %copy-start.1 = (bf16[25,96,256]{2,1,0:T(8,128)(2,1)S(1)}, bf16[25,96,256]{2,1,0:T(8,128)(2,1)}, u32[]{:S(2)}) copy-start(bf16[25,96,256]{2,1,0:T(8,128)(2,1)} %weight_ref.1) | copy-start | bytes 3686404
  67.3 8.4 %copy-start.4 = (bf16[4,32]{1,0:T(4,128)(2,1)S(1)}, bf16[4,32]{1,0:T(4,128)(2,1)}, u32[]{:S(2)}) copy-start(bf16[4,32]{1,0:T(4,128)(2,1)} %param.19) | copy-start | bytes 772
  75.3 0.9 copy-start.3
  78.9 1.2 %collective-permute-start.6 = (f32[3]{0:T(128)S(1)}, f32[3]{0:T(128)S(1)}, u32[]{:S(2)}, u32[]{:S(2)}) collective-permute-start(f32[3]{0:T(128)S(1)} %pad_maximum_fusion.2), channel_id=1, source_target_pairs={{0,1},{1,0},{2,3},{3,2},{4,5},{5,4},{6,7},{7,6},{8,9},{9,8},{10,11... | collective-permute-start | bytes 44 | tf_op jit(solution)/shard_map/ppermute | solution.py:63
  80.1 3.6 %collective-permute-start.7 = (f32[3]{0:T(128)S(1)}, f32[3]{0:T(128)S(1)}, u32[]{:S(2)}, u32[]{:S(2)}) collective-permute-start(f32[3]{0:T(128)S(1)} %add.74), channel_id=1, source_target_pairs={{0,2},{2,0},{4,6},{6,4},{8,10},{10,8},{12,14},{14,12},{1,3},{3,1},... | collective-permute-start | bytes 44 | tf_op jit(solution)/shard_map/ppermute | solution.py:63
  83.7 3.6 %collective-permute-start.8 = (f32[3]{0:T(128)S(1)}, f32[3]{0:T(128)S(1)}, u32[]{:S(2)}, u32[]{:S(2)}) collective-permute-start(f32[3]{0:T(128)S(1)} %add.75), channel_id=1, source_target_pairs={{0,4},{2,6},{4,0},{6,2},{8,12},{10,14},{12,8},{14,10},{1,5},{3,7},... | collective-permute-start | bytes 44 | tf_op jit(solution)/shard_map/ppermute | solution.py:63
  87.3 4.5 %collective-permute-start.9 = (f32[3]{0:T(128)S(1)}, f32[3]{0:T(128)S(1)}, u32[]{:S(2)}, u32[]{:S(2)}) collective-permute-start(f32[3]{0:T(128)S(1)} %add.76), channel_id=1, source_target_pairs={{0,8},{2,10},{4,12},{6,14},{8,0},{10,2},{12,4},{14,6},{1,9},{3,11}... | collective-permute-start | bytes 44 | tf_op jit(solution)/shard_map/ppermute | solution.py:63

commit v7 on v5

--- a/solution.py
+++ b/solution.py
@@ -66,7 +66,7 @@
     return value
 
 
-def aspp_pass(x, aspp_point, aspp_dilated, extra, geometry, part, finish):
+def aspp_pass(x, aspp_point, aspp_dilated, extra, geometry, part, finish, lead=0):
     front, pitch, margin, block, blocks = geometry
     width = aspp_point.shape[0]
     channels = x.shape[1]
@@ -136,7 +136,13 @@
                 mixed = term if mixed is None else mixed + term
             mixed = mixed + pool_ref[...]
             rounded = relu_bf16(mixed).astype(jnp.float32)
-            out_ref[rows, :] = jnp.where(keep_ref[...] > 0.5, rounded, 0.0)
+            out_ref[pl.ds(lead + index * block, block), :] = jnp.where(
+                keep_ref[...] > 0.5, rounded, 0.0
+            )
+        if finish:
+            zeros = jnp.zeros((lead, width), jnp.float32)
+            out_ref[pl.ds(0, lead), :] = zeros
+            out_ref[pl.ds(lead + blocks * block, lead), :] = zeros
         if not finish:
             for index in range(blocks):
                 block_copy(index).wait()
@@ -149,7 +155,7 @@
     scratch = [pltpu.VMEM(sums_shape, jnp.float32), pltpu.SemaphoreType.DMA((blocks,))]
     if finish:
         flops += 2 * blocks * block * branches * width * width
-        out_shape = jax.ShapeDtypeStruct((blocks * block, width), jnp.float32)
+        out_shape = jax.ShapeDtypeStruct((blocks * block + 2 * lead, width), jnp.float32)
         in_specs = [vmem, vmem, vmem, hbm, vmem, vmem, vmem]
         out_specs = vmem
     else:
@@ -307,11 +313,16 @@
         geometry,
         1,
         True,
+        lead=(1 + 2) * pitch,
     )
     head_reach = 2
-    head_in = jnp.pad(
-        with_rims(projected_flat, "row", 0, head_reach * pitch), ((pitch, pitch), (0, 0))
-    )
+    rim = head_reach * pitch
+    lead = pitch + rim
+    band_flat = lax.slice_in_dim(projected_flat, lead, lead + blocks * block, axis=0)
+    edges = jnp.concatenate([band_flat[:rim], band_flat[-rim:]], 0)
+    rimmed = with_rims(edges, "row", 0, rim)
+    head_in = lax.dynamic_update_slice(projected_flat, rimmed[:rim], (pitch, 0))
+    head_in = lax.dynamic_update_slice(head_in, rimmed[-rim:], (lead + blocks * block, 0))
     head_flat = head_kernel_call(head_in, head_weight, (pitch, pitch, head_reach, block, blocks))
     head_out = jnp.transpose(
         head_flat.reshape(band_rows, pitch, head_weight.shape[1])[:, pad_columns:], (2, 0, 1)

time: 94.7 us -> 96 us (1.014)
  local copies, waits for them, and re-layouts: 3.42 us -> 5.17 us
    concatenate x1 -> x0, other arithmetic: 1.95 us -> none  [with_rims(): return jnp.concatenate([low, block, high], axis=dim)]
    unnamed x12 -> x14, local copies, waits for them, and re-layouts: 1.06 us -> 2.81 us
    dynamic_update_slice x0 -> x2, other arithmetic: none -> 1.34 us  [the longest x1 0.67 us: shards(): head_in = lax.dynamic_update_slice(projected_flat, rimmed[:rim], (pitch, 0))]
where the time goes in v7:
time: 96 us; the launch traced here: 95.5 us
  Pallas kernels  44.2 us (46%)
  other arithmetic  16.7 us (17%)
  waiting for transfers between devices  13.6 us (14%)
  starting transfers between devices  7.73 us (8%)
  local copies, waits for them, and re-layouts  5.17 us (5%)
  matrix products  4.48 us (5%)
  between operations  3.48 us (4%)
    pallas_call x2, Pallas kernels, aspp_pass(): pl.pallas_call(body, out_shape=out_shape, in_specs=in_specs, out_specs=ou...  36.2 us
    ppermute x6, waiting for transfers between devices, all_sum(): other = lax.ppermute(value, axis, pairs)  12.4 us
    pallas_call x1, Pallas kernels, head_kernel_call(): pl.pallas_call(body, out_shape=jax.ShapeDtypeStruct((blocks * block, outp...  7.99 us
    ppermute x1, starting transfers between devices, shifted(): return lax.ppermute(value, axis, pairs)  6.09 us
    reshape x2, other arithmetic, flat_of(): return jnp.pad(jnp.transpose(wide, (1, 2, 0)).astype(jnp.float32), ((1, 1...  5.85 us
    unnamed x14, local copies, waits for them, and re-layouts  2.81 us
    select_n x3, other arithmetic, with_rims(): jnp.where(first, lax.slice_in_dim(block, size - width, None, axis=dim), l...  2.24 us
    dot_general x1, matrix products, shards(): jnp.einsum('sk,khw->shw', inst_stats, onehot, precision=lax.Precision.HIG...  2.23 us
  transfers between devices with their start and end apart: 10, of which 6 were waited for; matrix products, arithmetic and copies ran while one was open for 14% of the time, Pallas kernels for 16%

profile of v7, /device:TPU:0, one launch (start us, length us, event | category | flops | bytes accessed | tf_op | source)
XLA Modules:
  0.0 95.5 jit_solution(5896273645183678226)
XLA Ops:
  0.7 6.1 %collective-permute-start = (bf16[256,32,48]{0,2,1:T(8,128)(2,1)}, bf16[256,32,48]{0,2,1:T(8,128)(2,1)S(1)}, u32[]{:S(2)}, u32[]{:S(2)}) collective-permute-start(bf16[256,32,48]{0,2,1:T(8,128)(2,1)} %bitcast.75), channel_id=1, source_target_pairs={{0,14},{2,0},{4,2},{6,4},{8,6},{10,8},{12,10},{14,12},{1,15},{3,1}... | collective-permute-start | bytes 2359304 | tf_op jit(solution)/shard_map/ppermute | solution.py:51
  6.7 1.2 %slice_select_fusion = bf16[256,18,48]{0,2,1:T(8,128)(2,1)S(1)} fusion(bf16[256,32,48]{0,2,1:T(8,128)(2,1)} %bitcast.76, pred[]{:T(512)S(6)} %eq.28), kind=kLoop, calls=%fused_computation.14 | loop fusion | flops 221184 | bytes 1327105 | tf_op jit(solution)/shard_map/jit(_where)/select_n | solution.py:36
  8.0 0.7 and_bitcast_fusion
  8.8 1.3 %convert_reduce_fusion.2 = (f32[64]{0:T(128)S(1)}, f32[64]{0:T(128)S(1)}, f32[64]{0:T(128)S(1)}) fusion(s32[32,48]{1,0:T(8,128)} %bitcast.81, pred[32,48]{1,0:T(8,128)(4,1)S(1)} %get-tuple-element.10, f32[32]{0:T(128)S(1)} %add_convert_fusion), kind=kLoop, calls=%fused_computation.9 | loop fusion | flops 786240 | bytes 8576 | tf_op jit(solution)/shard_map/reduce_sum | solution.py:290
  10.7 0.8 fusion.9.rest_3_
  11.5 1.2 %dynamic_slice.4 = s32[1]{0:T(128)} dynamic-slice(s32[8]{0:T(128)} %param.11, s32[]{:T(128)S(6)} %select_n.88), dynamic_slice_sizes={1} | dynamic-slice | bytes 12 | tf_op jit(solution)/shard_map/jit(dynamic_index_in_dim)/dynamic_slice | solution.py:253
  13.4 2.2 %fusion.1 = f32[3,32,48]{2,0,1:T(4,128)S(1)} fusion(s32[32,48]{1,0:T(8,128)} %bitcast.82, pred[32,48]{1,0:T(8,128)(4,1)S(1)} %get-tuple-element.10, f32[3,64]{1,0:T(4,128)S(1)} %collective-permute-done.5, f32[1,64]{1,0:T(1,128)S(1)} %bitcast.92, f32[1,64]{1,0:T(1,128)S(1)} %bitcast.94, f32[1,64]{1,0:T(1,128)S(1)} %bitcast.90), kind=kOutput, calls=%fused_computation.12 | convolution fusion | flops 3736128 | bytes 27648 | tf_op jit(solution)/shard_map/sk,khw->shw/dot_general | solution.py:331
  16.1 2.9 %bitcast_convert_fusion.x_ref = f32[5040,256]{1,0:T(8,128)} fusion(bf16[70,72,256]{2,1,0:T(8,128)(2,1)S(1)} %pad.10), kind=kLoop, calls=%fused_computation | loop fusion | flops 1290240 | bytes 7741440 | tf_op jit(solution)/shard_map/reshape | solution.py:272
  19.0 15.1 %shard_map.113.rest_0_ = f32[4,2304,256]{2,1,0:T(8,128)} custom-call(f32[5040,256]{1,0:T(8,128)} %bitcast_convert_fusion.x_ref, bf16[256,512]{1,0:T(8,128)(2,1)} %point_ref.3, bf16[3,9,256,512]{3,2,1,0:T(8,128)(2,1)} %dilated_ref.3), custom_call_target="tpu_custom_call" | custom-call | flops 8455716864 | bytes 18137088 | tf_op jit(solution)/shard_map/pallas_call | solution.py:165
  36.0 1.7 %fusion.15.rest_2_ = f32[1,256]{1,0:T(1,128)} fusion(bf16[256,1]{0,1:T(2,128)(2,1)S(1)} %reshape.81, bf16[256,1280]{1,0:T(8,128)(2,1)} %rest_1_.1), kind=kOutput, calls=%fused_computation.37 | convolution fusion | flops 131072 | bytes 132608 | tf_op jit(solution)/shard_map/dot_general | solution.py:303
  38.1 2.9 %bitcast_convert_fusion.1.x_ref = f32[5040,256]{1,0:T(8,128)} fusion(bf16[70,72,256]{2,1,0:T(8,128)(2,1)S(1)} %pad.9), kind=kLoop, calls=%fused_computation.1 | loop fusion | flops 1290240 | bytes 7741440 | tf_op jit(solution)/shard_map/reshape | solution.py:272
  41.0 21.2 %shard_map.114 = f32[2736,256]{1,0:T(8,128)} custom-call(f32[5040,256]{1,0:T(8,128)} %bitcast_convert_fusion.1.x_ref, bf16[256,512]{1,0:T(8,128)(2,1)} %point_ref.3, bf16[3,9,256,512]{3,2,1,0:T(8,128)(2,1)} %dilated_ref.3, f32[4,2304,256]{2,1,0:T(8,128)} %shard_map.113.rest_0_, bf16[256,1280]{1,0:T(8,128)(2,1)} %rest_1_.1, f32[1,256]{1,0:T(1,128)} %fusion.15.rest_2_, ...), custom_call_target="tpu_custom_call" | custom-call | flops 9663676416 | bytes 18137088 | tf_op jit(solution)/shard_map/pallas_call | solution.py:165
  62.2 1.0 %slice_select_fusion.2 = f32[144,256]{1,0:T(8,128)S(1)} fusion(f32[2736,256]{1,0:T(8,128)} %shard_map.114, pred[]{:T(512)S(6)} %eq.28), kind=kLoop, calls=%fused_computation.34 | loop fusion | flops 36864 | bytes 442369 | tf_op jit(solution)/shard_map/jit(_where)/select_n | solution.py:36
  63.5 1.2 %collective-permute-done.4 = f32[144,256]{1,0:T(8,128)S(1)} collective-permute-done((f32[144,256]{1,0:T(8,128)S(1)}, f32[144,256]{1,0:T(8,128)S(1)}, u32[]{:S(2)}, u32[]{:S(2)}) %collective-permute-start.4) | collective-permute-done | bytes 147488 | tf_op jit(solution)/shard_map/ppermute | solution.py:41
  64.7 0.7 select_dynamic-update-slice_fusion.1
  65.4 0.7 select_dynamic-update-slice_fusion.x_ref
  66.0 1.8 %copy-done.1 = f32[2736,256]{1,0:T(8,128)S(1)} copy-done((f32[2736,256]{1,0:T(8,128)S(1)}, f32[2736,256]{1,0:T(8,128)}, u32[]{:S(2)}) %copy-start.1) | copy-done | bytes 2801688
  67.8 8.0 %shard_map.115 = bf16[2304,96]{1,0:T(8,128)(2,1)S(1)} custom-call(f32[2736,256]{1,0:T(8,128)S(1)} %copy-done.1, bf16[25,96,256]{2,1,0:T(8,128)(2,1)S(1)} %copy-done.2), custom_call_target="tpu_custom_call" | custom-call | flops 2831155200 | bytes 4472832 | tf_op jit(solution)/shard_map/pallas_call | solution.py:204
  76.7 0.7 multiply_reduce_fusion
  77.5 2.0 %pad_maximum_fusion.2 = f32[3]{0:T(128)S(1)} fusion(f32[1]{0:T(128)} %bitcast.37, f32[1]{0:T(128)} %bitcast.36, f32[1]{0:T(128)} %bitcast.33), kind=kLoop, calls=%fused_computation.54 | loop fusion | flops 6 | bytes 24 | tf_op jit(solution)/shard_map/stack | solution.py:349
  80.6 3.6 %collective-permute-done.7 = f32[3]{0:T(128)S(1)} collective-permute-done((f32[3]{0:T(128)S(1)}, f32[3]{0:T(128)S(1)}, u32[]{:S(2)}, u32[]{:S(2)}) %collective-permute-start.7) | collective-permute-done | bytes 44 | tf_op jit(solution)/shard_map/ppermute | solution.py:63
  84.2 3.6 %collective-permute-done.8 = f32[3]{0:T(128)S(1)} collective-permute-done((f32[3]{0:T(128)S(1)}, f32[3]{0:T(128)S(1)}, u32[]{:S(2)}, u32[]{:S(2)}) %collective-permute-start.8) | collective-permute-done | bytes 44 | tf_op jit(solution)/shard_map/ppermute | solution.py:63
  87.8 4.5 %collective-permute-done.9 = f32[3]{0:T(128)S(1)} collective-permute-done((f32[3]{0:T(128)S(1)}, f32[3]{0:T(128)S(1)}, u32[]{:S(2)}, u32[]{:S(2)}) %collective-permute-start.9) | collective-permute-done | bytes 44 | tf_op jit(solution)/shard_map/ppermute | solution.py:63
  92.3 0.7 fusion.27
  (56 shorter events, 6.3 us)
Async XLA Ops:
  0.6 35.2 %copy-start = (bf16[256,512]{1,0:T(8,128)(2,1)S(1)}, bf16[256,512]{1,0:T(8,128)(2,1)}, u32[]{:S(2)}) copy-start(bf16[256,512]{1,0:T(8,128)(2,1)} %param.16) | copy-start | bytes 786436
  0.6 15.1 %copy-start.3 = (bf16[1,256,32,48]{1,3,2,0:T(8,128)(2,1)S(1)}, bf16[1,256,32,48]{1,3,2,0:T(8,128)(2,1)}, u32[]{:S(2)}) copy-start(bf16[1,256,32,48]{1,3,2,0:T(8,128)(2,1)} %param.10) | copy-start | bytes 2359300
  0.7 33.5 %collective-permute-start = (bf16[256,32,48]{0,2,1:T(8,128)(2,1)}, bf16[256,32,48]{0,2,1:T(8,128)(2,1)S(1)}, u32[]{:S(2)}, u32[]{:S(2)}) collective-permute-start(bf16[256,32,48]{0,2,1:T(8,128)(2,1)} %bitcast.75), channel_id=1, source_target_pairs={{0,14},{2,0},{4,2},{6,4},{8,6},{10,8},{12,10},{14,12},{1,15},{3,1}... | collective-permute-start | bytes 2359304 | tf_op jit(solution)/shard_map/ppermute | solution.py:51
  7.9 7.7 %collective-permute-start.2 = (bf16[256,18,48]{0,2,1:T(8,128)(2,1)S(1)}, bf16[256,18,48]{0,2,1:T(8,128)(2,1)S(1)}, u32[]{:S(2)}, u32[]{:S(2)}) collective-permute-start(bf16[256,18,48]{0,2,1:T(8,128)(2,1)S(1)} %slice_select_fusion), channel_id=1, source_target_pairs={{0,1},{1,0},{2,3},{3,2},{4,5},{5,4},{6,7},{7,6},{8,9},{9,8},{10,11... | collective-permute-start | bytes 1327112 | tf_op jit(solution)/shard_map/ppermute | solution.py:41
  10.1 3.3 %collective-permute-start.5 = (f32[3,64]{1,0:T(4,128)S(1)}, f32[3,64]{1,0:T(4,128)S(1)}, u32[]{:S(2)}, u32[]{:S(2)}) collective-permute-start(f32[3,64]{1,0:T(4,128)S(1)} %pad_maximum_fusion.1), channel_id=1, source_target_pairs={{0,1},{1,0},{2,3},{3,2},{4,5},{5,4},{6,7},{7,6},{8,9},{9,8},{10,11... | collective-permute-start | bytes 2312 | tf_op jit(solution)/shard_map/ppermute | solution.py:63
  34.6 1.2 %collective-permute-start.3 = (f32[512]{0:T(512)S(1)}, f32[512]{0:T(512)S(1)}, u32[]{:S(2)}, u32[]{:S(2)}) collective-permute-start(f32[512]{0:T(512)S(1)} %pad_maximum_fusion), channel_id=1, source_target_pairs={{0,1},{1,0},{2,3},{3,2},{4,5},{5,4},{6,7},{7,6},{8,9},{9,8},{10,11... | collective-permute-start | bytes 6152 | tf_op jit(solution)/shard_map/ppermute | solution.py:63
  34.7 3.0 %collective-permute-start.1 = (bf16[256,18,48]{0,2,1:T(8,128)(2,1)S(1)}, bf16[256,18,48]{0,2,1:T(8,128)(2,1)S(1)}, u32[]{:S(2)}, u32[]{:S(2)}) collective-permute-start(bf16[256,18,48]{0,2,1:T(8,128)(2,1)S(1)} %slice_select_fusion.1), channel_id=1, source_target_pairs={{0,1},{1,0},{2,3},{3,2},{4,5},{5,4},{6,7},{7,6},{8,9},{9,8},{10,11... | collective-permute-start | bytes 1327112 | tf_op jit(solution)/shard_map/ppermute | solution.py:41
  41.0 25.0 %copy-start.2 = (bf16[25,96,256]{2,1,0:T(8,128)(2,1)S(1)}, bf16[25,96,256]{2,1,0:T(8,128)(2,1)}, u32[]{:S(2)}) copy-start(bf16[25,96,256]{2,1,0:T(8,128)(2,1)} %weight_ref.1) | copy-start | bytes 3686404
  63.2 1.4 %collective-permute-start.4 = (f32[144,256]{1,0:T(8,128)S(1)}, f32[144,256]{1,0:T(8,128)S(1)}, u32[]{:S(2)}, u32[]{:S(2)}) collective-permute-start(f32[144,256]{1,0:T(8,128)S(1)} %slice_select_fusion.2), channel_id=1, source_target_pairs={{0,1},{1,0},{2,3},{3,2},{4,5},{5,4},{6,7},{7,6},{8,9},{9,8},{10,11... | collective-permute-start | bytes 442376 | tf_op jit(solution)/shard_map/ppermute | solution.py:41
  66.0 1.8 %copy-start.1 = (f32[2736,256]{1,0:T(8,128)S(1)}, f32[2736,256]{1,0:T(8,128)}, u32[]{:S(2)}) copy-start(f32[2736,256]{1,0:T(8,128)} %select_dynamic-update-slice_fusion.x_ref) | copy-start | bytes 8404996
  67.8 8.4 %copy-start.5 = (bf16[4,32]{1,0:T(4,128)(2,1)S(1)}, bf16[4,32]{1,0:T(4,128)(2,1)}, u32[]{:S(2)}) copy-start(bf16[4,32]{1,0:T(4,128)(2,1)} %param.19) | copy-start | bytes 772
  75.8 0.9 copy-start.4
  79.5 1.2 %collective-permute-start.6 = (f32[3]{0:T(128)S(1)}, f32[3]{0:T(128)S(1)}, u32[]{:S(2)}, u32[]{:S(2)}) collective-permute-start(f32[3]{0:T(128)S(1)} %pad_maximum_fusion.2), channel_id=1, source_target_pairs={{0,1},{1,0},{2,3},{3,2},{4,5},{5,4},{6,7},{7,6},{8,9},{9,8},{10,11... | collective-permute-start | bytes 44 | tf_op jit(solution)/shard_map/ppermute | solution.py:63
  80.6 3.6 %collective-permute-start.7 = (f32[3]{0:T(128)S(1)}, f32[3]{0:T(128)S(1)}, u32[]{:S(2)}, u32[]{:S(2)}) collective-permute-start(f32[3]{0:T(128)S(1)} %add.72), channel_id=1, source_target_pairs={{0,2},{2,0},{4,6},{6,4},{8,10},{10,8},{12,14},{14,12},{1,3},{3,1},... | collective-permute-start | bytes 44 | tf_op jit(solution)/shard_map/ppermute | solution.py:63
  84.2 3.6 %collective-permute-start.8 = (f32[3]{0:T(128)S(1)}, f32[3]{0:T(128)S(1)}, u32[]{:S(2)}, u32[]{:S(2)}) collective-permute-start(f32[3]{0:T(128)S(1)} %add.73), channel_id=1, source_target_pairs={{0,4},{2,6},{4,0},{6,2},{8,12},{10,14},{12,8},{14,10},{1,5},{3,7},... | collective-permute-start | bytes 44 | tf_op jit(solution)/shard_map/ppermute | solution.py:63
  87.8 4.5 %collective-permute-start.9 = (f32[3]{0:T(128)S(1)}, f32[3]{0:T(128)S(1)}, u32[]{:S(2)}, u32[]{:S(2)}) collective-permute-start(f32[3]{0:T(128)S(1)} %add.74), channel_id=1, source_target_pairs={{0,8},{2,10},{4,12},{6,14},{8,0},{10,2},{12,4},{14,6},{1,9},{3,11}... | collective-permute-start | bytes 44 | tf_op jit(solution)/shard_map/ppermute | solution.py:63

commit v8 on v5

--- a/solution.py
+++ b/solution.py
@@ -100,7 +100,7 @@
                 block_copy(index).wait()
 
             def window(shift):
-                return x_ref[pl.ds(base + shift, block), :].astype(jnp.bfloat16)
+                return x_ref[pl.ds(base + shift, block), :]
 
             sums = [
                 lax.dot_general(
@@ -166,7 +166,7 @@
         cost_estimate=pl.CostEstimate(
             flops=flops,
             transcendentals=0,
-            bytes_accessed=x.size * 4
+            bytes_accessed=x.size * 2
             + aspp_dilated.size
             + branches * blocks * block * width * 4,
         ),
@@ -250,7 +250,7 @@
     extra_rows = aspp_reach - rim_rows
 
     wide_rows = band_rows + 2 * aspp_reach
-    pitch = -(-(columns + aspp_reach) // 8) * 8
+    pitch = -(-(columns + aspp_reach) // 16) * 16
     front = pitch
     block_rows = 8 if band_rows % 8 == 0 else band_rows
     block = block_rows * pitch
@@ -261,7 +261,7 @@
             with_rims(band, "row", 1, rim_rows), ((0, 0), (extra_rows, extra_rows), (0, 0))
         )
         return jnp.pad(
-            jnp.transpose(wide, (1, 2, 0)).astype(jnp.float32),
+            jnp.transpose(wide, (1, 2, 0)),
             ((1, 1), (pitch - columns, 0), (0, 0)),
         ).reshape((wide_rows + 2) * pitch, channel_count)
 

time: 94.7 us -> 94.2 us (level)
  other arithmetic: 17.4 us -> 11.6 us
  local copies, waits for them, and re-layouts: 3.42 us -> 6.74 us
  Pallas kernels: 44 us -> 45.9 us
    reshape x2 -> x0, other arithmetic: 5.85 us -> none  [flat_of(): return jnp.pad(jnp.transpose(wide, (1, 2, 0)).astype(jnp.float32), ((1, 1...]
    pad x2, local copies, waits for them, and re-layouts: 0.34 us -> 3.67 us  [flat_of(): jnp.pad(jnp.transpose(wide, (1, 2, 0)), ((1, 1), (pitch - columns, 0), (0...]
    pallas_call x2, Pallas kernels: 36 us -> 37.1 us  [aspp_pass(): pl.pallas_call(body, out_shape=out_shape, in_specs=in_specs, out_specs=ou...]
  transfers between devices with their start and end apart: 10 -> 10, of which waited for: 6 -> 6; matrix products, arithmetic and copies ran while one was open for 14% -> 13% of each run, Pallas kernels for 16% -> 16%
where the time goes in v8:
time: 94.2 us; the launch traced here: 93.7 us
  Pallas kernels  45.9 us (49%)
  waiting for transfers between devices  13.7 us (15%)
  other arithmetic  11.6 us (12%)
  starting transfers between devices  7.72 us (8%)
  local copies, waits for them, and re-layouts  6.74 us (7%)
  matrix products  4.49 us (5%)
  between operations  3.48 us (4%)
    pallas_call x2, Pallas kernels, aspp_pass(): pl.pallas_call(body, out_shape=out_shape, in_specs=in_specs, out_specs=ou...  37.1 us
    ppermute x6, waiting for transfers between devices, all_sum(): other = lax.ppermute(value, axis, pairs)  12.4 us
    pallas_call x1, Pallas kernels, head_kernel_call(): pl.pallas_call(body, out_shape=jax.ShapeDtypeStruct((blocks * block, outp...  8.83 us
    ppermute x1, starting transfers between devices, shifted(): return lax.ppermute(value, axis, pairs)  6.09 us
    pad x2, local copies, waits for them, and re-layouts, flat_of(): jnp.pad(jnp.transpose(wide, (1, 2, 0)), ((1, 1), (pitch - columns, 0), (0...  3.67 us
    select_n x3, other arithmetic, with_rims(): jnp.where(first, lax.slice_in_dim(block, size - width, None, axis=dim), l...  2.26 us
    dot_general x1, matrix products, shards(): jnp.einsum('sk,khw->shw', inst_stats, onehot, precision=lax.Precision.HIG...  2.23 us
    concatenate x1, other arithmetic, with_rims(): return jnp.concatenate([low, block, high], axis=dim)  2.04 us
  transfers between devices with their start and end apart: 10, of which 6 were waited for; matrix products, arithmetic and copies ran while one was open for 13% of the time, Pallas kernels for 16%

profile of v8, /device:TPU:0, one launch (start us, length us, event | category | flops | bytes accessed | tf_op | source)
XLA Modules:
  0.0 93.7 jit_solution(9080522148326626739)
XLA Ops:
  0.7 6.1 %collective-permute-start = (bf16[256,32,48]{0,2,1:T(8,128)(2,1)}, bf16[256,32,48]{0,2,1:T(8,128)(2,1)S(1)}, u32[]{:S(2)}, u32[]{:S(2)}) collective-permute-start(bf16[256,32,48]{0,2,1:T(8,128)(2,1)} %bitcast.71), channel_id=1, source_target_pairs={{0,14},{2,0},{4,2},{6,4},{8,6},{10,8},{12,10},{14,12},{1,15},{3,1}... | collective-permute-start | bytes 2359304 | tf_op jit(solution)/shard_map/ppermute | solution.py:51
  6.7 1.2 %slice_select_fusion = bf16[256,18,48]{0,2,1:T(8,128)(2,1)S(1)} fusion(bf16[256,32,48]{0,2,1:T(8,128)(2,1)} %bitcast.72, pred[]{:T(512)S(6)} %eq.28), kind=kLoop, calls=%fused_computation.18 | loop fusion | flops 221184 | bytes 1327105 | tf_op jit(solution)/shard_map/jit(_where)/select_n | solution.py:36
  8.0 0.7 and_bitcast_fusion
  8.8 1.3 %convert_reduce_fusion.2 = (f32[64]{0:T(128)S(1)}, f32[64]{0:T(128)S(1)}, f32[64]{0:T(128)S(1)}) fusion(s32[32,48]{1,0:T(8,128)} %bitcast.79, pred[32,48]{1,0:T(8,128)(4,1)S(1)} %get-tuple-element.10, f32[32]{0:T(128)S(1)} %add_convert_fusion), kind=kLoop, calls=%fused_computation.12 | loop fusion | flops 786240 | bytes 8576 | tf_op jit(solution)/shard_map/reduce_sum | solution.py:284
  10.7 0.9 fusion.10.rest_3_
  11.5 1.2 %dynamic_slice.4 = s32[1]{0:T(128)} dynamic-slice(s32[8]{0:T(128)} %param.11, s32[]{:T(128)S(6)} %select_n.89), dynamic_slice_sizes={1} | dynamic-slice | bytes 12 | tf_op jit(solution)/shard_map/jit(dynamic_index_in_dim)/dynamic_slice | solution.py:247
  13.4 2.2 %fusion.2 = f32[3,32,48]{2,0,1:T(4,128)S(1)} fusion(s32[32,48]{1,0:T(8,128)} %bitcast.80, pred[32,48]{1,0:T(8,128)(4,1)S(1)} %get-tuple-element.10, f32[3,64]{1,0:T(4,128)S(1)} %collective-permute-done.5, f32[1,64]{1,0:T(1,128)S(1)} %bitcast.90, f32[1,64]{1,0:T(1,128)S(1)} %bitcast.92, f32[1,64]{1,0:T(1,128)S(1)} %bitcast.88), kind=kOutput, calls=%fused_computation.15 | convolution fusion | flops 3736128 | bytes 27648 | tf_op jit(solution)/shard_map/sk,khw->shw/dot_general | solution.py:320
  16.0 1.8 %pad.12 = bf16[70,80,256]{2,1,0:T(8,128)(2,1)} pad(bf16[68,48,256]{2,1,0:T(8,128)(2,1)S(1)} %maximum_bitcast_fusion.1, bf16[]{:T(256)} %constant.59.clone.1), padding=1_1x32_0x0_0 | pad | bytes 4538370 | tf_op jit(solution)/shard_map/jit(_pad)/pad | solution.py:263
  17.8 15.3 %shard_map.113.rest_0_ = f32[4,2560,256]{2,1,0:T(8,128)} custom-call(bf16[5600,256]{1,0:T(8,128)(2,1)} %bitcast.75, bf16[256,512]{1,0:T(8,128)(2,1)} %point_ref.3, bf16[3,9,256,512]{3,2,1,0:T(8,128)(2,1)} %dilated_ref.3), custom_call_target="tpu_custom_call" | custom-call | flops 9395240960 | bytes 16891904 | tf_op jit(solution)/shard_map/pallas_call | solution.py:159
  35.1 1.7 %fusion.16.rest_2_ = f32[1,256]{1,0:T(1,128)} fusion(bf16[256,1]{0,1:T(2,128)(2,1)S(1)} %reshape.71, bf16[256,1280]{1,0:T(8,128)(2,1)} %rest_1_.1), kind=kOutput, calls=%fused_computation.38 | convolution fusion | flops 131072 | bytes 132608 | tf_op jit(solution)/shard_map/dot_general | solution.py:297
  37.0 1.8 %pad.11 = bf16[70,80,256]{2,1,0:T(8,128)(2,1)} pad(bf16[68,48,256]{2,1,0:T(8,128)(2,1)S(1)} %maximum_bitcast_fusion, bf16[]{:T(256)} %constant.59.clone.1), padding=1_1x32_0x0_0 | pad | bytes 4538370 | tf_op jit(solution)/shard_map/jit(_pad)/pad | solution.py:263
  38.8 21.8 %shard_map.114 = f32[2560,256]{1,0:T(8,128)} custom-call(bf16[5600,256]{1,0:T(8,128)(2,1)} %bitcast.74, bf16[256,512]{1,0:T(8,128)(2,1)} %point_ref.3, bf16[3,9,256,512]{3,2,1,0:T(8,128)(2,1)} %dilated_ref.3, f32[4,2560,256]{2,1,0:T(8,128)} %shard_map.113.rest_0_, bf16[256,1280]{1,0:T(8,128)(2,1)} %rest_1_.1, f32[1,256]{1,0:T(1,128)} %fusion.16.rest_2_, ...), custom_call_target="tpu_custom_call" | custom-call | flops 10737418240 | bytes 16891904 | tf_op jit(solution)/shard_map/pallas_call | solution.py:159
  60.6 1.0 %slice_select_fusion.2 = f32[160,256]{1,0:T(8,128)S(1)} fusion(f32[2560,256]{1,0:T(8,128)} %shard_map.114, pred[]{:T(512)S(6)} %eq.28), kind=kLoop, calls=%fused_computation.37 | loop fusion | flops 40960 | bytes 491521 | tf_op jit(solution)/shard_map/jit(_where)/select_n | solution.py:36
  61.9 1.2 %collective-permute-done.4 = f32[160,256]{1,0:T(8,128)S(1)} collective-permute-done((f32[160,256]{1,0:T(8,128)S(1)}, f32[160,256]{1,0:T(8,128)S(1)}, u32[]{:S(2)}, u32[]{:S(2)}) %collective-permute-start.4) | collective-permute-done | bytes 163872 | tf_op jit(solution)/shard_map/ppermute | solution.py:41
  63.1 2.0 %select_maximum_fusion.x_ref = f32[3040,256]{1,0:T(8,128)S(1)} fusion(f32[160,256]{1,0:T(8,128)S(1)} %get-tuple-element.20, f32[2560,256]{1,0:T(8,128)} %shard_map.114, f32[160,256]{1,0:T(8,128)S(1)} %get-tuple-element.19), kind=kLoop, calls=%fused_computation.2 | loop fusion | flops 6225920 | bytes 6062080 | tf_op jit(solution)/shard_map/concatenate | solution.py:45
  65.2 8.8 %shard_map.115 = bf16[2560,96]{1,0:T(8,128)(2,1)S(1)} custom-call(f32[3040,256]{1,0:T(8,128)S(1)} %select_maximum_fusion.x_ref, bf16[25,96,256]{2,1,0:T(8,128)(2,1)S(1)} %copy-done.1), custom_call_target="tpu_custom_call" | custom-call | flops 3145728000 | bytes 4833280 | tf_op jit(solution)/shard_map/pallas_call | solution.py:198
  74.9 0.7 multiply_reduce_fusion
  75.7 2.0 %pad_maximum_fusion.2 = f32[3]{0:T(128)S(1)} fusion(f32[1]{0:T(128)} %bitcast.37, f32[1]{0:T(128)} %bitcast.36, f32[1]{0:T(128)} %bitcast.33), kind=kLoop, calls=%fused_computation.57 | loop fusion | flops 6 | bytes 24 | tf_op jit(solution)/shard_map/stack | solution.py:338
  77.9 0.6 copy.18
  78.8 3.6 %collective-permute-done.7 = f32[3]{0:T(128)S(1)} collective-permute-done((f32[3]{0:T(128)S(1)}, f32[3]{0:T(128)S(1)}, u32[]{:S(2)}, u32[]{:S(2)}) %collective-permute-start.7) | collective-permute-done | bytes 44 | tf_op jit(solution)/shard_map/ppermute | solution.py:63
  82.4 3.6 %collective-permute-done.8 = f32[3]{0:T(128)S(1)} collective-permute-done((f32[3]{0:T(128)S(1)}, f32[3]{0:T(128)S(1)}, u32[]{:S(2)}, u32[]{:S(2)}) %collective-permute-start.8) | collective-permute-done | bytes 44 | tf_op jit(solution)/shard_map/ppermute | solution.py:63
  86.0 4.5 %collective-permute-done.9 = f32[3]{0:T(128)S(1)} collective-permute-done((f32[3]{0:T(128)S(1)}, f32[3]{0:T(128)S(1)}, u32[]{:S(2)}, u32[]{:S(2)}) %collective-permute-start.9) | collective-permute-done | bytes 44 | tf_op jit(solution)/shard_map/ppermute | solution.py:63
  90.5 0.7 fusion.28
  93.1 0.6 pad_maximum_fusion.3
  (52 shorter events, 4.8 us)
Async XLA Ops:
  0.6 34.2 %copy-start = (bf16[256,512]{1,0:T(8,128)(2,1)S(1)}, bf16[256,512]{1,0:T(8,128)(2,1)}, u32[]{:S(2)}) copy-start(bf16[256,512]{1,0:T(8,128)(2,1)} %param.16) | copy-start | bytes 786436
  0.6 15.1 %copy-start.2 = (bf16[1,256,32,48]{1,3,2,0:T(8,128)(2,1)S(1)}, bf16[1,256,32,48]{1,3,2,0:T(8,128)(2,1)}, u32[]{:S(2)}) copy-start(bf16[1,256,32,48]{1,3,2,0:T(8,128)(2,1)} %param.10) | copy-start | bytes 2359300
  0.7 32.5 %collective-permute-start = (bf16[256,32,48]{0,2,1:T(8,128)(2,1)}, bf16[256,32,48]{0,2,1:T(8,128)(2,1)S(1)}, u32[]{:S(2)}, u32[]{:S(2)}) collective-permute-start(bf16[256,32,48]{0,2,1:T(8,128)(2,1)} %bitcast.71), channel_id=1, source_target_pairs={{0,14},{2,0},{4,2},{6,4},{8,6},{10,8},{12,10},{14,12},{1,15},{3,1}... | collective-permute-start | bytes 2359304 | tf_op jit(solution)/shard_map/ppermute | solution.py:51
  7.9 7.7 %collective-permute-start.2 = (bf16[256,18,48]{0,2,1:T(8,128)(2,1)S(1)}, bf16[256,18,48]{0,2,1:T(8,128)(2,1)S(1)}, u32[]{:S(2)}, u32[]{:S(2)}) collective-permute-start(bf16[256,18,48]{0,2,1:T(8,128)(2,1)S(1)} %slice_select_fusion), channel_id=1, source_target_pairs={{0,1},{1,0},{2,3},{3,2},{4,5},{5,4},{6,7},{7,6},{8,9},{9,8},{10,11... | collective-permute-start | bytes 1327112 | tf_op jit(solution)/shard_map/ppermute | solution.py:41
  10.1 3.3 %collective-permute-start.5 = (f32[3,64]{1,0:T(4,128)S(1)}, f32[3,64]{1,0:T(4,128)S(1)}, u32[]{:S(2)}, u32[]{:S(2)}) collective-permute-start(f32[3,64]{1,0:T(4,128)S(1)} %pad_maximum_fusion.1), channel_id=1, source_target_pairs={{0,1},{1,0},{2,3},{3,2},{4,5},{5,4},{6,7},{7,6},{8,9},{9,8},{10,11... | collective-permute-start | bytes 2312 | tf_op jit(solution)/shard_map/ppermute | solution.py:63
  33.6 1.2 %collective-permute-start.3 = (f32[512]{0:T(512)S(1)}, f32[512]{0:T(512)S(1)}, u32[]{:S(2)}, u32[]{:S(2)}) collective-permute-start(f32[512]{0:T(512)S(1)} %pad_maximum_fusion), channel_id=1, source_target_pairs={{0,1},{1,0},{2,3},{3,2},{4,5},{5,4},{6,7},{7,6},{8,9},{9,8},{10,11... | collective-permute-start | bytes 6152 | tf_op jit(solution)/shard_map/ppermute | solution.py:63
  33.7 3.0 %collective-permute-start.1 = (bf16[256,18,48]{0,2,1:T(8,128)(2,1)S(1)}, bf16[256,18,48]{0,2,1:T(8,128)(2,1)S(1)}, u32[]{:S(2)}, u32[]{:S(2)}) collective-permute-start(bf16[256,18,48]{0,2,1:T(8,128)(2,1)S(1)} %slice_select_fusion.1), channel_id=1, source_target_pairs={{0,1},{1,0},{2,3},{3,2},{4,5},{5,4},{6,7},{7,6},{8,9},{9,8},{10,11... | collective-permute-start | bytes 1327112 | tf_op jit(solution)/shard_map/ppermute | solution.py:41
  61.6 1.5 %collective-permute-start.4 = (f32[160,256]{1,0:T(8,128)S(1)}, f32[160,256]{1,0:T(8,128)S(1)}, u32[]{:S(2)}, u32[]{:S(2)}) collective-permute-start(f32[160,256]{1,0:T(8,128)S(1)} %slice_select_fusion.2), channel_id=1, source_target_pairs={{0,1},{1,0},{2,3},{3,2},{4,5},{5,4},{6,7},{7,6},{8,9},{9,8},{10,11... | collective-permute-start | bytes 491528 | tf_op jit(solution)/shard_map/ppermute | solution.py:41
  63.1 2.1 %copy-start.1 = (bf16[25,96,256]{2,1,0:T(8,128)(2,1)S(1)}, bf16[25,96,256]{2,1,0:T(8,128)(2,1)}, u32[]{:S(2)}) copy-start(bf16[25,96,256]{2,1,0:T(8,128)(2,1)} %weight_ref.1) | copy-start | bytes 3686404
  65.2 9.3 %copy-start.4 = (bf16[4,32]{1,0:T(4,128)(2,1)S(1)}, bf16[4,32]{1,0:T(4,128)(2,1)}, u32[]{:S(2)}) copy-start(bf16[4,32]{1,0:T(4,128)(2,1)} %param.19) | copy-start | bytes 772
  74.0 0.9 copy-start.3
  77.7 1.2 %collective-permute-start.6 = (f32[3]{0:T(128)S(1)}, f32[3]{0:T(128)S(1)}, u32[]{:S(2)}, u32[]{:S(2)}) collective-permute-start(f32[3]{0:T(128)S(1)} %pad_maximum_fusion.2), channel_id=1, source_target_pairs={{0,1},{1,0},{2,3},{3,2},{4,5},{5,4},{6,7},{7,6},{8,9},{9,8},{10,11... | collective-permute-start | bytes 44 | tf_op jit(solution)/shard_map/ppermute | solution.py:63
  78.8 3.6 %collective-permute-start.7 = (f32[3]{0:T(128)S(1)}, f32[3]{0:T(128)S(1)}, u32[]{:S(2)}, u32[]{:S(2)}) collective-permute-start(f32[3]{0:T(128)S(1)} %add.74), channel_id=1, source_target_pairs={{0,2},{2,0},{4,6},{6,4},{8,10},{10,8},{12,14},{14,12},{1,3},{3,1},... | collective-permute-start | bytes 44 | tf_op jit(solution)/shard_map/ppermute | solution.py:63
  82.4 3.6 %collective-permute-start.8 = (f32[3]{0:T(128)S(1)}, f32[3]{0:T(128)S(1)}, u32[]{:S(2)}, u32[]{:S(2)}) collective-permute-start(f32[3]{0:T(128)S(1)} %add.75), channel_id=1, source_target_pairs={{0,4},{2,6},{4,0},{6,2},{8,12},{10,14},{12,8},{14,10},{1,5},{3,7},... | collective-permute-start | bytes 44 | tf_op jit(solution)/shard_map/ppermute | solution.py:63
  86.0 4.5 %collective-permute-start.9 = (f32[3]{0:T(128)S(1)}, f32[3]{0:T(128)S(1)}, u32[]{:S(2)}, u32[]{:S(2)}) collective-permute-start(f32[3]{0:T(128)S(1)} %add.76), channel_id=1, source_target_pairs={{0,8},{2,10},{4,12},{6,14},{8,0},{10,2},{12,4},{14,6},{1,9},{3,11}... | collective-permute-start | bytes 44 | tf_op jit(solution)/shard_map/ppermute | solution.py:63

commit v9 on v8

--- a/solution.py
+++ b/solution.py
@@ -90,14 +90,17 @@
                 out_ref.at[:, rows, :], out_hbm.at[:, rows, :], sems.at[index]
             )
 
+        ahead = 2
         if finish:
-            for index in range(blocks):
+            for index in range(min(ahead, blocks)):
                 block_copy(index).start()
         for index in range(blocks):
             base = front + margin * pitch + index * block
             rows = pl.ds(index * block, block)
             if finish:
                 block_copy(index).wait()
+                if index + ahead < blocks:
+                    block_copy(index + ahead).start()
 
             def window(shift):
                 return x_ref[pl.ds(base + shift, block), :]

time: 94.2 us -> 94.2 us (level)
  no operation moved by 1% of the time
where the time goes in v9:
time: 94.2 us; the launch traced here: 93.7 us
  Pallas kernels  45.9 us (49%)
  waiting for transfers between devices  13.7 us (15%)
  other arithmetic  11.6 us (12%)
  starting transfers between devices  7.72 us (8%)
  local copies, waits for them, and re-layouts  6.74 us (7%)
  matrix products  4.49 us (5%)
  between operations  3.48 us (4%)
    pallas_call x2, Pallas kernels, aspp_pass(): pl.pallas_call(body, out_shape=out_shape, in_specs=in_specs, out_specs=ou...  37.1 us
    ppermute x6, waiting for transfers between devices, all_sum(): other = lax.ppermute(value, axis, pairs)  12.5 us
    pallas_call x1, Pallas kernels, head_kernel_call(): pl.pallas_call(body, out_shape=jax.ShapeDtypeStruct((blocks * block, outp...  8.84 us
    ppermute x1, starting transfers between devices, shifted(): return lax.ppermute(value, axis, pairs)  6.09 us
    pad x2, local copies, waits for them, and re-layouts, flat_of(): jnp.pad(jnp.transpose(wide, (1, 2, 0)), ((1, 1), (pitch - columns, 0), (0...  3.67 us
    select_n x3, other arithmetic, with_rims(): jnp.where(first, lax.slice_in_dim(block, size - width, None, axis=dim), l...  2.26 us
    dot_general x1, matrix products, shards(): jnp.einsum('sk,khw->shw', inst_stats, onehot, precision=lax.Precision.HIG...  2.23 us
    concatenate x1, other arithmetic, with_rims(): return jnp.concatenate([low, block, high], axis=dim)  2.04 us
  transfers between devices with their start and end apart: 10, of which 6 were waited for; matrix products, arithmetic and copies ran while one was open for 13% of the time, Pallas kernels for 16%

profile of v9, /device:TPU:0, one launch (start us, length us, event | category | flops | bytes accessed | tf_op | source)
XLA Modules:
  0.0 93.7 jit_solution(4263803373602062988)
XLA Ops:
  0.7 6.1 %collective-permute-start = (bf16[256,32,48]{0,2,1:T(8,128)(2,1)}, bf16[256,32,48]{0,2,1:T(8,128)(2,1)S(1)}, u32[]{:S(2)}, u32[]{:S(2)}) collective-permute-start(bf16[256,32,48]{0,2,1:T(8,128)(2,1)} %bitcast.71), channel_id=1, source_target_pairs={{0,14},{2,0},{4,2},{6,4},{8,6},{10,8},{12,10},{14,12},{1,15},{3,1}... | collective-permute-start | bytes 2359304 | tf_op jit(solution)/shard_map/ppermute | solution.py:51
  6.7 1.2 %slice_select_fusion = bf16[256,18,48]{0,2,1:T(8,128)(2,1)S(1)} fusion(bf16[256,32,48]{0,2,1:T(8,128)(2,1)} %bitcast.72, pred[]{:T(512)S(6)} %eq.28), kind=kLoop, calls=%fused_computation.18 | loop fusion | flops 221184 | bytes 1327105 | tf_op jit(solution)/shard_map/jit(_where)/select_n | solution.py:36
  8.0 0.7 and_bitcast_fusion
  8.8 1.3 %convert_reduce_fusion.2 = (f32[64]{0:T(128)S(1)}, f32[64]{0:T(128)S(1)}, f32[64]{0:T(128)S(1)}) fusion(s32[32,48]{1,0:T(8,128)} %bitcast.79, pred[32,48]{1,0:T(8,128)(4,1)S(1)} %get-tuple-element.10, f32[32]{0:T(128)S(1)} %add_convert_fusion), kind=kLoop, calls=%fused_computation.12 | loop fusion | flops 786240 | bytes 8576 | tf_op jit(solution)/shard_map/reduce_sum | solution.py:287
  10.7 0.9 fusion.10.rest_3_
  11.5 1.2 %dynamic_slice.4 = s32[1]{0:T(128)} dynamic-slice(s32[8]{0:T(128)} %param.11, s32[]{:T(128)S(6)} %select_n.89), dynamic_slice_sizes={1} | dynamic-slice | bytes 12 | tf_op jit(solution)/shard_map/jit(dynamic_index_in_dim)/dynamic_slice | solution.py:250
  13.4 2.2 %fusion.2 = f32[3,32,48]{2,0,1:T(4,128)S(1)} fusion(s32[32,48]{1,0:T(8,128)} %bitcast.80, pred[32,48]{1,0:T(8,128)(4,1)S(1)} %get-tuple-element.10, f32[3,64]{1,0:T(4,128)S(1)} %collective-permute-done.5, f32[1,64]{1,0:T(1,128)S(1)} %bitcast.90, f32[1,64]{1,0:T(1,128)S(1)} %bitcast.92, f32[1,64]{1,0:T(1,128)S(1)} %bitcast.88), kind=kOutput, calls=%fused_computation.15 | convolution fusion | flops 3736128 | bytes 27648 | tf_op jit(solution)/shard_map/sk,khw->shw/dot_general | solution.py:323
  16.0 1.8 %pad.12 = bf16[70,80,256]{2,1,0:T(8,128)(2,1)} pad(bf16[68,48,256]{2,1,0:T(8,128)(2,1)S(1)} %maximum_bitcast_fusion.1, bf16[]{:T(256)} %constant.59.clone.1), padding=1_1x32_0x0_0 | pad | bytes 4538370 | tf_op jit(solution)/shard_map/jit(_pad)/pad | solution.py:266
  17.8 15.3 %shard_map.113.rest_0_ = f32[4,2560,256]{2,1,0:T(8,128)} custom-call(bf16[5600,256]{1,0:T(8,128)(2,1)} %bitcast.75, bf16[256,512]{1,0:T(8,128)(2,1)} %point_ref.3, bf16[3,9,256,512]{3,2,1,0:T(8,128)(2,1)} %dilated_ref.3), custom_call_target="tpu_custom_call" | custom-call | flops 9395240960 | bytes 16891904 | tf_op jit(solution)/shard_map/pallas_call | solution.py:162
  35.1 1.7 %fusion.16.rest_2_ = f32[1,256]{1,0:T(1,128)} fusion(bf16[256,1]{0,1:T(2,128)(2,1)S(1)} %reshape.71, bf16[256,1280]{1,0:T(8,128)(2,1)} %rest_1_.1), kind=kOutput, calls=%fused_computation.38 | convolution fusion | flops 131072 | bytes 132608 | tf_op jit(solution)/shard_map/dot_general | solution.py:300
  37.0 1.8 %pad.11 = bf16[70,80,256]{2,1,0:T(8,128)(2,1)} pad(bf16[68,48,256]{2,1,0:T(8,128)(2,1)S(1)} %maximum_bitcast_fusion, bf16[]{:T(256)} %constant.59.clone.1), padding=1_1x32_0x0_0 | pad | bytes 4538370 | tf_op jit(solution)/shard_map/jit(_pad)/pad | solution.py:266
  38.8 21.8 %shard_map.114 = f32[2560,256]{1,0:T(8,128)} custom-call(bf16[5600,256]{1,0:T(8,128)(2,1)} %bitcast.74, bf16[256,512]{1,0:T(8,128)(2,1)} %point_ref.3, bf16[3,9,256,512]{3,2,1,0:T(8,128)(2,1)} %dilated_ref.3, f32[4,2560,256]{2,1,0:T(8,128)} %shard_map.113.rest_0_, bf16[256,1280]{1,0:T(8,128)(2,1)} %rest_1_.1, f32[1,256]{1,0:T(1,128)} %fusion.16.rest_2_, ...), custom_call_target="tpu_custom_call" | custom-call | flops 10737418240 | bytes 16891904 | tf_op jit(solution)/shard_map/pallas_call | solution.py:162
  60.6 1.0 %slice_select_fusion.2 = f32[160,256]{1,0:T(8,128)S(1)} fusion(f32[2560,256]{1,0:T(8,128)} %shard_map.114, pred[]{:T(512)S(6)} %eq.28), kind=kLoop, calls=%fused_computation.37 | loop fusion | flops 40960 | bytes 491521 | tf_op jit(solution)/shard_map/jit(_where)/select_n | solution.py:36
  61.9 1.2 %collective-permute-done.4 = f32[160,256]{1,0:T(8,128)S(1)} collective-permute-done((f32[160,256]{1,0:T(8,128)S(1)}, f32[160,256]{1,0:T(8,128)S(1)}, u32[]{:S(2)}, u32[]{:S(2)}) %collective-permute-start.4) | collective-permute-done | bytes 163872 | tf_op jit(solution)/shard_map/ppermute | solution.py:41
  63.1 2.0 %select_maximum_fusion.x_ref = f32[3040,256]{1,0:T(8,128)S(1)} fusion(f32[160,256]{1,0:T(8,128)S(1)} %get-tuple-element.20, f32[2560,256]{1,0:T(8,128)} %shard_map.114, f32[160,256]{1,0:T(8,128)S(1)} %get-tuple-element.19), kind=kLoop, calls=%fused_computation.2 | loop fusion | flops 6225920 | bytes 6062080 | tf_op jit(solution)/shard_map/concatenate | solution.py:45
  65.2 8.8 %shard_map.115 = bf16[2560,96]{1,0:T(8,128)(2,1)S(1)} custom-call(f32[3040,256]{1,0:T(8,128)S(1)} %select_maximum_fusion.x_ref, bf16[25,96,256]{2,1,0:T(8,128)(2,1)S(1)} %copy-done.1), custom_call_target="tpu_custom_call" | custom-call | flops 3145728000 | bytes 4833280 | tf_op jit(solution)/shard_map/pallas_call | solution.py:201
  75.0 0.7 multiply_reduce_fusion
  75.7 2.0 %pad_maximum_fusion.2 = f32[3]{0:T(128)S(1)} fusion(f32[1]{0:T(128)} %bitcast.37, f32[1]{0:T(128)} %bitcast.36, f32[1]{0:T(128)} %bitcast.33), kind=kLoop, calls=%fused_computation.57 | loop fusion | flops 6 | bytes 24 | tf_op jit(solution)/shard_map/stack | solution.py:341
  77.9 0.6 copy.18
  78.9 3.6 %collective-permute-done.7 = f32[3]{0:T(128)S(1)} collective-permute-done((f32[3]{0:T(128)S(1)}, f32[3]{0:T(128)S(1)}, u32[]{:S(2)}, u32[]{:S(2)}) %collective-permute-start.7) | collective-permute-done | bytes 44 | tf_op jit(solution)/shard_map/ppermute | solution.py:63
  82.4 3.6 %collective-permute-done.8 = f32[3]{0:T(128)S(1)} collective-permute-done((f32[3]{0:T(128)S(1)}, f32[3]{0:T(128)S(1)}, u32[]{:S(2)}, u32[]{:S(2)}) %collective-permute-start.8) | collective-permute-done | bytes 44 | tf_op jit(solution)/shard_map/ppermute | solution.py:63
  86.0 4.5 %collective-permute-done.9 = f32[3]{0:T(128)S(1)} collective-permute-done((f32[3]{0:T(128)S(1)}, f32[3]{0:T(128)S(1)}, u32[]{:S(2)}, u32[]{:S(2)}) %collective-permute-start.9) | collective-permute-done | bytes 44 | tf_op jit(solution)/shard_map/ppermute | solution.py:63
  90.5 0.7 fusion.28
  93.1 0.6 pad_maximum_fusion.3
  (52 shorter events, 4.8 us)
Async XLA Ops:
  0.6 34.2 %copy-start = (bf16[256,512]{1,0:T(8,128)(2,1)S(1)}, bf16[256,512]{1,0:T(8,128)(2,1)}, u32[]{:S(2)}) copy-start(bf16[256,512]{1,0:T(8,128)(2,1)} %param.16) | copy-start | bytes 786436
  0.6 15.1 %copy-start.2 = (bf16[1,256,32,48]{1,3,2,0:T(8,128)(2,1)S(1)}, bf16[1,256,32,48]{1,3,2,0:T(8,128)(2,1)}, u32[]{:S(2)}) copy-start(bf16[1,256,32,48]{1,3,2,0:T(8,128)(2,1)} %param.10) | copy-start | bytes 2359300
  0.7 32.5 %collective-permute-start = (bf16[256,32,48]{0,2,1:T(8,128)(2,1)}, bf16[256,32,48]{0,2,1:T(8,128)(2,1)S(1)}, u32[]{:S(2)}, u32[]{:S(2)}) collective-permute-start(bf16[256,32,48]{0,2,1:T(8,128)(2,1)} %bitcast.71), channel_id=1, source_target_pairs={{0,14},{2,0},{4,2},{6,4},{8,6},{10,8},{12,10},{14,12},{1,15},{3,1}... | collective-permute-start | bytes 2359304 | tf_op jit(solution)/shard_map/ppermute | solution.py:51
  7.9 7.7 %collective-permute-start.2 = (bf16[256,18,48]{0,2,1:T(8,128)(2,1)S(1)}, bf16[256,18,48]{0,2,1:T(8,128)(2,1)S(1)}, u32[]{:S(2)}, u32[]{:S(2)}) collective-permute-start(bf16[256,18,48]{0,2,1:T(8,128)(2,1)S(1)} %slice_select_fusion), channel_id=1, source_target_pairs={{0,1},{1,0},{2,3},{3,2},{4,5},{5,4},{6,7},{7,6},{8,9},{9,8},{10,11... | collective-permute-start | bytes 1327112 | tf_op jit(solution)/shard_map/ppermute | solution.py:41
  10.1 3.3 %collective-permute-start.5 = (f32[3,64]{1,0:T(4,128)S(1)}, f32[3,64]{1,0:T(4,128)S(1)}, u32[]{:S(2)}, u32[]{:S(2)}) collective-permute-start(f32[3,64]{1,0:T(4,128)S(1)} %pad_maximum_fusion.1), channel_id=1, source_target_pairs={{0,1},{1,0},{2,3},{3,2},{4,5},{5,4},{6,7},{7,6},{8,9},{9,8},{10,11... | collective-permute-start | bytes 2312 | tf_op jit(solution)/shard_map/ppermute | solution.py:63
  33.6 1.2 %collective-permute-start.3 = (f32[512]{0:T(512)S(1)}, f32[512]{0:T(512)S(1)}, u32[]{:S(2)}, u32[]{:S(2)}) collective-permute-start(f32[512]{0:T(512)S(1)} %pad_maximum_fusion), channel_id=1, source_target_pairs={{0,1},{1,0},{2,3},{3,2},{4,5},{5,4},{6,7},{7,6},{8,9},{9,8},{10,11... | collective-permute-start | bytes 6152 | tf_op jit(solution)/shard_map/ppermute | solution.py:63
  33.7 3.0 %collective-permute-start.1 = (bf16[256,18,48]{0,2,1:T(8,128)(2,1)S(1)}, bf16[256,18,48]{0,2,1:T(8,128)(2,1)S(1)}, u32[]{:S(2)}, u32[]{:S(2)}) collective-permute-start(bf16[256,18,48]{0,2,1:T(8,128)(2,1)S(1)} %slice_select_fusion.1), channel_id=1, source_target_pairs={{0,1},{1,0},{2,3},{3,2},{4,5},{5,4},{6,7},{7,6},{8,9},{9,8},{10,11... | collective-permute-start | bytes 1327112 | tf_op jit(solution)/shard_map/ppermute | solution.py:41
  61.6 1.5 %collective-permute-start.4 = (f32[160,256]{1,0:T(8,128)S(1)}, f32[160,256]{1,0:T(8,128)S(1)}, u32[]{:S(2)}, u32[]{:S(2)}) collective-permute-start(f32[160,256]{1,0:T(8,128)S(1)} %slice_select_fusion.2), channel_id=1, source_target_pairs={{0,1},{1,0},{2,3},{3,2},{4,5},{5,4},{6,7},{7,6},{8,9},{9,8},{10,11... | collective-permute-start | bytes 491528 | tf_op jit(solution)/shard_map/ppermute | solution.py:41
  63.1 2.1 %copy-start.1 = (bf16[25,96,256]{2,1,0:T(8,128)(2,1)S(1)}, bf16[25,96,256]{2,1,0:T(8,128)(2,1)}, u32[]{:S(2)}) copy-start(bf16[25,96,256]{2,1,0:T(8,128)(2,1)} %weight_ref.1) | copy-start | bytes 3686404
  65.2 9.3 %copy-start.4 = (bf16[4,32]{1,0:T(4,128)(2,1)S(1)}, bf16[4,32]{1,0:T(4,128)(2,1)}, u32[]{:S(2)}) copy-start(bf16[4,32]{1,0:T(4,128)(2,1)} %param.19) | copy-start | bytes 772
  74.0 0.9 copy-start.3
  77.7 1.2 %collective-permute-start.6 = (f32[3]{0:T(128)S(1)}, f32[3]{0:T(128)S(1)}, u32[]{:S(2)}, u32[]{:S(2)}) collective-permute-start(f32[3]{0:T(128)S(1)} %pad_maximum_fusion.2), channel_id=1, source_target_pairs={{0,1},{1,0},{2,3},{3,2},{4,5},{5,4},{6,7},{7,6},{8,9},{9,8},{10,11... | collective-permute-start | bytes 44 | tf_op jit(solution)/shard_map/ppermute | solution.py:63
  78.9 3.6 %collective-permute-start.7 = (f32[3]{0:T(128)S(1)}, f32[3]{0:T(128)S(1)}, u32[]{:S(2)}, u32[]{:S(2)}) collective-permute-start(f32[3]{0:T(128)S(1)} %add.74), channel_id=1, source_target_pairs={{0,2},{2,0},{4,6},{6,4},{8,10},{10,8},{12,14},{14,12},{1,3},{3,1},... | collective-permute-start | bytes 44 | tf_op jit(solution)/shard_map/ppermute | solution.py:63
  82.4 3.6 %collective-permute-start.8 = (f32[3]{0:T(128)S(1)}, f32[3]{0:T(128)S(1)}, u32[]{:S(2)}, u32[]{:S(2)}) collective-permute-start(f32[3]{0:T(128)S(1)} %add.75), channel_id=1, source_target_pairs={{0,4},{2,6},{4,0},{6,2},{8,12},{10,14},{12,8},{14,10},{1,5},{3,7},... | collective-permute-start | bytes 44 | tf_op jit(solution)/shard_map/ppermute | solution.py:63
  86.0 4.5 %collective-permute-start.9 = (f32[3]{0:T(128)S(1)}, f32[3]{0:T(128)S(1)}, u32[]{:S(2)}, u32[]{:S(2)}) collective-permute-start(f32[3]{0:T(128)S(1)} %add.76), channel_id=1, source_target_pairs={{0,8},{2,10},{4,12},{6,14},{8,0},{10,2},{12,4},{14,6},{1,9},{3,11}... | collective-permute-start | bytes 44 | tf_op jit(solution)/shard_map/ppermute | solution.py:63

commit v10 on v9

--- a/solution.py
+++ b/solution.py
@@ -105,11 +105,27 @@
             def window(shift):
                 return x_ref[pl.ds(base + shift, block), :]
 
-            sums = [
+            state = {"mixed": None}
+
+            def consume(branch, total):
+                if not finish:
+                    out_ref[branch, rows, :] = total
+                    return
+                term = lax.dot_general(
+                    relu_bf16(earlier_ref[branch, rows, :] + total),
+                    proj_ref[:, branch * width : (branch + 1) * width],
+                    contract,
+                    preferred_element_type=jnp.float32,
+                )
+                mixed = state["mixed"]
+                state["mixed"] = term if mixed is None else mixed + term
+
+            consume(
+                0,
                 lax.dot_general(
                     window(0), point_ref[:, lanes], contract, preferred_element_type=jnp.float32
-                )
-            ]
+                ),
+            )
             for branch, spread in enumerate(DILATIONS):
                 total = None
                 for vertical in range(3):
@@ -122,21 +138,11 @@
                             preferred_element_type=jnp.float32,
                         )
                         total = term if total is None else total + term
-                sums.append(total)
+                consume(branch + 1, total)
             if not finish:
-                for branch, total in enumerate(sums):
-                    out_ref[branch, rows, :] = total
                 block_copy(index).start()
                 continue
-            mixed = None
-            for branch, total in enumerate(sums):
-                term = lax.dot_general(
-                    relu_bf16(earlier_ref[branch, rows, :] + total),
-                    proj_ref[:, branch * width : (branch + 1) * width],
-                    contract,
-                    preferred_element_type=jnp.float32,
-                )
-                mixed = term if mixed is None else mixed + term
+            mixed = state["mixed"]
             mixed = mixed + pool_ref[...]
             rounded = relu_bf16(mixed).astype(jnp.float32)
             out_ref[rows, :] = jnp.where(keep_ref[...] > 0.5, rounded, 0.0)

time: 94.2 us -> 96.1 us (1.020)
  Pallas kernels: 45.9 us -> 47.9 us
    pallas_call x2, Pallas kernels: 37.1 us -> 39 us  [aspp_pass(): pl.pallas_call(body, out_shape=out_shape, in_specs=in_specs, out_specs=ou...]
where the time goes in v10:
time: 96.1 us; the launch traced here: 95.6 us
  Pallas kernels  47.9 us (50%)
  waiting for transfers between devices  13.6 us (14%)
  other arithmetic  11.6 us (12%)
  starting transfers between devices  7.74 us (8%)
  local copies, waits for them, and re-layouts  6.74 us (7%)
  matrix products  4.48 us (5%)
  between operations  3.48 us (4%)
    pallas_call x2, Pallas kernels, aspp_pass(): pl.pallas_call(body, out_shape=out_shape, in_specs=in_specs, out_specs=ou...  39 us
    ppermute x6, waiting for transfers between devices, all_sum(): other = lax.ppermute(value, axis, pairs)  12.4 us
    pallas_call x1, Pallas kernels, head_kernel_call(): pl.pallas_call(body, out_shape=jax.ShapeDtypeStruct((blocks * block, outp...  8.84 us
    ppermute x1, starting transfers between devices, shifted(): return lax.ppermute(value, axis, pairs)  6.09 us
    pad x2, local copies, waits for them, and re-layouts, flat_of(): jnp.pad(jnp.transpose(wide, (1, 2, 0)), ((1, 1), (pitch - columns, 0), (0...  3.67 us
    select_n x3, other arithmetic, with_rims(): jnp.where(first, lax.slice_in_dim(block, size - width, None, axis=dim), l...  2.26 us
    dot_general x1, matrix products, shards(): jnp.einsum('sk,khw->shw', inst_stats, onehot, precision=lax.Precision.HIG...  2.23 us
    concatenate x1, other arithmetic, with_rims(): return jnp.concatenate([low, block, high], axis=dim)  2.04 us
  transfers between devices with their start and end apart: 10, of which 6 were waited for; matrix products, arithmetic and copies ran while one was open for 13% of the time, Pallas kernels for 16%

profile of v10, /device:TPU:0, one launch (start us, length us, event | category | flops | bytes accessed | tf_op | source)
XLA Modules:
  0.0 95.6 jit_solution(5086245016822050166)
XLA Ops:
  0.7 6.1 %collective-permute-start = (bf16[256,32,48]{0,2,1:T(8,128)(2,1)}, bf16[256,32,48]{0,2,1:T(8,128)(2,1)S(1)}, u32[]{:S(2)}, u32[]{:S(2)}) collective-permute-start(bf16[256,32,48]{0,2,1:T(8,128)(2,1)} %bitcast.71), channel_id=1, source_target_pairs={{0,14},{2,0},{4,2},{6,4},{8,6},{10,8},{12,10},{14,12},{1,15},{3,1}... | collective-permute-start | bytes 2359304 | tf_op jit(solution)/shard_map/ppermute | solution.py:51
  6.7 1.2 %slice_select_fusion = bf16[256,18,48]{0,2,1:T(8,128)(2,1)S(1)} fusion(bf16[256,32,48]{0,2,1:T(8,128)(2,1)} %bitcast.72, pred[]{:T(512)S(6)} %eq.28), kind=kLoop, calls=%fused_computation.18 | loop fusion | flops 221184 | bytes 1327105 | tf_op jit(solution)/shard_map/jit(_where)/select_n | solution.py:36
  8.0 0.7 and_bitcast_fusion
  8.8 1.3 %convert_reduce_fusion.2 = (f32[64]{0:T(128)S(1)}, f32[64]{0:T(128)S(1)}, f32[64]{0:T(128)S(1)}) fusion(s32[32,48]{1,0:T(8,128)} %bitcast.79, pred[32,48]{1,0:T(8,128)(4,1)S(1)} %get-tuple-element.10, f32[32]{0:T(128)S(1)} %add_convert_fusion), kind=kLoop, calls=%fused_computation.12 | loop fusion | flops 786240 | bytes 8576 | tf_op jit(solution)/shard_map/reduce_sum | solution.py:293
  10.7 0.9 fusion.10.rest_3_
  11.5 1.2 %dynamic_slice.4 = s32[1]{0:T(128)} dynamic-slice(s32[8]{0:T(128)} %param.11, s32[]{:T(128)S(6)} %select_n.89), dynamic_slice_sizes={1} | dynamic-slice | bytes 12 | tf_op jit(solution)/shard_map/jit(dynamic_index_in_dim)/dynamic_slice | solution.py:256
  13.4 2.2 %fusion.2 = f32[3,32,48]{2,0,1:T(4,128)S(1)} fusion(s32[32,48]{1,0:T(8,128)} %bitcast.80, pred[32,48]{1,0:T(8,128)(4,1)S(1)} %get-tuple-element.10, f32[3,64]{1,0:T(4,128)S(1)} %collective-permute-done.5, f32[1,64]{1,0:T(1,128)S(1)} %bitcast.90, f32[1,64]{1,0:T(1,128)S(1)} %bitcast.92, f32[1,64]{1,0:T(1,128)S(1)} %bitcast.88), kind=kOutput, calls=%fused_computation.15 | convolution fusion | flops 3736128 | bytes 27648 | tf_op jit(solution)/shard_map/sk,khw->shw/dot_general | solution.py:329
  16.0 1.8 %pad.12 = bf16[70,80,256]{2,1,0:T(8,128)(2,1)} pad(bf16[68,48,256]{2,1,0:T(8,128)(2,1)S(1)} %maximum_bitcast_fusion.1, bf16[]{:T(256)} %constant.59.clone.1), padding=1_1x32_0x0_0 | pad | bytes 4538370 | tf_op jit(solution)/shard_map/jit(_pad)/pad | solution.py:272
  17.8 15.3 %shard_map.113.rest_0_ = f32[4,2560,256]{2,1,0:T(8,128)} custom-call(bf16[5600,256]{1,0:T(8,128)(2,1)} %bitcast.75, bf16[256,512]{1,0:T(8,128)(2,1)} %point_ref.3, bf16[3,9,256,512]{3,2,1,0:T(8,128)(2,1)} %dilated_ref.3), custom_call_target="tpu_custom_call" | custom-call | flops 9395240960 | bytes 16891904 | tf_op jit(solution)/shard_map/pallas_call | solution.py:168
  35.1 1.7 %fusion.16.rest_2_ = f32[1,256]{1,0:T(1,128)} fusion(bf16[256,1]{0,1:T(2,128)(2,1)S(1)} %reshape.71, bf16[256,1280]{1,0:T(8,128)(2,1)} %rest_1_.1), kind=kOutput, calls=%fused_computation.38 | convolution fusion | flops 131072 | bytes 132608 | tf_op jit(solution)/shard_map/dot_general | solution.py:306
  37.0 1.8 %pad.11 = bf16[70,80,256]{2,1,0:T(8,128)(2,1)} pad(bf16[68,48,256]{2,1,0:T(8,128)(2,1)S(1)} %maximum_bitcast_fusion, bf16[]{:T(256)} %constant.59.clone.1), padding=1_1x32_0x0_0 | pad | bytes 4538370 | tf_op jit(solution)/shard_map/jit(_pad)/pad | solution.py:272
  38.8 23.7 %shard_map.114 = f32[2560,256]{1,0:T(8,128)} custom-call(bf16[5600,256]{1,0:T(8,128)(2,1)} %bitcast.74, bf16[256,512]{1,0:T(8,128)(2,1)} %point_ref.3, bf16[3,9,256,512]{3,2,1,0:T(8,128)(2,1)} %dilated_ref.3, f32[4,2560,256]{2,1,0:T(8,128)} %shard_map.113.rest_0_, bf16[256,1280]{1,0:T(8,128)(2,1)} %rest_1_.1, f32[1,256]{1,0:T(1,128)} %fusion.16.rest_2_, ...), custom_call_target="tpu_custom_call" | custom-call | flops 10737418240 | bytes 16891904 | tf_op jit(solution)/shard_map/pallas_call | solution.py:168
  62.5 1.0 %slice_select_fusion.2 = f32[160,256]{1,0:T(8,128)S(1)} fusion(f32[2560,256]{1,0:T(8,128)} %shard_map.114, pred[]{:T(512)S(6)} %eq.28), kind=kLoop, calls=%fused_computation.37 | loop fusion | flops 40960 | bytes 491521 | tf_op jit(solution)/shard_map/jit(_where)/select_n | solution.py:36
  63.8 1.2 %collective-permute-done.4 = f32[160,256]{1,0:T(8,128)S(1)} collective-permute-done((f32[160,256]{1,0:T(8,128)S(1)}, f32[160,256]{1,0:T(8,128)S(1)}, u32[]{:S(2)}, u32[]{:S(2)}) %collective-permute-start.4) | collective-permute-done | bytes 163872 | tf_op jit(solution)/shard_map/ppermute | solution.py:41
  65.1 2.0 %select_maximum_fusion.x_ref = f32[3040,256]{1,0:T(8,128)S(1)} fusion(f32[160,256]{1,0:T(8,128)S(1)} %get-tuple-element.20, f32[2560,256]{1,0:T(8,128)} %shard_map.114, f32[160,256]{1,0:T(8,128)S(1)} %get-tuple-element.19), kind=kLoop, calls=%fused_computation.2 | loop fusion | flops 6225920 | bytes 6062080 | tf_op jit(solution)/shard_map/concatenate | solution.py:45
  67.1 8.8 %shard_map.115 = bf16[2560,96]{1,0:T(8,128)(2,1)S(1)} custom-call(f32[3040,256]{1,0:T(8,128)S(1)} %select_maximum_fusion.x_ref, bf16[25,96,256]{2,1,0:T(8,128)(2,1)S(1)} %copy-done.1), custom_call_target="tpu_custom_call" | custom-call | flops 3145728000 | bytes 4833280 | tf_op jit(solution)/shard_map/pallas_call | solution.py:207
  76.9 0.7 multiply_reduce_fusion
  77.6 2.0 %pad_maximum_fusion.2 = f32[3]{0:T(128)S(1)} fusion(f32[1]{0:T(128)} %bitcast.37, f32[1]{0:T(128)} %bitcast.36, f32[1]{0:T(128)} %bitcast.33), kind=kLoop, calls=%fused_computation.57 | loop fusion | flops 6 | bytes 24 | tf_op jit(solution)/shard_map/stack | solution.py:347
  79.9 0.6 copy.18
  80.8 3.6 %collective-permute-done.7 = f32[3]{0:T(128)S(1)} collective-permute-done((f32[3]{0:T(128)S(1)}, f32[3]{0:T(128)S(1)}, u32[]{:S(2)}, u32[]{:S(2)}) %collective-permute-start.7) | collective-permute-done | bytes 44 | tf_op jit(solution)/shard_map/ppermute | solution.py:63
  84.4 3.6 %collective-permute-done.8 = f32[3]{0:T(128)S(1)} collective-permute-done((f32[3]{0:T(128)S(1)}, f32[3]{0:T(128)S(1)}, u32[]{:S(2)}, u32[]{:S(2)}) %collective-permute-start.8) | collective-permute-done | bytes 44 | tf_op jit(solution)/shard_map/ppermute | solution.py:63
  87.9 4.5 %collective-permute-done.9 = f32[3]{0:T(128)S(1)} collective-permute-done((f32[3]{0:T(128)S(1)}, f32[3]{0:T(128)S(1)}, u32[]{:S(2)}, u32[]{:S(2)}) %collective-permute-start.9) | collective-permute-done | bytes 44 | tf_op jit(solution)/shard_map/ppermute | solution.py:63
  92.4 0.7 fusion.28
  95.0 0.6 pad_maximum_fusion.3
  (52 shorter events, 4.8 us)
Async XLA Ops:
  0.6 34.2 %copy-start = (bf16[256,512]{1,0:T(8,128)(2,1)S(1)}, bf16[256,512]{1,0:T(8,128)(2,1)}, u32[]{:S(2)}) copy-start(bf16[256,512]{1,0:T(8,128)(2,1)} %param.16) | copy-start | bytes 786436
  0.6 15.1 %copy-start.2 = (bf16[1,256,32,48]{1,3,2,0:T(8,128)(2,1)S(1)}, bf16[1,256,32,48]{1,3,2,0:T(8,128)(2,1)}, u32[]{:S(2)}) copy-start(bf16[1,256,32,48]{1,3,2,0:T(8,128)(2,1)} %param.10) | copy-start | bytes 2359300
  0.7 32.5 %collective-permute-start = (bf16[256,32,48]{0,2,1:T(8,128)(2,1)}, bf16[256,32,48]{0,2,1:T(8,128)(2,1)S(1)}, u32[]{:S(2)}, u32[]{:S(2)}) collective-permute-start(bf16[256,32,48]{0,2,1:T(8,128)(2,1)} %bitcast.71), channel_id=1, source_target_pairs={{0,14},{2,0},{4,2},{6,4},{8,6},{10,8},{12,10},{14,12},{1,15},{3,1}... | collective-permute-start | bytes 2359304 | tf_op jit(solution)/shard_map/ppermute | solution.py:51
  7.9 7.7 %collective-permute-start.2 = (bf16[256,18,48]{0,2,1:T(8,128)(2,1)S(1)}, bf16[256,18,48]{0,2,1:T(8,128)(2,1)S(1)}, u32[]{:S(2)}, u32[]{:S(2)}) collective-permute-start(bf16[256,18,48]{0,2,1:T(8,128)(2,1)S(1)} %slice_select_fusion), channel_id=1, source_target_pairs={{0,1},{1,0},{2,3},{3,2},{4,5},{5,4},{6,7},{7,6},{8,9},{9,8},{10,11... | collective-permute-start | bytes 1327112 | tf_op jit(solution)/shard_map/ppermute | solution.py:41
  10.1 3.3 %collective-permute-start.5 = (f32[3,64]{1,0:T(4,128)S(1)}, f32[3,64]{1,0:T(4,128)S(1)}, u32[]{:S(2)}, u32[]{:S(2)}) collective-permute-start(f32[3,64]{1,0:T(4,128)S(1)} %pad_maximum_fusion.1), channel_id=1, source_target_pairs={{0,1},{1,0},{2,3},{3,2},{4,5},{5,4},{6,7},{7,6},{8,9},{9,8},{10,11... | collective-permute-start | bytes 2312 | tf_op jit(solution)/shard_map/ppermute | solution.py:63
  33.6 1.2 %collective-permute-start.3 = (f32[512]{0:T(512)S(1)}, f32[512]{0:T(512)S(1)}, u32[]{:S(2)}, u32[]{:S(2)}) collective-permute-start(f32[512]{0:T(512)S(1)} %pad_maximum_fusion), channel_id=1, source_target_pairs={{0,1},{1,0},{2,3},{3,2},{4,5},{5,4},{6,7},{7,6},{8,9},{9,8},{10,11... | collective-permute-start | bytes 6152 | tf_op jit(solution)/shard_map/ppermute | solution.py:63
  33.7 3.0 %collective-permute-start.1 = (bf16[256,18,48]{0,2,1:T(8,128)(2,1)S(1)}, bf16[256,18,48]{0,2,1:T(8,128)(2,1)S(1)}, u32[]{:S(2)}, u32[]{:S(2)}) collective-permute-start(bf16[256,18,48]{0,2,1:T(8,128)(2,1)S(1)} %slice_select_fusion.1), channel_id=1, source_target_pairs={{0,1},{1,0},{2,3},{3,2},{4,5},{5,4},{6,7},{7,6},{8,9},{9,8},{10,11... | collective-permute-start | bytes 1327112 | tf_op jit(solution)/shard_map/ppermute | solution.py:41
  63.6 1.5 %collective-permute-start.4 = (f32[160,256]{1,0:T(8,128)S(1)}, f32[160,256]{1,0:T(8,128)S(1)}, u32[]{:S(2)}, u32[]{:S(2)}) collective-permute-start(f32[160,256]{1,0:T(8,128)S(1)} %slice_select_fusion.2), channel_id=1, source_target_pairs={{0,1},{1,0},{2,3},{3,2},{4,5},{5,4},{6,7},{7,6},{8,9},{9,8},{10,11... | collective-permute-start | bytes 491528 | tf_op jit(solution)/shard_map/ppermute | solution.py:41
  65.0 2.1 %copy-start.1 = (bf16[25,96,256]{2,1,0:T(8,128)(2,1)S(1)}, bf16[25,96,256]{2,1,0:T(8,128)(2,1)}, u32[]{:S(2)}) copy-start(bf16[25,96,256]{2,1,0:T(8,128)(2,1)} %weight_ref.1) | copy-start | bytes 3686404
  67.1 9.3 %copy-start.4 = (bf16[4,32]{1,0:T(4,128)(2,1)S(1)}, bf16[4,32]{1,0:T(4,128)(2,1)}, u32[]{:S(2)}) copy-start(bf16[4,32]{1,0:T(4,128)(2,1)} %param.19) | copy-start | bytes 772
  76.0 0.9 copy-start.3
  79.6 1.2 %collective-permute-start.6 = (f32[3]{0:T(128)S(1)}, f32[3]{0:T(128)S(1)}, u32[]{:S(2)}, u32[]{:S(2)}) collective-permute-start(f32[3]{0:T(128)S(1)} %pad_maximum_fusion.2), channel_id=1, source_target_pairs={{0,1},{1,0},{2,3},{3,2},{4,5},{5,4},{6,7},{7,6},{8,9},{9,8},{10,11... | collective-permute-start | bytes 44 | tf_op jit(solution)/shard_map/ppermute | solution.py:63
  80.8 3.6 %collective-permute-start.7 = (f32[3]{0:T(128)S(1)}, f32[3]{0:T(128)S(1)}, u32[]{:S(2)}, u32[]{:S(2)}) collective-permute-start(f32[3]{0:T(128)S(1)} %add.74), channel_id=1, source_target_pairs={{0,2},{2,0},{4,6},{6,4},{8,10},{10,8},{12,14},{14,12},{1,3},{3,1},... | collective-permute-start | bytes 44 | tf_op jit(solution)/shard_map/ppermute | solution.py:63
  84.4 3.6 %collective-permute-start.8 = (f32[3]{0:T(128)S(1)}, f32[3]{0:T(128)S(1)}, u32[]{:S(2)}, u32[]{:S(2)}) collective-permute-start(f32[3]{0:T(128)S(1)} %add.75), channel_id=1, source_target_pairs={{0,4},{2,6},{4,0},{6,2},{8,12},{10,14},{12,8},{14,10},{1,5},{3,7},... | collective-permute-start | bytes 44 | tf_op jit(solution)/shard_map/ppermute | solution.py:63
  87.9 4.5 %collective-permute-start.9 = (f32[3]{0:T(128)S(1)}, f32[3]{0:T(128)S(1)}, u32[]{:S(2)}, u32[]{:S(2)}) collective-permute-start(f32[3]{0:T(128)S(1)} %add.76), channel_id=1, source_target_pairs={{0,8},{2,10},{4,12},{6,14},{8,0},{10,2},{12,4},{14,6},{1,9},{3,11}... | collective-permute-start | bytes 44 | tf_op jit(solution)/shard_map/ppermute | solution.py:63

commit v11 on v8

--- a/solution.py
+++ b/solution.py
@@ -244,7 +244,7 @@
     time_index = lax.axis_index("tm")
     row_index = lax.axis_index("row")
     ahead = (time_index + 1) % frame_count
-    at_end = lax.dynamic_index_in_dim(clip_start, ahead, 0, keepdims=False) == 1
+    at_end = jnp.sum(jnp.where(jnp.arange(frame_count) == ahead, clip_start, 0)) == 1
     later_band = jnp.where(at_end, own_band, shifted(own_band, "tm", -1))
     rim_rows = min(aspp_reach, band_rows)
     extra_rows = aspp_reach - rim_rows
@@ -317,7 +317,9 @@
         head_flat.reshape(band_rows, pitch, head_weight.shape[1])[:, pad_columns:], (2, 0, 1)
     )
     predictions = emit_heads(head_out, out_weight)
-    pixel = jnp.einsum("sk,khw->shw", inst_stats, onehot, precision=lax.Precision.HIGHEST)
+    pixel = jnp.sum(
+        jnp.where(onehot[None] > 0.5, inst_stats[:, :, None, None], 0.0), axis=1
+    )
     counts = jnp.where(counted, pixel[0], 1.0)
     centre_row = pixel[1] / counts
     centre_col = pixel[2] / counts

time: 94.2 us -> 93.3 us (level)
  other arithmetic: 11.6 us -> 15.1 us
  matrix products: 4.49 us -> 2.26 us
  local copies, waits for them, and re-layouts: 6.74 us -> 5.46 us
    dot_general x1 -> x0, matrix products: 2.23 us -> none  [shards(): jnp.einsum('sk,khw->shw', inst_stats, onehot, precision=lax.Precision.HIG...]
    reduce_sum x0 -> x2, other arithmetic: none -> 2.03 us  [the longest x1 1.29 us: shards(): jnp.sum(jnp.where(jnp.arange(frame_count) == ahead, clip_start, 0)) == 1]
    gt x0 -> x1, other arithmetic: none -> 1.28 us  [shards(): onehot[None] > 0.5]
    dynamic_slice x1 -> x0, local copies, waits for them, and re-layouts: 1.24 us -> none  [shards(): at_end = lax.dynamic_index_in_dim(clip_start, ahead, 0, keepdims=False) == 1]
  transfers between devices with their start and end apart: 10 -> 10, of which waited for: 6 -> 6; matrix products, arithmetic and copies ran while one was open for 13% -> 13% of each run, Pallas kernels for 16% -> 17%
where the time goes in v11:
time: 93.3 us; the launch traced here: 92.8 us
  Pallas kernels  45.9 us (49%)
  other arithmetic  15.1 us (16%)
  waiting for transfers between devices  12.9 us (14%)
  starting transfers between devices  7.75 us (8%)
  local copies, waits for them, and re-layouts  5.46 us (6%)
  between operations  3.5 us (4%)
  matrix products  2.26 us (2%)
    pallas_call x2, Pallas kernels, aspp_pass(): pl.pallas_call(body, out_shape=out_shape, in_specs=in_specs, out_specs=ou...  37.1 us
    ppermute x6, waiting for transfers between devices, all_sum(): other = lax.ppermute(value, axis, pairs)  12.4 us
    pallas_call x1, Pallas kernels, head_kernel_call(): pl.pallas_call(body, out_shape=jax.ShapeDtypeStruct((blocks * block, outp...  8.83 us
    ppermute x1, starting transfers between devices, shifted(): return lax.ppermute(value, axis, pairs)  6.09 us
    pad x2, local copies, waits for them, and re-layouts, flat_of(): jnp.pad(jnp.transpose(wide, (1, 2, 0)), ((1, 1), (pitch - columns, 0), (0...  3.66 us
    select_n x3, other arithmetic, with_rims(): jnp.where(first, lax.slice_in_dim(block, size - width, None, axis=dim), l...  2.26 us
    another operation x1, other arithmetic, shards(): jnp.stack([center_err, offset_err, counted_local])  2.06 us
    concatenate x1, other arithmetic, with_rims(): return jnp.concatenate([low, block, high], axis=dim)  2.04 us
  transfers between devices with their start and end apart: 10, of which 6 were waited for; matrix products, arithmetic and copies ran while one was open for 13% of the time, Pallas kernels for 17%

profile of v11, /device:TPU:0, one launch (start us, length us, event | category | flops | bytes accessed | tf_op | source)
XLA Modules:
  0.0 92.8 jit_solution(14595937413489610933)
XLA Ops:
  0.7 6.1 %collective-permute-start = (bf16[256,32,48]{0,2,1:T(8,128)(2,1)}, bf16[256,32,48]{0,2,1:T(8,128)(2,1)S(1)}, u32[]{:S(2)}, u32[]{:S(2)}) collective-permute-start(bf16[256,32,48]{0,2,1:T(8,128)(2,1)} %bitcast.90), channel_id=1, source_target_pairs={{0,14},{2,0},{4,2},{6,4},{8,6},{10,8},{12,10},{14,12},{1,15},{3,1}... | collective-permute-start | bytes 2359304 | tf_op jit(solution)/shard_map/ppermute | solution.py:51
  6.7 1.2 %slice_select_fusion = bf16[256,18,48]{0,2,1:T(8,128)(2,1)S(1)} fusion(bf16[256,32,48]{0,2,1:T(8,128)(2,1)} %bitcast.91, pred[]{:T(512)S(6)} %eq.35), kind=kLoop, calls=%fused_computation.19 | loop fusion | flops 221184 | bytes 1327105 | tf_op jit(solution)/shard_map/jit(_where)/select_n | solution.py:36
  8.0 0.7 and_bitcast_fusion
  8.8 1.3 %convert_reduce_fusion.2 = (f32[64]{0:T(128)S(1)}, f32[64]{0:T(128)S(1)}, f32[64]{0:T(128)S(1)}) fusion(s32[32,48]{1,0:T(8,128)} %bitcast.98, pred[32,48]{1,0:T(8,128)(4,1)S(1)} %get-tuple-element.12, f32[32]{0:T(128)S(1)} %add_convert_fusion), kind=kLoop, calls=%fused_computation.11 | loop fusion | flops 786240 | bytes 8576 | tf_op jit(solution)/shard_map/reduce_sum | solution.py:284
  10.7 1.3 %convert_compare_fusion = pred[64,32,48]{0,2,1:T(8,128)(4,1)S(1)} fusion(s32[32,48]{1,0:T(8,128)} %bitcast.99, pred[32,48]{1,0:T(8,128)(4,1)S(1)} %get-tuple-element.12), kind=kLoop, calls=%fused_computation.12 | loop fusion | flops 393216 | bytes 105984 | tf_op jit(solution)/shard_map/gt | solution.py:321
  12.0 0.9 fusion.6.rest_3_
  12.8 1.3 %fusion.17 = s32[]{:T(128)} fusion(s32[8]{0:T(128)} %param.11, s32[]{:T(128)S(6)} %select_n.92), kind=kLoop, calls=%fused_computation.59 | loop fusion | flops 23 | bytes 40 | tf_op jit(solution)/shard_map/reduce_sum | solution.py:247
  15.1 1.8 %pad.12 = bf16[70,80,256]{2,1,0:T(8,128)(2,1)} pad(bf16[68,48,256]{2,1,0:T(8,128)(2,1)S(1)} %maximum_bitcast_fusion.1, bf16[]{:T(256)} %constant.55.clone.1), padding=1_1x32_0x0_0 | pad | bytes 4538370 | tf_op jit(solution)/shard_map/jit(_pad)/pad | solution.py:263
  16.9 15.3 %shard_map.113.rest_0_ = f32[4,2560,256]{2,1,0:T(8,128)} custom-call(bf16[5600,256]{1,0:T(8,128)(2,1)} %bitcast.94, bf16[256,512]{1,0:T(8,128)(2,1)} %point_ref.3, bf16[3,9,256,512]{3,2,1,0:T(8,128)(2,1)} %dilated_ref.3), custom_call_target="tpu_custom_call" | custom-call | flops 9395240960 | bytes 16891904 | tf_op jit(solution)/shard_map/pallas_call | solution.py:159
  34.2 1.7 %fusion.12.rest_2_ = f32[1,256]{1,0:T(1,128)} fusion(bf16[256,1]{0,1:T(2,128)(2,1)S(1)} %reshape.77, bf16[256,1280]{1,0:T(8,128)(2,1)} %rest_1_.1), kind=kOutput, calls=%fused_computation.37 | convolution fusion | flops 131072 | bytes 132608 | tf_op jit(solution)/shard_map/dot_general | solution.py:297
  36.1 1.8 %pad.11 = bf16[70,80,256]{2,1,0:T(8,128)(2,1)} pad(bf16[68,48,256]{2,1,0:T(8,128)(2,1)S(1)} %maximum_bitcast_fusion, bf16[]{:T(256)} %constant.55.clone.1), padding=1_1x32_0x0_0 | pad | bytes 4538370 | tf_op jit(solution)/shard_map/jit(_pad)/pad | solution.py:263
  37.9 21.7 %shard_map.114 = f32[2560,256]{1,0:T(8,128)} custom-call(bf16[5600,256]{1,0:T(8,128)(2,1)} %bitcast.93, bf16[256,512]{1,0:T(8,128)(2,1)} %point_ref.3, bf16[3,9,256,512]{3,2,1,0:T(8,128)(2,1)} %dilated_ref.3, f32[4,2560,256]{2,1,0:T(8,128)} %shard_map.113.rest_0_, bf16[256,1280]{1,0:T(8,128)(2,1)} %rest_1_.1, f32[1,256]{1,0:T(1,128)} %fusion.12.rest_2_, ...), custom_call_target="tpu_custom_call" | custom-call | flops 10737418240 | bytes 16891904 | tf_op jit(solution)/shard_map/pallas_call | solution.py:159
  59.7 1.0 %slice_select_fusion.2 = f32[160,256]{1,0:T(8,128)S(1)} fusion(f32[2560,256]{1,0:T(8,128)} %shard_map.114, pred[]{:T(512)S(6)} %eq.35), kind=kLoop, calls=%fused_computation.36 | loop fusion | flops 40960 | bytes 491521 | tf_op jit(solution)/shard_map/jit(_where)/select_n | solution.py:36
  60.9 0.7 select_reduce_fusion
  62.2 2.0 %select_maximum_fusion.x_ref = f32[3040,256]{1,0:T(8,128)S(1)} fusion(f32[160,256]{1,0:T(8,128)S(1)} %get-tuple-element.22, f32[2560,256]{1,0:T(8,128)} %shard_map.114, f32[160,256]{1,0:T(8,128)S(1)} %get-tuple-element.21), kind=kLoop, calls=%fused_computation.2 | loop fusion | flops 6225920 | bytes 6062080 | tf_op jit(solution)/shard_map/concatenate | solution.py:45
  64.2 8.8 %shard_map.115 = bf16[2560,96]{1,0:T(8,128)(2,1)S(1)} custom-call(f32[3040,256]{1,0:T(8,128)S(1)} %select_maximum_fusion.x_ref, bf16[25,96,256]{2,1,0:T(8,128)(2,1)S(1)} %copy-done.1), custom_call_target="tpu_custom_call" | custom-call | flops 3145728000 | bytes 4833280 | tf_op jit(solution)/shard_map/pallas_call | solution.py:198
  74.0 0.8 multiply_reduce_fusion
  74.8 2.1 %pad_maximum_fusion.2 = f32[3]{0:T(128)S(1)} fusion(f32[1]{0:T(128)} %bitcast.35, f32[1]{0:T(128)} %bitcast.34, f32[1]{0:T(128)} %bitcast.31), kind=kLoop, calls=%fused_computation.60 | loop fusion | flops 6 | bytes 24 | tf_op jit(solution)/shard_map/stack | solution.py:340
  77.1 0.6 copy.19
  78.0 3.6 %collective-permute-done.7 = f32[3]{0:T(128)S(1)} collective-permute-done((f32[3]{0:T(128)S(1)}, f32[3]{0:T(128)S(1)}, u32[]{:S(2)}, u32[]{:S(2)}) %collective-permute-start.7) | collective-permute-done | bytes 44 | tf_op jit(solution)/shard_map/ppermute | solution.py:63
  81.6 3.6 %collective-permute-done.8 = f32[3]{0:T(128)S(1)} collective-permute-done((f32[3]{0:T(128)S(1)}, f32[3]{0:T(128)S(1)}, u32[]{:S(2)}, u32[]{:S(2)}) %collective-permute-start.8) | collective-permute-done | bytes 44 | tf_op jit(solution)/shard_map/ppermute | solution.py:63
  85.2 4.5 %collective-permute-done.9 = f32[3]{0:T(128)S(1)} collective-permute-done((f32[3]{0:T(128)S(1)}, f32[3]{0:T(128)S(1)}, u32[]{:S(2)}, u32[]{:S(2)}) %collective-permute-start.9) | collective-permute-done | bytes 44 | tf_op jit(solution)/shard_map/ppermute | solution.py:63
  89.6 0.7 fusion.26
  92.2 0.6 pad_maximum_fusion.3
  (53 shorter events, 5.2 us)
Async XLA Ops:
  0.6 33.3 %copy-start = (bf16[256,512]{1,0:T(8,128)(2,1)S(1)}, bf16[256,512]{1,0:T(8,128)(2,1)}, u32[]{:S(2)}) copy-start(bf16[256,512]{1,0:T(8,128)(2,1)} %param.16) | copy-start | bytes 786436
  0.6 14.2 %copy-start.2 = (bf16[1,256,32,48]{1,3,2,0:T(8,128)(2,1)S(1)}, bf16[1,256,32,48]{1,3,2,0:T(8,128)(2,1)}, u32[]{:S(2)}) copy-start(bf16[1,256,32,48]{1,3,2,0:T(8,128)(2,1)} %param.10) | copy-start | bytes 2359300
  0.7 31.6 %collective-permute-start = (bf16[256,32,48]{0,2,1:T(8,128)(2,1)}, bf16[256,32,48]{0,2,1:T(8,128)(2,1)S(1)}, u32[]{:S(2)}, u32[]{:S(2)}) collective-permute-start(bf16[256,32,48]{0,2,1:T(8,128)(2,1)} %bitcast.90), channel_id=1, source_target_pairs={{0,14},{2,0},{4,2},{6,4},{8,6},{10,8},{12,10},{14,12},{1,15},{3,1}... | collective-permute-start | bytes 2359304 | tf_op jit(solution)/shard_map/ppermute | solution.py:51
  7.9 6.9 %collective-permute-start.2 = (bf16[256,18,48]{0,2,1:T(8,128)(2,1)S(1)}, bf16[256,18,48]{0,2,1:T(8,128)(2,1)S(1)}, u32[]{:S(2)}, u32[]{:S(2)}) collective-permute-start(bf16[256,18,48]{0,2,1:T(8,128)(2,1)S(1)} %slice_select_fusion), channel_id=1, source_target_pairs={{0,1},{1,0},{2,3},{3,2},{4,5},{5,4},{6,7},{7,6},{8,9},{9,8},{10,11... | collective-permute-start | bytes 1327112 | tf_op jit(solution)/shard_map/ppermute | solution.py:41
  10.1 4.7 %collective-permute-start.5 = (f32[3,64]{1,0:T(4,128)S(1)}, f32[3,64]{1,0:T(4,128)S(1)}, u32[]{:S(2)}, u32[]{:S(2)}) collective-permute-start(f32[3,64]{1,0:T(4,128)S(1)} %pad_maximum_fusion.1), channel_id=1, source_target_pairs={{0,1},{1,0},{2,3},{3,2},{4,5},{5,4},{6,7},{7,6},{8,9},{9,8},{10,11... | collective-permute-start | bytes 2312 | tf_op jit(solution)/shard_map/ppermute | solution.py:63
  32.7 1.2 %collective-permute-start.3 = (f32[512]{0:T(512)S(1)}, f32[512]{0:T(512)S(1)}, u32[]{:S(2)}, u32[]{:S(2)}) collective-permute-start(f32[512]{0:T(512)S(1)} %pad_maximum_fusion), channel_id=1, source_target_pairs={{0,1},{1,0},{2,3},{3,2},{4,5},{5,4},{6,7},{7,6},{8,9},{9,8},{10,11... | collective-permute-start | bytes 6152 | tf_op jit(solution)/shard_map/ppermute | solution.py:63
  32.9 2.9 %collective-permute-start.1 = (bf16[256,18,48]{0,2,1:T(8,128)(2,1)S(1)}, bf16[256,18,48]{0,2,1:T(8,128)(2,1)S(1)}, u32[]{:S(2)}, u32[]{:S(2)}) collective-permute-start(bf16[256,18,48]{0,2,1:T(8,128)(2,1)S(1)} %slice_select_fusion.1), channel_id=1, source_target_pairs={{0,1},{1,0},{2,3},{3,2},{4,5},{5,4},{6,7},{7,6},{8,9},{9,8},{10,11... | collective-permute-start | bytes 1327112 | tf_op jit(solution)/shard_map/ppermute | solution.py:41
  60.7 1.5 %collective-permute-start.4 = (f32[160,256]{1,0:T(8,128)S(1)}, f32[160,256]{1,0:T(8,128)S(1)}, u32[]{:S(2)}, u32[]{:S(2)}) collective-permute-start(f32[160,256]{1,0:T(8,128)S(1)} %slice_select_fusion.2), channel_id=1, source_target_pairs={{0,1},{1,0},{2,3},{3,2},{4,5},{5,4},{6,7},{7,6},{8,9},{9,8},{10,11... | collective-permute-start | bytes 491528 | tf_op jit(solution)/shard_map/ppermute | solution.py:41
  62.2 2.1 %copy-start.1 = (bf16[25,96,256]{2,1,0:T(8,128)(2,1)S(1)}, bf16[25,96,256]{2,1,0:T(8,128)(2,1)}, u32[]{:S(2)}) copy-start(bf16[25,96,256]{2,1,0:T(8,128)(2,1)} %weight_ref.1) | copy-start | bytes 3686404
  64.2 9.3 %copy-start.4 = (bf16[4,32]{1,0:T(4,128)(2,1)S(1)}, bf16[4,32]{1,0:T(4,128)(2,1)}, u32[]{:S(2)}) copy-start(bf16[4,32]{1,0:T(4,128)(2,1)} %param.19) | copy-start | bytes 772
  73.1 0.9 copy-start.3
  76.8 1.2 %collective-permute-start.6 = (f32[3]{0:T(128)S(1)}, f32[3]{0:T(128)S(1)}, u32[]{:S(2)}, u32[]{:S(2)}) collective-permute-start(f32[3]{0:T(128)S(1)} %pad_maximum_fusion.2), channel_id=1, source_target_pairs={{0,1},{1,0},{2,3},{3,2},{4,5},{5,4},{6,7},{7,6},{8,9},{9,8},{10,11... | collective-permute-start | bytes 44 | tf_op jit(solution)/shard_map/ppermute | solution.py:63
  78.0 3.6 %collective-permute-start.7 = (f32[3]{0:T(128)S(1)}, f32[3]{0:T(128)S(1)}, u32[]{:S(2)}, u32[]{:S(2)}) collective-permute-start(f32[3]{0:T(128)S(1)} %add.69), channel_id=1, source_target_pairs={{0,2},{2,0},{4,6},{6,4},{8,10},{10,8},{12,14},{14,12},{1,3},{3,1},... | collective-permute-start | bytes 44 | tf_op jit(solution)/shard_map/ppermute | solution.py:63
  81.6 3.6 %collective-permute-start.8 = (f32[3]{0:T(128)S(1)}, f32[3]{0:T(128)S(1)}, u32[]{:S(2)}, u32[]{:S(2)}) collective-permute-start(f32[3]{0:T(128)S(1)} %add.70), channel_id=1, source_target_pairs={{0,4},{2,6},{4,0},{6,2},{8,12},{10,14},{12,8},{14,10},{1,5},{3,7},... | collective-permute-start | bytes 44 | tf_op jit(solution)/shard_map/ppermute | solution.py:63
  85.2 4.5 %collective-permute-start.9 = (f32[3]{0:T(128)S(1)}, f32[3]{0:T(128)S(1)}, u32[]{:S(2)}, u32[]{:S(2)}) collective-permute-start(f32[3]{0:T(128)S(1)} %add.71), channel_id=1, source_target_pairs={{0,8},{2,10},{4,12},{6,14},{8,0},{10,2},{12,4},{14,6},{1,9},{3,11}... | collective-permute-start | bytes 44 | tf_op jit(solution)/shard_map/ppermute | solution.py:63

commit v12 on v11

--- a/solution.py
+++ b/solution.py
@@ -33,11 +33,7 @@
         return padded_2(block, ((axis, dim),), width)
     first = lax.axis_index(axis) == 0
     size = block.shape[dim]
-    sent = jnp.where(
-        first,
-        lax.slice_in_dim(block, size - width, None, axis=dim),
-        lax.slice_in_dim(block, 0, width, axis=dim),
-    )
+    sent = lax.dynamic_slice_in_dim(block, jnp.where(first, size - width, 0), width, axis=dim)
     got = lax.ppermute(sent, axis, [(0, 1), (1, 0)])
     empty = jnp.zeros_like(got)
     low = jnp.where(first, empty, got)

time: 93.3 us -> 93.1 us (level)
  other arithmetic: 15.1 us -> 12.8 us
  local copies, waits for them, and re-layouts: 5.46 us -> 7.5 us
    select_n x3 -> x0, other arithmetic: 2.26 us -> none  [with_rims(): jnp.where(first, lax.slice_in_dim(block, size - width, None, axis=dim), l...]
    dynamic_slice x0 -> x3, local copies, waits for them, and re-layouts: none -> 2.04 us  [with_rims(): lax.dynamic_slice_in_dim(block, jnp.where(first, size - width, 0), width,...]
where the time goes in v12:
time: 93.1 us; the launch traced here: 92.6 us
  Pallas kernels  45.9 us (49%)
  waiting for transfers between devices  13 us (14%)
  other arithmetic  12.8 us (14%)
  starting transfers between devices  7.73 us (8%)
  local copies, waits for them, and re-layouts  7.5 us (8%)
  between operations  3.5 us (4%)
  matrix products  2.26 us (2%)
    pallas_call x2, Pallas kernels, aspp_pass(): pl.pallas_call(body, out_shape=out_shape, in_specs=in_specs, out_specs=ou...  37.1 us
    ppermute x6, waiting for transfers between devices, all_sum(): other = lax.ppermute(value, axis, pairs)  12.5 us
    pallas_call x1, Pallas kernels, head_kernel_call(): pl.pallas_call(body, out_shape=jax.ShapeDtypeStruct((blocks * block, outp...  8.82 us
    ppermute x1, starting transfers between devices, shifted(): return lax.ppermute(value, axis, pairs)  6.09 us
    pad x2, local copies, waits for them, and re-layouts, flat_of(): jnp.pad(jnp.transpose(wide, (1, 2, 0)), ((1, 1), (pitch - columns, 0), (0...  3.66 us
    another operation x1, other arithmetic, shards(): jnp.stack([center_err, offset_err, counted_local])  2.06 us
    dynamic_slice x3, local copies, waits for them, and re-layouts, with_rims(): lax.dynamic_slice_in_dim(block, jnp.where(first, size - width, 0), width,...  2.04 us
    concatenate x1, other arithmetic, with_rims(): return jnp.concatenate([low, block, high], axis=dim)  2.04 us
  transfers between devices with their start and end apart: 10, of which 6 were waited for; matrix products, arithmetic and copies ran while one was open for 13% of the time, Pallas kernels for 17%

profile of v12, /device:TPU:0, one launch (start us, length us, event | category | flops | bytes accessed | tf_op | source)
XLA Modules:
  0.0 92.6 jit_solution(9492557023455643803)
XLA Ops:
  0.7 6.1 %collective-permute-start = (bf16[256,32,48]{0,2,1:T(8,128)(2,1)}, bf16[256,32,48]{0,2,1:T(8,128)(2,1)S(1)}, u32[]{:S(2)}, u32[]{:S(2)}) collective-permute-start(bf16[256,32,48]{0,2,1:T(8,128)(2,1)} %bitcast.92), channel_id=1, source_target_pairs={{0,14},{2,0},{4,2},{6,4},{8,6},{10,8},{12,10},{14,12},{1,15},{3,1}... | collective-permute-start | bytes 2359304 | tf_op jit(solution)/shard_map/ppermute | solution.py:47
  6.7 1.1 %dynamic-slice_bitcast_fusion = bf16[256,18,48]{0,2,1:T(8,128)(2,1)S(1)} fusion(bf16[1,256,32,48]{1,3,2,0:T(8,128)(2,1)} %param.10, s32[]{:T(128)S(6)} %select_n.95), kind=kLoop, calls=%fused_computation.19 | loop fusion | bytes 884740 | tf_op jit(solution)/shard_map/dynamic_slice | solution.py:36
  7.9 0.7 and_bitcast_fusion
  8.7 1.3 %convert_reduce_fusion.2 = (f32[64]{0:T(128)S(1)}, f32[64]{0:T(128)S(1)}, f32[64]{0:T(128)S(1)}) fusion(s32[32,48]{1,0:T(8,128)} %bitcast.99, pred[32,48]{1,0:T(8,128)(4,1)S(1)} %get-tuple-element.12, f32[32]{0:T(128)S(1)} %add_convert_fusion), kind=kLoop, calls=%fused_computation.11 | loop fusion | flops 786240 | bytes 8576 | tf_op jit(solution)/shard_map/reduce_sum | solution.py:280
  10.6 1.3 %convert_compare_fusion = pred[64,32,48]{0,2,1:T(8,128)(4,1)S(1)} fusion(s32[32,48]{1,0:T(8,128)} %bitcast.100, pred[32,48]{1,0:T(8,128)(4,1)S(1)} %get-tuple-element.12), kind=kLoop, calls=%fused_computation.12 | loop fusion | flops 393216 | bytes 105984 | tf_op jit(solution)/shard_map/gt | solution.py:317
  11.9 0.9 fusion.6.rest_3_
  12.7 1.3 %fusion.17 = s32[]{:T(128)} fusion(s32[8]{0:T(128)} %param.11, s32[]{:T(128)S(6)} %select_n.91), kind=kLoop, calls=%fused_computation.59 | loop fusion | flops 23 | bytes 40 | tf_op jit(solution)/shard_map/reduce_sum | solution.py:243
  15.0 1.8 %pad.12 = bf16[70,80,256]{2,1,0:T(8,128)(2,1)} pad(bf16[68,48,256]{2,1,0:T(8,128)(2,1)S(1)} %maximum_bitcast_fusion.1, bf16[]{:T(256)} %constant.61.clone.1), padding=1_1x32_0x0_0 | pad | bytes 4538370 | tf_op jit(solution)/shard_map/jit(_pad)/pad | solution.py:259
  16.8 15.3 %shard_map.113.rest_0_ = f32[4,2560,256]{2,1,0:T(8,128)} custom-call(bf16[5600,256]{1,0:T(8,128)(2,1)} %bitcast.95, bf16[256,512]{1,0:T(8,128)(2,1)} %point_ref.3, bf16[3,9,256,512]{3,2,1,0:T(8,128)(2,1)} %dilated_ref.3), custom_call_target="tpu_custom_call" | custom-call | flops 9395240960 | bytes 16891904 | tf_op jit(solution)/shard_map/pallas_call | solution.py:155
  34.1 1.7 %fusion.12.rest_2_ = f32[1,256]{1,0:T(1,128)} fusion(bf16[256,1]{0,1:T(2,128)(2,1)S(1)} %reshape.78, bf16[256,1280]{1,0:T(8,128)(2,1)} %rest_1_.1), kind=kOutput, calls=%fused_computation.35 | convolution fusion | flops 131072 | bytes 132608 | tf_op jit(solution)/shard_map/dot_general | solution.py:293
  36.0 1.8 %pad.11 = bf16[70,80,256]{2,1,0:T(8,128)(2,1)} pad(bf16[68,48,256]{2,1,0:T(8,128)(2,1)S(1)} %maximum_bitcast_fusion, bf16[]{:T(256)} %constant.61.clone.1), padding=1_1x32_0x0_0 | pad | bytes 4538370 | tf_op jit(solution)/shard_map/jit(_pad)/pad | solution.py:259
  37.8 21.7 %shard_map.114 = f32[2560,256]{1,0:T(8,128)} custom-call(bf16[5600,256]{1,0:T(8,128)(2,1)} %bitcast.94, bf16[256,512]{1,0:T(8,128)(2,1)} %point_ref.3, bf16[3,9,256,512]{3,2,1,0:T(8,128)(2,1)} %dilated_ref.3, f32[4,2560,256]{2,1,0:T(8,128)} %shard_map.113.rest_0_, bf16[256,1280]{1,0:T(8,128)(2,1)} %rest_1_.1, f32[1,256]{1,0:T(1,128)} %fusion.12.rest_2_, ...), custom_call_target="tpu_custom_call" | custom-call | flops 10737418240 | bytes 16891904 | tf_op jit(solution)/shard_map/pallas_call | solution.py:155
  59.6 0.9 %constant_dynamic-slice_fusion = f32[160,256]{1,0:T(8,128)S(1)} fusion(f32[2560,256]{1,0:T(8,128)} %shard_map.114, s32[]{:T(128)S(6)} %select_n.101), kind=kLoop, calls=%fused_computation.57 | loop fusion | bytes 327684 | tf_op jit(solution)/shard_map/dynamic_slice | solution.py:36
  60.7 0.7 select_reduce_fusion
  62.0 2.0 %select_maximum_fusion.x_ref = f32[3040,256]{1,0:T(8,128)S(1)} fusion(f32[160,256]{1,0:T(8,128)S(1)} %get-tuple-element.22, f32[2560,256]{1,0:T(8,128)} %shard_map.114, f32[160,256]{1,0:T(8,128)S(1)} %get-tuple-element.21), kind=kLoop, calls=%fused_computation.2 | loop fusion | flops 6225920 | bytes 6062080 | tf_op jit(solution)/shard_map/concatenate | solution.py:41
  64.1 8.8 %shard_map.115 = bf16[2560,96]{1,0:T(8,128)(2,1)S(1)} custom-call(f32[3040,256]{1,0:T(8,128)S(1)} %select_maximum_fusion.x_ref, bf16[25,96,256]{2,1,0:T(8,128)(2,1)S(1)} %copy-done.1), custom_call_target="tpu_custom_call" | custom-call | flops 3145728000 | bytes 4833280 | tf_op jit(solution)/shard_map/pallas_call | solution.py:194
  73.8 0.8 multiply_reduce_fusion
  74.6 2.1 %pad_maximum_fusion.2 = f32[3]{0:T(128)S(1)} fusion(f32[1]{0:T(128)} %bitcast.36, f32[1]{0:T(128)} %bitcast.35, f32[1]{0:T(128)} %bitcast.32), kind=kLoop, calls=%fused_computation.60 | loop fusion | flops 6 | bytes 24 | tf_op jit(solution)/shard_map/stack | solution.py:336
  76.9 0.6 copy.19
  77.8 3.6 %collective-permute-done.7 = f32[3]{0:T(128)S(1)} collective-permute-done((f32[3]{0:T(128)S(1)}, f32[3]{0:T(128)S(1)}, u32[]{:S(2)}, u32[]{:S(2)}) %collective-permute-start.7) | collective-permute-done | bytes 44 | tf_op jit(solution)/shard_map/ppermute | solution.py:59
  81.4 3.6 %collective-permute-done.8 = f32[3]{0:T(128)S(1)} collective-permute-done((f32[3]{0:T(128)S(1)}, f32[3]{0:T(128)S(1)}, u32[]{:S(2)}, u32[]{:S(2)}) %collective-permute-start.8) | collective-permute-done | bytes 44 | tf_op jit(solution)/shard_map/ppermute | solution.py:59
  85.0 4.5 %collective-permute-done.9 = f32[3]{0:T(128)S(1)} collective-permute-done((f32[3]{0:T(128)S(1)}, f32[3]{0:T(128)S(1)}, u32[]{:S(2)}, u32[]{:S(2)}) %collective-permute-start.9) | collective-permute-done | bytes 44 | tf_op jit(solution)/shard_map/ppermute | solution.py:59
  89.5 0.7 fusion.26
  92.1 0.6 pad_maximum_fusion.3
  (53 shorter events, 5.2 us)
Async XLA Ops:
  0.6 33.2 %copy-start = (bf16[256,512]{1,0:T(8,128)(2,1)S(1)}, bf16[256,512]{1,0:T(8,128)(2,1)}, u32[]{:S(2)}) copy-start(bf16[256,512]{1,0:T(8,128)(2,1)} %param.16) | copy-start | bytes 786436
  0.6 14.1 %copy-start.2 = (bf16[1,256,32,48]{1,3,2,0:T(8,128)(2,1)S(1)}, bf16[1,256,32,48]{1,3,2,0:T(8,128)(2,1)}, u32[]{:S(2)}) copy-start(bf16[1,256,32,48]{1,3,2,0:T(8,128)(2,1)} %param.10) | copy-start | bytes 2359300
  0.7 31.5 %collective-permute-start = (bf16[256,32,48]{0,2,1:T(8,128)(2,1)}, bf16[256,32,48]{0,2,1:T(8,128)(2,1)S(1)}, u32[]{:S(2)}, u32[]{:S(2)}) collective-permute-start(bf16[256,32,48]{0,2,1:T(8,128)(2,1)} %bitcast.92), channel_id=1, source_target_pairs={{0,14},{2,0},{4,2},{6,4},{8,6},{10,8},{12,10},{14,12},{1,15},{3,1}... | collective-permute-start | bytes 2359304 | tf_op jit(solution)/shard_map/ppermute | solution.py:47
  7.8 6.9 %collective-permute-start.2 = (bf16[256,18,48]{0,2,1:T(8,128)(2,1)S(1)}, bf16[256,18,48]{0,2,1:T(8,128)(2,1)S(1)}, u32[]{:S(2)}, u32[]{:S(2)}) collective-permute-start(bf16[256,18,48]{0,2,1:T(8,128)(2,1)S(1)} %dynamic-slice_bitcast_fusion), channel_id=1, source_target_pairs={{0,1},{1,0},{2,3},{3,2},{4,5},{5,4},{6,7},{7,6},{8,9},{9,8},{10,11... | collective-permute-start | bytes 1327112 | tf_op jit(solution)/shard_map/ppermute | solution.py:37
  10.0 4.7 %collective-permute-start.5 = (f32[3,64]{1,0:T(4,128)S(1)}, f32[3,64]{1,0:T(4,128)S(1)}, u32[]{:S(2)}, u32[]{:S(2)}) collective-permute-start(f32[3,64]{1,0:T(4,128)S(1)} %pad_maximum_fusion.1), channel_id=1, source_target_pairs={{0,1},{1,0},{2,3},{3,2},{4,5},{5,4},{6,7},{7,6},{8,9},{9,8},{10,11... | collective-permute-start | bytes 2312 | tf_op jit(solution)/shard_map/ppermute | solution.py:59
  32.6 1.2 %collective-permute-start.3 = (f32[512]{0:T(512)S(1)}, f32[512]{0:T(512)S(1)}, u32[]{:S(2)}, u32[]{:S(2)}) collective-permute-start(f32[512]{0:T(512)S(1)} %pad_maximum_fusion), channel_id=1, source_target_pairs={{0,1},{1,0},{2,3},{3,2},{4,5},{5,4},{6,7},{7,6},{8,9},{9,8},{10,11... | collective-permute-start | bytes 6152 | tf_op jit(solution)/shard_map/ppermute | solution.py:59
  32.7 3.0 %collective-permute-start.1 = (bf16[256,18,48]{0,2,1:T(8,128)(2,1)S(1)}, bf16[256,18,48]{0,2,1:T(8,128)(2,1)S(1)}, u32[]{:S(2)}, u32[]{:S(2)}) collective-permute-start(bf16[256,18,48]{0,2,1:T(8,128)(2,1)S(1)} %constant_dynamic-slice_fusion.1), channel_id=1, source_target_pairs={{0,1},{1,0},{2,3},{3,2},{4,5},{5,4},{6,7},{7,6},{8,9},{9,8},{10,11... | collective-permute-start | bytes 1327112 | tf_op jit(solution)/shard_map/ppermute | solution.py:37
  60.5 1.5 %collective-permute-start.4 = (f32[160,256]{1,0:T(8,128)S(1)}, f32[160,256]{1,0:T(8,128)S(1)}, u32[]{:S(2)}, u32[]{:S(2)}) collective-permute-start(f32[160,256]{1,0:T(8,128)S(1)} %constant_dynamic-slice_fusion), channel_id=1, source_target_pairs={{0,1},{1,0},{2,3},{3,2},{4,5},{5,4},{6,7},{7,6},{8,9},{9,8},{10,11... | collective-permute-start | bytes 491528 | tf_op jit(solution)/shard_map/ppermute | solution.py:37
  62.0 2.1 %copy-start.1 = (bf16[25,96,256]{2,1,0:T(8,128)(2,1)S(1)}, bf16[25,96,256]{2,1,0:T(8,128)(2,1)}, u32[]{:S(2)}) copy-start(bf16[25,96,256]{2,1,0:T(8,128)(2,1)} %weight_ref.1) | copy-start | bytes 3686404
  64.1 9.2 %copy-start.4 = (bf16[4,32]{1,0:T(4,128)(2,1)S(1)}, bf16[4,32]{1,0:T(4,128)(2,1)}, u32[]{:S(2)}) copy-start(bf16[4,32]{1,0:T(4,128)(2,1)} %param.19) | copy-start | bytes 772
  72.9 0.9 copy-start.3
  76.7 1.2 %collective-permute-start.6 = (f32[3]{0:T(128)S(1)}, f32[3]{0:T(128)S(1)}, u32[]{:S(2)}, u32[]{:S(2)}) collective-permute-start(f32[3]{0:T(128)S(1)} %pad_maximum_fusion.2), channel_id=1, source_target_pairs={{0,1},{1,0},{2,3},{3,2},{4,5},{5,4},{6,7},{7,6},{8,9},{9,8},{10,11... | collective-permute-start | bytes 44 | tf_op jit(solution)/shard_map/ppermute | solution.py:59
  77.8 3.6 %collective-permute-start.7 = (f32[3]{0:T(128)S(1)}, f32[3]{0:T(128)S(1)}, u32[]{:S(2)}, u32[]{:S(2)}) collective-permute-start(f32[3]{0:T(128)S(1)} %add.72), channel_id=1, source_target_pairs={{0,2},{2,0},{4,6},{6,4},{8,10},{10,8},{12,14},{14,12},{1,3},{3,1},... | collective-permute-start | bytes 44 | tf_op jit(solution)/shard_map/ppermute | solution.py:59
  81.4 3.6 %collective-permute-start.8 = (f32[3]{0:T(128)S(1)}, f32[3]{0:T(128)S(1)}, u32[]{:S(2)}, u32[]{:S(2)}) collective-permute-start(f32[3]{0:T(128)S(1)} %add.73), channel_id=1, source_target_pairs={{0,4},{2,6},{4,0},{6,2},{8,12},{10,14},{12,8},{14,10},{1,5},{3,7},... | collective-permute-start | bytes 44 | tf_op jit(solution)/shard_map/ppermute | solution.py:59
  85.0 4.5 %collective-permute-start.9 = (f32[3]{0:T(128)S(1)}, f32[3]{0:T(128)S(1)}, u32[]{:S(2)}, u32[]{:S(2)}) collective-permute-start(f32[3]{0:T(128)S(1)} %add.74), channel_id=1, source_target_pairs={{0,8},{2,10},{4,12},{6,14},{8,0},{10,2},{12,4},{14,6},{1,9},{3,11}... | collective-permute-start | bytes 44 | tf_op jit(solution)/shard_map/ppermute | solution.py:59

commit v13 on v11

--- a/solution.py
+++ b/solution.py
@@ -135,8 +135,8 @@
                 )
                 mixed = term if mixed is None else mixed + term
             mixed = mixed + pool_ref[...]
-            rounded = relu_bf16(mixed).astype(jnp.float32)
-            out_ref[rows, :] = jnp.where(keep_ref[...] > 0.5, rounded, 0.0)
+            rounded = relu_bf16(mixed)
+            out_ref[rows, :] = jnp.where(keep_ref[...] > 0.5, rounded, jnp.zeros_like(rounded))
         if not finish:
             for index in range(blocks):
                 block_copy(index).wait()
@@ -149,7 +149,7 @@
     scratch = [pltpu.VMEM(sums_shape, jnp.float32), pltpu.SemaphoreType.DMA((blocks,))]
     if finish:
         flops += 2 * blocks * block * branches * width * width
-        out_shape = jax.ShapeDtypeStruct((blocks * block, width), jnp.float32)
+        out_shape = jax.ShapeDtypeStruct((blocks * block, width), jnp.bfloat16)
         in_specs = [vmem, vmem, vmem, hbm, vmem, vmem, vmem]
         out_specs = vmem
     else:
@@ -187,7 +187,7 @@
                 for lateral in range(side):
                     shift = (vertical - reach) * pitch + (lateral - reach)
                     term = lax.dot_general(
-                        x_ref[pl.ds(base + shift, block), :].astype(jnp.bfloat16),
+                        x_ref[pl.ds(base + shift, block), :],
                         weight_ref[side * vertical + lateral],
                         contract,
                         preferred_element_type=jnp.float32,
@@ -202,7 +202,7 @@
         cost_estimate=pl.CostEstimate(
             flops=2 * blocks * block * x.shape[1] * outputs * side * side,
             transcendentals=0,
-            bytes_accessed=x.size * 4 + head_weight.size * 2 + blocks * block * outputs * 2,
+            bytes_accessed=x.size * 2 + head_weight.size * 2 + blocks * block * outputs * 2,
         ),
     )(x, head_weight)
 

time: 93.3 us -> 91.7 us (0.983)
  other arithmetic: 15.1 us -> 13.7 us
where the time goes in v13:
time: 91.7 us; the launch traced here: 91.2 us
  Pallas kernels  45.5 us (50%)
  other arithmetic  13.7 us (15%)
  waiting for transfers between devices  12.7 us (14%)
  starting transfers between devices  7.85 us (9%)
  local copies, waits for them, and re-layouts  5.7 us (6%)
  between operations  3.51 us (4%)
  matrix products  2.25 us (2%)
    pallas_call x2, Pallas kernels, aspp_pass(): pl.pallas_call(body, out_shape=out_shape, in_specs=in_specs, out_specs=ou...  36.7 us
    ppermute x6, waiting for transfers between devices, all_sum(): other = lax.ppermute(value, axis, pairs)  12.3 us
    pallas_call x1, Pallas kernels, head_kernel_call(): pl.pallas_call(body, out_shape=jax.ShapeDtypeStruct((blocks * block, outp...  8.85 us
    ppermute x1, starting transfers between devices, shifted(): return lax.ppermute(value, axis, pairs)  6.09 us
    pad x2, local copies, waits for them, and re-layouts, flat_of(): jnp.pad(jnp.transpose(wide, (1, 2, 0)), ((1, 1), (pitch - columns, 0), (0...  3.66 us
    select_n x3, other arithmetic, with_rims(): jnp.where(first, lax.slice_in_dim(block, size - width, None, axis=dim), l...  2.18 us
    another operation x1, other arithmetic, shards(): jnp.stack([center_err, offset_err, counted_local])  2.06 us
  transfers between devices with their start and end apart: 10, of which 6 were waited for; matrix products, arithmetic and copies ran while one was open for 13% of the time, Pallas kernels for 17%

profile of v13, /device:TPU:0, one launch (start us, length us, event | category | flops | bytes accessed | tf_op | source)
XLA Modules:
  0.0 91.2 jit_solution(8138797371959322987)
XLA Ops:
  0.7 6.1 %collective-permute-start = (bf16[256,32,48]{0,2,1:T(8,128)(2,1)}, bf16[256,32,48]{0,2,1:T(8,128)(2,1)S(1)}, u32[]{:S(2)}, u32[]{:S(2)}) collective-permute-start(bf16[256,32,48]{0,2,1:T(8,128)(2,1)} %bitcast.90), channel_id=1, source_target_pairs={{0,14},{2,0},{4,2},{6,4},{8,6},{10,8},{12,10},{14,12},{1,15},{3,1}... | collective-permute-start | bytes 2359304 | tf_op jit(solution)/shard_map/ppermute | solution.py:51
  6.8 1.2 %slice_select_fusion = bf16[256,18,48]{0,2,1:T(8,128)(2,1)S(1)} fusion(bf16[256,32,48]{0,2,1:T(8,128)(2,1)} %bitcast.91, pred[]{:T(512)S(6)} %eq.35), kind=kLoop, calls=%fused_computation.22 | loop fusion | flops 221184 | bytes 1327105 | tf_op jit(solution)/shard_map/jit(_where)/select_n | solution.py:36
  8.0 0.7 and_bitcast_fusion
  8.8 1.3 %convert_reduce_fusion.2 = (f32[64]{0:T(128)S(1)}, f32[64]{0:T(128)S(1)}, f32[64]{0:T(128)S(1)}) fusion(s32[32,48]{1,0:T(8,128)} %bitcast.98, pred[32,48]{1,0:T(8,128)(4,1)S(1)} %get-tuple-element.12, f32[32]{0:T(128)S(1)} %add_convert_fusion), kind=kLoop, calls=%fused_computation.14 | loop fusion | flops 786240 | bytes 8576 | tf_op jit(solution)/shard_map/reduce_sum | solution.py:284
  10.7 1.3 %convert_compare_fusion = pred[64,32,48]{0,2,1:T(8,128)(4,1)S(1)} fusion(s32[32,48]{1,0:T(8,128)} %bitcast.99, pred[32,48]{1,0:T(8,128)(4,1)S(1)} %get-tuple-element.12), kind=kLoop, calls=%fused_computation.15 | loop fusion | flops 393216 | bytes 105984 | tf_op jit(solution)/shard_map/gt | solution.py:321
  12.0 0.9 fusion.11.rest_3_
  12.9 0.6 fusion.22
  14.5 1.8 %pad.12 = bf16[70,80,256]{2,1,0:T(8,128)(2,1)} pad(bf16[68,48,256]{2,1,0:T(8,128)(2,1)S(1)} %maximum_bitcast_fusion.1, bf16[]{:T(256)} %constant.53.clone.1), padding=1_1x32_0x0_0 | pad | bytes 4538370 | tf_op jit(solution)/shard_map/jit(_pad)/pad | solution.py:263
  16.3 15.3 %shard_map.113.rest_0_ = f32[4,2560,256]{2,1,0:T(8,128)} custom-call(bf16[5600,256]{1,0:T(8,128)(2,1)} %bitcast.94, bf16[256,512]{1,0:T(8,128)(2,1)} %point_ref.3, bf16[3,9,256,512]{3,2,1,0:T(8,128)(2,1)} %dilated_ref.3), custom_call_target="tpu_custom_call" | custom-call | flops 9395240960 | bytes 16891904 | tf_op jit(solution)/shard_map/pallas_call | solution.py:159
  33.5 1.7 %fusion.17.rest_2_ = f32[1,256]{1,0:T(1,128)} fusion(bf16[256,1]{0,1:T(2,128)(2,1)S(1)} %reshape.77, bf16[256,1280]{1,0:T(8,128)(2,1)} %rest_1_.1), kind=kOutput, calls=%fused_computation.39 | convolution fusion | flops 131072 | bytes 132608 | tf_op jit(solution)/shard_map/dot_general | solution.py:297
  35.5 1.8 %pad.11 = bf16[70,80,256]{2,1,0:T(8,128)(2,1)} pad(bf16[68,48,256]{2,1,0:T(8,128)(2,1)S(1)} %maximum_bitcast_fusion, bf16[]{:T(256)} %constant.53.clone.1), padding=1_1x32_0x0_0 | pad | bytes 4538370 | tf_op jit(solution)/shard_map/jit(_pad)/pad | solution.py:263
  37.3 21.3 %shard_map.114 = bf16[2560,256]{1,0:T(8,128)(2,1)} custom-call(bf16[5600,256]{1,0:T(8,128)(2,1)} %bitcast.93, bf16[256,512]{1,0:T(8,128)(2,1)} %point_ref.3, bf16[3,9,256,512]{3,2,1,0:T(8,128)(2,1)} %dilated_ref.3, f32[4,2560,256]{2,1,0:T(8,128)} %shard_map.113.rest_0_, bf16[256,1280]{1,0:T(8,128)(2,1)} %rest_1_.1, f32[1,256]{1,0:T(1,128)} %fusion.17.rest_2_, ...), custom_call_target="tpu_custom_call" | custom-call | flops 10737418240 | bytes 16891904 | tf_op jit(solution)/shard_map/pallas_call | solution.py:159
  58.6 0.9 %slice_select_fusion.2 = bf16[160,256]{1,0:T(8,128)(2,1)S(1)} fusion(bf16[2560,256]{1,0:T(8,128)(2,1)} %shard_map.114, pred[]{:T(512)S(6)} %eq.35), kind=kLoop, calls=%fused_computation.41 | loop fusion | flops 40960 | bytes 245761 | tf_op jit(solution)/shard_map/jit(_where)/select_n | solution.py:36
  59.8 0.7 select_reduce_fusion
  60.9 1.4 %fusion.5.x_ref = bf16[3040,256]{1,0:T(8,128)(2,1)S(1)} fusion(bf16[160,256]{1,0:T(8,128)(2,1)S(1)} %get-tuple-element.22, bf16[2560,256]{1,0:T(8,128)(2,1)} %shard_map.114, bf16[160,256]{1,0:T(8,128)(2,1)S(1)} %get-tuple-element.21), kind=kLoop, calls=%fused_computation.12 | loop fusion | flops 9338880 | bytes 3031040 | tf_op jit(solution)/shard_map/concatenate | solution.py:45
  62.4 8.8 %shard_map.115 = bf16[2560,96]{1,0:T(8,128)(2,1)S(1)} custom-call(bf16[3040,256]{1,0:T(8,128)(2,1)S(1)} %fusion.5.x_ref, bf16[25,96,256]{2,1,0:T(8,128)(2,1)S(1)} %copy-done.1), custom_call_target="tpu_custom_call" | custom-call | flops 3145728000 | bytes 3276800 | tf_op jit(solution)/shard_map/pallas_call | solution.py:198
  72.4 0.8 multiply_reduce_fusion
  73.2 2.1 %pad_maximum_fusion.2 = f32[3]{0:T(128)S(1)} fusion(f32[1]{0:T(128)} %bitcast.35, f32[1]{0:T(128)} %bitcast.34, f32[1]{0:T(128)} %bitcast.31), kind=kLoop, calls=%fused_computation.63 | loop fusion | flops 6 | bytes 24 | tf_op jit(solution)/shard_map/stack | solution.py:340
  75.6 0.6 copy.19
  76.4 3.6 %collective-permute-done.7 = f32[3]{0:T(128)S(1)} collective-permute-done((f32[3]{0:T(128)S(1)}, f32[3]{0:T(128)S(1)}, u32[]{:S(2)}, u32[]{:S(2)}) %collective-permute-start.7) | collective-permute-done | bytes 44 | tf_op jit(solution)/shard_map/ppermute | solution.py:63
  80.0 3.6 %collective-permute-done.8 = f32[3]{0:T(128)S(1)} collective-permute-done((f32[3]{0:T(128)S(1)}, f32[3]{0:T(128)S(1)}, u32[]{:S(2)}, u32[]{:S(2)}) %collective-permute-start.8) | collective-permute-done | bytes 44 | tf_op jit(solution)/shard_map/ppermute | solution.py:63
  83.6 4.5 %collective-permute-done.9 = f32[3]{0:T(128)S(1)} collective-permute-done((f32[3]{0:T(128)S(1)}, f32[3]{0:T(128)S(1)}, u32[]{:S(2)}, u32[]{:S(2)}) %collective-permute-start.9) | collective-permute-done | bytes 44 | tf_op jit(solution)/shard_map/ppermute | solution.py:63
  88.0 0.7 fusion.31
  90.6 0.6 pad_maximum_fusion.3
  (55 shorter events, 5.3 us)
Async XLA Ops:
  0.6 32.7 %copy-start = (bf16[256,512]{1,0:T(8,128)(2,1)S(1)}, bf16[256,512]{1,0:T(8,128)(2,1)}, u32[]{:S(2)}) copy-start(bf16[256,512]{1,0:T(8,128)(2,1)} %param.16) | copy-start | bytes 786436
  0.6 13.6 %copy-start.2 = (bf16[1,256,32,48]{1,3,2,0:T(8,128)(2,1)S(1)}, bf16[1,256,32,48]{1,3,2,0:T(8,128)(2,1)}, u32[]{:S(2)}) copy-start(bf16[1,256,32,48]{1,3,2,0:T(8,128)(2,1)} %param.10) | copy-start | bytes 2359300
  0.7 12.2 %copy-start.5 = (s32[8]{0:T(128)S(1)}, s32[8]{0:T(128)}, u32[]{:S(2)}) copy-start(s32[8]{0:T(128)} %param.11) | copy-start | bytes 100
  0.7 31.0 %collective-permute-start = (bf16[256,32,48]{0,2,1:T(8,128)(2,1)}, bf16[256,32,48]{0,2,1:T(8,128)(2,1)S(1)}, u32[]{:S(2)}, u32[]{:S(2)}) collective-permute-start(bf16[256,32,48]{0,2,1:T(8,128)(2,1)} %bitcast.90), channel_id=1, source_target_pairs={{0,14},{2,0},{4,2},{6,4},{8,6},{10,8},{12,10},{14,12},{1,15},{3,1}... | collective-permute-start | bytes 2359304 | tf_op jit(solution)/shard_map/ppermute | solution.py:51
  7.9 6.2 %collective-permute-start.2 = (bf16[256,18,48]{0,2,1:T(8,128)(2,1)S(1)}, bf16[256,18,48]{0,2,1:T(8,128)(2,1)S(1)}, u32[]{:S(2)}, u32[]{:S(2)}) collective-permute-start(bf16[256,18,48]{0,2,1:T(8,128)(2,1)S(1)} %slice_select_fusion), channel_id=1, source_target_pairs={{0,1},{1,0},{2,3},{3,2},{4,5},{5,4},{6,7},{7,6},{8,9},{9,8},{10,11... | collective-permute-start | bytes 1327112 | tf_op jit(solution)/shard_map/ppermute | solution.py:41
  10.1 4.0 %collective-permute-start.5 = (f32[3,64]{1,0:T(4,128)S(1)}, f32[3,64]{1,0:T(4,128)S(1)}, u32[]{:S(2)}, u32[]{:S(2)}) collective-permute-start(f32[3,64]{1,0:T(4,128)S(1)} %pad_maximum_fusion.1), channel_id=1, source_target_pairs={{0,1},{1,0},{2,3},{3,2},{4,5},{5,4},{6,7},{7,6},{8,9},{9,8},{10,11... | collective-permute-start | bytes 2312 | tf_op jit(solution)/shard_map/ppermute | solution.py:63
  32.1 1.2 %collective-permute-start.3 = (f32[512]{0:T(512)S(1)}, f32[512]{0:T(512)S(1)}, u32[]{:S(2)}, u32[]{:S(2)}) collective-permute-start(f32[512]{0:T(512)S(1)} %pad_maximum_fusion), channel_id=1, source_target_pairs={{0,1},{1,0},{2,3},{3,2},{4,5},{5,4},{6,7},{7,6},{8,9},{9,8},{10,11... | collective-permute-start | bytes 6152 | tf_op jit(solution)/shard_map/ppermute | solution.py:63
  32.2 3.0 %collective-permute-start.1 = (bf16[256,18,48]{0,2,1:T(8,128)(2,1)S(1)}, bf16[256,18,48]{0,2,1:T(8,128)(2,1)S(1)}, u32[]{:S(2)}, u32[]{:S(2)}) collective-permute-start(bf16[256,18,48]{0,2,1:T(8,128)(2,1)S(1)} %slice_select_fusion.1), channel_id=1, source_target_pairs={{0,1},{1,0},{2,3},{3,2},{4,5},{5,4},{6,7},{7,6},{8,9},{9,8},{10,11... | collective-permute-start | bytes 1327112 | tf_op jit(solution)/shard_map/ppermute | solution.py:41
  59.6 1.3 %collective-permute-start.4 = (bf16[160,256]{1,0:T(8,128)(2,1)S(1)}, bf16[160,256]{1,0:T(8,128)(2,1)S(1)}, u32[]{:S(2)}, u32[]{:S(2)}) collective-permute-start(bf16[160,256]{1,0:T(8,128)(2,1)S(1)} %slice_select_fusion.2), channel_id=1, source_target_pairs={{0,1},{1,0},{2,3},{3,2},{4,5},{5,4},{6,7},{7,6},{8,9},{9,8},{10,11... | collective-permute-start | bytes 245768 | tf_op jit(solution)/shard_map/ppermute | solution.py:41
  60.6 1.8 %copy-start.1 = (bf16[25,96,256]{2,1,0:T(8,128)(2,1)S(1)}, bf16[25,96,256]{2,1,0:T(8,128)(2,1)}, u32[]{:S(2)}) copy-start(bf16[25,96,256]{2,1,0:T(8,128)(2,1)} %weight_ref.1) | copy-start | bytes 3686404
  71.2 0.7 copy-start.4
  71.2 1.2 %copy-start.3 = (s32[1,32,48]{2,1,0:T(8,128)S(1)}, s32[1,32,48]{2,1,0:T(8,128)}, u32[]{:S(2)}) copy-start(s32[1,32,48]{2,1,0:T(8,128)} %param.13) | copy-start | bytes 18436
  75.2 1.2 %collective-permute-start.6 = (f32[3]{0:T(128)S(1)}, f32[3]{0:T(128)S(1)}, u32[]{:S(2)}, u32[]{:S(2)}) collective-permute-start(f32[3]{0:T(128)S(1)} %pad_maximum_fusion.2), channel_id=1, source_target_pairs={{0,1},{1,0},{2,3},{3,2},{4,5},{5,4},{6,7},{7,6},{8,9},{9,8},{10,11... | collective-permute-start | bytes 44 | tf_op jit(solution)/shard_map/ppermute | solution.py:63
  76.4 3.6 %collective-permute-start.7 = (f32[3]{0:T(128)S(1)}, f32[3]{0:T(128)S(1)}, u32[]{:S(2)}, u32[]{:S(2)}) collective-permute-start(f32[3]{0:T(128)S(1)} %add.69), channel_id=1, source_target_pairs={{0,2},{2,0},{4,6},{6,4},{8,10},{10,8},{12,14},{14,12},{1,3},{3,1},... | collective-permute-start | bytes 44 | tf_op jit(solution)/shard_map/ppermute | solution.py:63
  80.0 3.6 %collective-permute-start.8 = (f32[3]{0:T(128)S(1)}, f32[3]{0:T(128)S(1)}, u32[]{:S(2)}, u32[]{:S(2)}) collective-permute-start(f32[3]{0:T(128)S(1)} %add.70), channel_id=1, source_target_pairs={{0,4},{2,6},{4,0},{6,2},{8,12},{10,14},{12,8},{14,10},{1,5},{3,7},... | collective-permute-start | bytes 44 | tf_op jit(solution)/shard_map/ppermute | solution.py:63
  83.6 4.5 %collective-permute-start.9 = (f32[3]{0:T(128)S(1)}, f32[3]{0:T(128)S(1)}, u32[]{:S(2)}, u32[]{:S(2)}) collective-permute-start(f32[3]{0:T(128)S(1)} %add.71), channel_id=1, source_target_pairs={{0,8},{2,10},{4,12},{6,14},{8,0},{10,2},{12,4},{14,6},{1,9},{3,11}... | collective-permute-start | bytes 44 | tf_op jit(solution)/shard_map/ppermute | solution.py:63

commit v14 on v13

--- a/solution.py
+++ b/solution.py
@@ -134,7 +134,12 @@
                     preferred_element_type=jnp.float32,
                 )
                 mixed = term if mixed is None else mixed + term
-            mixed = mixed + pool_ref[...]
+            mixed = mixed + lax.dot_general(
+                pool_ref[...],
+                proj_ref[:, branches * width : (branches + 1) * width],
+                contract,
+                preferred_element_type=jnp.float32,
+            )
             rounded = relu_bf16(mixed)
             out_ref[rows, :] = jnp.where(keep_ref[...] > 0.5, rounded, jnp.zeros_like(rounded))
         if not finish:
@@ -294,9 +299,7 @@
     pooled = (frame_totals / (height * columns)).astype(jnp.bfloat16)
     pool_feature = relu_bf16(jnp.dot(pool_weight, pooled, preferred_element_type=jnp.float32))
     aspp_width = aspp_point.shape[0]
-    pool_term = jnp.dot(
-        proj_weight[:, 4 * aspp_width :], pool_feature, preferred_element_type=jnp.float32
-    )[None]
+    pool_term = pool_feature[None]
     pad_columns = pitch - columns
     keep = (jnp.arange(block) % pitch >= pad_columns).astype(jnp.float32)[:, None]
     projected_flat = aspp_pass(

time: 91.7 us -> 91.4 us (level)
  matrix products: 2.25 us -> 0.6 us
    dot_general x1 -> x0, matrix products: 1.65 us -> none  [shards(): jnp.dot(proj_weight[:, 4 * aspp_width:], pool_feature, preferred_element_...]
  transfers between devices with their start and end apart: 10 -> 10, of which waited for: 6 -> 7; matrix products, arithmetic and copies ran while one was open for 13% -> 11% of each run, Pallas kernels for 17% -> 17%
where the time goes in v14:
time: 91.4 us; the launch traced here: 90.9 us
  Pallas kernels  46.1 us (50%)
  other arithmetic  13.8 us (15%)
  waiting for transfers between devices  12.6 us (14%)
  starting transfers between devices  8.05 us (9%)
  local copies, waits for them, and re-layouts  6.28 us (7%)
  between operations  3.5 us (4%)
    pallas_call x2, Pallas kernels, aspp_pass(): pl.pallas_call(body, out_shape=out_shape, in_specs=in_specs, out_specs=ou...  37.2 us
    ppermute x6, waiting for transfers between devices, all_sum(): other = lax.ppermute(value, axis, pairs)  12.3 us
    pallas_call x1, Pallas kernels, head_kernel_call(): pl.pallas_call(body, out_shape=jax.ShapeDtypeStruct((blocks * block, outp...  8.83 us
    ppermute x1, starting transfers between devices, shifted(): return lax.ppermute(value, axis, pairs)  6.09 us
    pad x2, local copies, waits for them, and re-layouts, flat_of(): jnp.pad(jnp.transpose(wide, (1, 2, 0)), ((1, 1), (pitch - columns, 0), (0...  3.66 us
    select_n x3, other arithmetic, with_rims(): jnp.where(first, lax.slice_in_dim(block, size - width, None, axis=dim), l...  2.18 us
    another operation x1, other arithmetic, shards(): jnp.stack([center_err, offset_err, counted_local])  2.06 us
  transfers between devices with their start and end apart: 10, of which 7 were waited for; matrix products, arithmetic and copies ran while one was open for 11% of the time, Pallas kernels for 17%

profile of v14, /device:TPU:0, one launch (start us, length us, event | category | flops | bytes accessed | tf_op | source)
XLA Modules:
  0.0 90.9 jit_solution(2041522201434514414)
XLA Ops:
  0.7 6.1 %collective-permute-start = (bf16[256,32,48]{0,2,1:T(8,128)(2,1)}, bf16[256,32,48]{0,2,1:T(8,128)(2,1)S(1)}, u32[]{:S(2)}, u32[]{:S(2)}) collective-permute-start(bf16[256,32,48]{0,2,1:T(8,128)(2,1)} %bitcast.88), channel_id=1, source_target_pairs={{0,14},{2,0},{4,2},{6,4},{8,6},{10,8},{12,10},{14,12},{1,15},{3,1}... | collective-permute-start | bytes 2359304 | tf_op jit(solution)/shard_map/ppermute | solution.py:51
  6.8 1.2 %slice_select_fusion = bf16[256,18,48]{0,2,1:T(8,128)(2,1)S(1)} fusion(bf16[256,32,48]{0,2,1:T(8,128)(2,1)} %bitcast.89, pred[]{:T(512)S(6)} %eq.35), kind=kLoop, calls=%fused_computation.22 | loop fusion | flops 221184 | bytes 1327105 | tf_op jit(solution)/shard_map/jit(_where)/select_n | solution.py:36
  8.0 0.7 and_bitcast_fusion
  8.8 1.3 %convert_reduce_fusion.2 = (f32[64]{0:T(128)S(1)}, f32[64]{0:T(128)S(1)}, f32[64]{0:T(128)S(1)}) fusion(s32[32,48]{1,0:T(8,128)} %bitcast.96, pred[32,48]{1,0:T(8,128)(4,1)S(1)} %get-tuple-element.12, f32[32]{0:T(128)S(1)} %add_convert_fusion), kind=kLoop, calls=%fused_computation.14 | loop fusion | flops 786240 | bytes 8576 | tf_op jit(solution)/shard_map/reduce_sum | solution.py:289
  10.7 1.3 %convert_compare_fusion = pred[64,32,48]{0,2,1:T(8,128)(4,1)S(1)} fusion(s32[32,48]{1,0:T(8,128)} %bitcast.97, pred[32,48]{1,0:T(8,128)(4,1)S(1)} %get-tuple-element.12), kind=kLoop, calls=%fused_computation.15 | loop fusion | flops 393216 | bytes 105984 | tf_op jit(solution)/shard_map/gt | solution.py:324
  12.0 0.9 fusion.11.rest_3_
  12.9 0.6 fusion.20
  14.5 1.8 %pad.12 = bf16[70,80,256]{2,1,0:T(8,128)(2,1)} pad(bf16[68,48,256]{2,1,0:T(8,128)(2,1)S(1)} %maximum_bitcast_fusion.1, bf16[]{:T(256)} %constant.53.clone.1), padding=1_1x32_0x0_0 | pad | bytes 4538370 | tf_op jit(solution)/shard_map/jit(_pad)/pad | solution.py:268
  16.3 15.3 %shard_map.113.rest_0_ = f32[4,2560,256]{2,1,0:T(8,128)} custom-call(bf16[5600,256]{1,0:T(8,128)(2,1)} %bitcast.92, bf16[256,512]{1,0:T(8,128)(2,1)} %point_ref.3, bf16[3,9,256,512]{3,2,1,0:T(8,128)(2,1)} %dilated_ref.3), custom_call_target="tpu_custom_call" | custom-call | flops 9395240960 | bytes 16891904 | tf_op jit(solution)/shard_map/pallas_call | solution.py:164
  33.5 0.6 broadcast_in_dim.58.rest_2_
  34.5 1.8 %pad.11 = bf16[70,80,256]{2,1,0:T(8,128)(2,1)} pad(bf16[68,48,256]{2,1,0:T(8,128)(2,1)S(1)} %maximum_bitcast_fusion, bf16[]{:T(256)} %constant.53.clone.1), padding=1_1x32_0x0_0 | pad | bytes 4538370 | tf_op jit(solution)/shard_map/jit(_pad)/pad | solution.py:268
  36.3 21.9 %shard_map.114 = bf16[2560,256]{1,0:T(8,128)(2,1)} custom-call(bf16[5600,256]{1,0:T(8,128)(2,1)} %bitcast.91, bf16[256,512]{1,0:T(8,128)(2,1)} %point_ref.3, bf16[3,9,256,512]{3,2,1,0:T(8,128)(2,1)} %dilated_ref.3, f32[4,2560,256]{2,1,0:T(8,128)} %shard_map.113.rest_0_, bf16[256,1280]{1,0:T(8,128)(2,1)} %rest_1_.1, bf16[1,256]{1,0:T(2,128)(2,1)} %broadcast_in_dim.58.rest_2_, ...), custom_call_target="tpu_custom_call" | custom-call | flops 10737418240 | bytes 16891904 | tf_op jit(solution)/shard_map/pallas_call | solution.py:164
  58.2 0.9 %slice_select_fusion.2 = bf16[160,256]{1,0:T(8,128)(2,1)S(1)} fusion(bf16[2560,256]{1,0:T(8,128)(2,1)} %shard_map.114, pred[]{:T(512)S(6)} %eq.35), kind=kLoop, calls=%fused_computation.39 | loop fusion | flops 40960 | bytes 245761 | tf_op jit(solution)/shard_map/jit(_where)/select_n | solution.py:36
  59.6 0.7 select_reduce_fusion
  60.5 1.5 %fusion.5.x_ref = bf16[3040,256]{1,0:T(8,128)(2,1)S(1)} fusion(bf16[160,256]{1,0:T(8,128)(2,1)S(1)} %get-tuple-element.22, bf16[2560,256]{1,0:T(8,128)(2,1)} %shard_map.114, bf16[160,256]{1,0:T(8,128)(2,1)S(1)} %get-tuple-element.21), kind=kLoop, calls=%fused_computation.12 | loop fusion | flops 9338880 | bytes 3031040 | tf_op jit(solution)/shard_map/concatenate | solution.py:45
  62.1 8.8 %shard_map.115 = bf16[2560,96]{1,0:T(8,128)(2,1)S(1)} custom-call(bf16[3040,256]{1,0:T(8,128)(2,1)S(1)} %fusion.5.x_ref, bf16[25,96,256]{2,1,0:T(8,128)(2,1)S(1)} %copy-done.1), custom_call_target="tpu_custom_call" | custom-call | flops 3145728000 | bytes 3276800 | tf_op jit(solution)/shard_map/pallas_call | solution.py:203
  72.1 0.8 multiply_reduce_fusion
  72.9 2.1 %pad_maximum_fusion.2 = f32[3]{0:T(128)S(1)} fusion(f32[1]{0:T(128)} %bitcast.34, f32[1]{0:T(128)} %bitcast.33, f32[1]{0:T(128)} %bitcast.30), kind=kLoop, calls=%fused_computation.61 | loop fusion | flops 6 | bytes 24 | tf_op jit(solution)/shard_map/stack | solution.py:343
  75.3 0.6 copy.19
  76.1 3.6 %collective-permute-done.7 = f32[3]{0:T(128)S(1)} collective-permute-done((f32[3]{0:T(128)S(1)}, f32[3]{0:T(128)S(1)}, u32[]{:S(2)}, u32[]{:S(2)}) %collective-permute-start.7) | collective-permute-done | bytes 44 | tf_op jit(solution)/shard_map/ppermute | solution.py:63
  79.7 3.6 %collective-permute-done.8 = f32[3]{0:T(128)S(1)} collective-permute-done((f32[3]{0:T(128)S(1)}, f32[3]{0:T(128)S(1)}, u32[]{:S(2)}, u32[]{:S(2)}) %collective-permute-start.8) | collective-permute-done | bytes 44 | tf_op jit(solution)/shard_map/ppermute | solution.py:63
  83.2 4.5 %collective-permute-done.9 = f32[3]{0:T(128)S(1)} collective-permute-done((f32[3]{0:T(128)S(1)}, f32[3]{0:T(128)S(1)}, u32[]{:S(2)}, u32[]{:S(2)}) %collective-permute-start.9) | collective-permute-done | bytes 44 | tf_op jit(solution)/shard_map/ppermute | solution.py:63
  87.7 0.7 fusion.29
  90.3 0.6 pad_maximum_fusion.3
  (54 shorter events, 5.4 us)
Async XLA Ops:
  0.6 32.7 %copy-start = (bf16[256,512]{1,0:T(8,128)(2,1)S(1)}, bf16[256,512]{1,0:T(8,128)(2,1)}, u32[]{:S(2)}) copy-start(bf16[256,512]{1,0:T(8,128)(2,1)} %param.16) | copy-start | bytes 786436
  0.6 13.6 %copy-start.2 = (bf16[1,256,32,48]{1,3,2,0:T(8,128)(2,1)S(1)}, bf16[1,256,32,48]{1,3,2,0:T(8,128)(2,1)}, u32[]{:S(2)}) copy-start(bf16[1,256,32,48]{1,3,2,0:T(8,128)(2,1)} %param.10) | copy-start | bytes 2359300
  0.7 12.2 %copy-start.5 = (s32[8]{0:T(128)S(1)}, s32[8]{0:T(128)}, u32[]{:S(2)}) copy-start(s32[8]{0:T(128)} %param.11) | copy-start | bytes 100
  0.7 31.0 %collective-permute-start = (bf16[256,32,48]{0,2,1:T(8,128)(2,1)}, bf16[256,32,48]{0,2,1:T(8,128)(2,1)S(1)}, u32[]{:S(2)}, u32[]{:S(2)}) collective-permute-start(bf16[256,32,48]{0,2,1:T(8,128)(2,1)} %bitcast.88), channel_id=1, source_target_pairs={{0,14},{2,0},{4,2},{6,4},{8,6},{10,8},{12,10},{14,12},{1,15},{3,1}... | collective-permute-start | bytes 2359304 | tf_op jit(solution)/shard_map/ppermute | solution.py:51
  7.9 6.2 %collective-permute-start.2 = (bf16[256,18,48]{0,2,1:T(8,128)(2,1)S(1)}, bf16[256,18,48]{0,2,1:T(8,128)(2,1)S(1)}, u32[]{:S(2)}, u32[]{:S(2)}) collective-permute-start(bf16[256,18,48]{0,2,1:T(8,128)(2,1)S(1)} %slice_select_fusion), channel_id=1, source_target_pairs={{0,1},{1,0},{2,3},{3,2},{4,5},{5,4},{6,7},{7,6},{8,9},{9,8},{10,11... | collective-permute-start | bytes 1327112 | tf_op jit(solution)/shard_map/ppermute | solution.py:41
  10.1 4.0 %collective-permute-start.5 = (f32[3,64]{1,0:T(4,128)S(1)}, f32[3,64]{1,0:T(4,128)S(1)}, u32[]{:S(2)}, u32[]{:S(2)}) collective-permute-start(f32[3,64]{1,0:T(4,128)S(1)} %pad_maximum_fusion.1), channel_id=1, source_target_pairs={{0,1},{1,0},{2,3},{3,2},{4,5},{5,4},{6,7},{7,6},{8,9},{9,8},{10,11... | collective-permute-start | bytes 2312 | tf_op jit(solution)/shard_map/ppermute | solution.py:63
  32.1 1.2 %collective-permute-start.3 = (f32[512]{0:T(512)S(1)}, f32[512]{0:T(512)S(1)}, u32[]{:S(2)}, u32[]{:S(2)}) collective-permute-start(f32[512]{0:T(512)S(1)} %pad_maximum_fusion), channel_id=1, source_target_pairs={{0,1},{1,0},{2,3},{3,2},{4,5},{5,4},{6,7},{7,6},{8,9},{9,8},{10,11... | collective-permute-start | bytes 6152 | tf_op jit(solution)/shard_map/ppermute | solution.py:63
  32.2 2.0 %collective-permute-start.1 = (bf16[256,18,48]{0,2,1:T(8,128)(2,1)S(1)}, bf16[256,18,48]{0,2,1:T(8,128)(2,1)S(1)}, u32[]{:S(2)}, u32[]{:S(2)}) collective-permute-start(bf16[256,18,48]{0,2,1:T(8,128)(2,1)S(1)} %slice_select_fusion.1), channel_id=1, source_target_pairs={{0,1},{1,0},{2,3},{3,2},{4,5},{5,4},{6,7},{7,6},{8,9},{9,8},{10,11... | collective-permute-start | bytes 1327112 | tf_op jit(solution)/shard_map/ppermute | solution.py:41
  59.2 1.4 %collective-permute-start.4 = (bf16[160,256]{1,0:T(8,128)(2,1)S(1)}, bf16[160,256]{1,0:T(8,128)(2,1)S(1)}, u32[]{:S(2)}, u32[]{:S(2)}) collective-permute-start(bf16[160,256]{1,0:T(8,128)(2,1)S(1)} %slice_select_fusion.2), channel_id=1, source_target_pairs={{0,1},{1,0},{2,3},{3,2},{4,5},{5,4},{6,7},{7,6},{8,9},{9,8},{10,11... | collective-permute-start | bytes 245768 | tf_op jit(solution)/shard_map/ppermute | solution.py:41
  60.3 1.7 %copy-start.1 = (bf16[25,96,256]{2,1,0:T(8,128)(2,1)S(1)}, bf16[25,96,256]{2,1,0:T(8,128)(2,1)}, u32[]{:S(2)}) copy-start(bf16[25,96,256]{2,1,0:T(8,128)(2,1)} %weight_ref.1) | copy-start | bytes 3686404
  70.9 0.7 copy-start.4
  70.9 1.2 %copy-start.3 = (s32[1,32,48]{2,1,0:T(8,128)S(1)}, s32[1,32,48]{2,1,0:T(8,128)}, u32[]{:S(2)}) copy-start(s32[1,32,48]{2,1,0:T(8,128)} %param.13) | copy-start | bytes 18436
  74.9 1.2 %collective-permute-start.6 = (f32[3]{0:T(128)S(1)}, f32[3]{0:T(128)S(1)}, u32[]{:S(2)}, u32[]{:S(2)}) collective-permute-start(f32[3]{0:T(128)S(1)} %pad_maximum_fusion.2), channel_id=1, source_target_pairs={{0,1},{1,0},{2,3},{3,2},{4,5},{5,4},{6,7},{7,6},{8,9},{9,8},{10,11... | collective-permute-start | bytes 44 | tf_op jit(solution)/shard_map/ppermute | solution.py:63
  76.1 3.6 %collective-permute-start.7 = (f32[3]{0:T(128)S(1)}, f32[3]{0:T(128)S(1)}, u32[]{:S(2)}, u32[]{:S(2)}) collective-permute-start(f32[3]{0:T(128)S(1)} %add.69), channel_id=1, source_target_pairs={{0,2},{2,0},{4,6},{6,4},{8,10},{10,8},{12,14},{14,12},{1,3},{3,1},... | collective-permute-start | bytes 44 | tf_op jit(solution)/shard_map/ppermute | solution.py:63
  79.7 3.6 %collective-permute-start.8 = (f32[3]{0:T(128)S(1)}, f32[3]{0:T(128)S(1)}, u32[]{:S(2)}, u32[]{:S(2)}) collective-permute-start(f32[3]{0:T(128)S(1)} %add.70), channel_id=1, source_target_pairs={{0,4},{2,6},{4,0},{6,2},{8,12},{10,14},{12,8},{14,10},{1,5},{3,7},... | collective-permute-start | bytes 44 | tf_op jit(solution)/shard_map/ppermute | solution.py:63
  83.2 4.5 %collective-permute-start.9 = (f32[3]{0:T(128)S(1)}, f32[3]{0:T(128)S(1)}, u32[]{:S(2)}, u32[]{:S(2)}) collective-permute-start(f32[3]{0:T(128)S(1)} %add.71), channel_id=1, source_target_pairs={{0,8},{2,10},{4,12},{6,14},{8,0},{10,2},{12,4},{14,6},{1,9},{3,11}... | collective-permute-start | bytes 44 | tf_op jit(solution)/shard_map/ppermute | solution.py:63
